TPU v7x, 32 devices: a whole 2x2x4 slice. The times are simulated.
32 devices in a mesh: ctx: 8 (over y, x, core), head: 4 (over z).
Axes of the slice: x: 2, y: 2, z: 4, core: 2. Of those that a mesh axis runs over, the one named last changes fastest.
Arguments:
- hidden_in: bfloat16 [4096, 5376], P('ctx'), may hold values from -40 to 40
- out_grad: bfloat16 [4096, 5376], P('ctx'), may hold values from -6 to 6
- w_query: bfloat16 [5376, 4096], P('ctx', 'head'), may hold values from -0.078125 to 0.078125
- key_weight: bfloat16 [5376, 2048], P('ctx', 'head'), may hold values from -0.078125 to 0.078125
- value_weight: bfloat16 [5376, 2048], P('ctx', 'head'), may hold values from -0.078125 to 0.078125
- w_out: bfloat16 [5376, 4096], P('ctx', 'head'), may hold values from -0.09375 to 0.09375
Outputs:
- in_grad: bfloat16 [4096, 5376], P('ctx', 'head')
- grad_query: float32 [5376, 4096], P('ctx', 'head')
- grad_key: float32 [5376, 2048], P('ctx', 'head')
- grad_value: float32 [5376, 2048], P('ctx', 'head')
- grad_out_w: float32 [5376, 4096], P('ctx', 'head')
All inputs are finite; a program needn't handle non-finite values.
Results may differ from a plain program's by a relative error of at most 0.02.
Values may be sent and summed in bfloat16 or wider, within the bound.
No kernel may reach another device: no remote copies, remote signals or barrier semaphores. Data moves between devices by JAX's collectives and lax.ppermute only.
A program may use at most 256 MiB of HBM per device.

v0:
```python
import jax
import jax.numpy as jnp
from jax import lax
from jax.sharding import PartitionSpec as P

HEAD_WIDTH = 128
WINDOW = 1024


QUERY_SCALE = 168.0 ** (-0.5)
ROPE_BASE = 10000.0
NEG_LARGE = -1e30


def from_behind(value, axis, steps):
    count = lax.axis_size(axis)
    initial, last = (max(0, -steps), min(count, count - steps))
    return lax.ppermute(value, axis, [(source, source + steps) for source in range(initial, last)])


def rope_tables(first, count, head_size):
    half = head_size // 2
    freq = ROPE_BASE ** (-(jnp.arange(half, dtype=jnp.float32) * 2.0 / head_size))
    places = first + jnp.arange(count, dtype=jnp.int32)
    angle = places.astype(jnp.float32)[:, None] * freq[None, :]
    return (jnp.cos(angle)[:, None, :], jnp.sin(angle)[:, None, :])


def apply_rotary(value_rows, cosine_table, sine_table):
    half = value_rows.shape[-1] // 2
    upper = value_rows[..., :half]
    lower = value_rows[..., half:]
    return jnp.concatenate(
        [upper * cosine_table - lower * sine_table, lower * cosine_table + upper * sine_table],
        axis=-1,
    )


def inverse_rotary(value_rows, cosine_table, sine_table):
    half = value_rows.shape[-1] // 2
    upper = value_rows[..., :half]
    lower = value_rows[..., half:]
    return jnp.concatenate(
        [upper * cosine_table + lower * sine_table, lower * cosine_table - upper * sine_table],
        axis=-1,
    )


def dot_rows(left, weight):
    return lax.dot_general(
        left, weight, (((1,), (1,)), ((), ())), preferred_element_type=jnp.float32
    )


def attend_forward(query_rows, key_rows, value_rows, allowed):
    score = jnp.einsum("ngrd,mgd->grnm", query_rows, key_rows, preferred_element_type=jnp.float32)
    score = jnp.where(allowed[None, None], score, NEG_LARGE)
    top = jnp.max(score, axis=-1, keepdims=True)
    expo = jnp.exp(score - top)
    prob = expo / jnp.sum(expo, axis=-1, keepdims=True)
    prob_b = prob.astype(jnp.bfloat16)
    attended = jnp.einsum(
        "grnm,mgd->ngrd", prob_b, value_rows, preferred_element_type=jnp.float32
    ).astype(jnp.bfloat16)
    return (prob, prob_b, attended)


def attend_backward(prob, prob_b, attended, gradient_list, query_rows, key_rows, value_rows):
    delta = jnp.sum(gradient_list.astype(jnp.float32) * attended.astype(jnp.float32), axis=-1)
    delta = jnp.transpose(delta, (1, 2, 0))[..., None]
    grad_prob = jnp.einsum(
        "ngrd,mgd->grnm", gradient_list, value_rows, preferred_element_type=jnp.float32
    )
    grad_score = (prob * (grad_prob - delta)).astype(jnp.bfloat16)
    grad_q = jnp.einsum("grnm,mgd->ngrd", grad_score, key_rows, preferred_element_type=jnp.float32)
    grad_k = jnp.einsum(
        "grnm,ngrd->mgd", grad_score, query_rows, preferred_element_type=jnp.float32
    )
    grad_v = jnp.einsum("grnm,ngrd->mgd", prob_b, gradient_list, preferred_element_type=jnp.float32)
    return (grad_q, grad_k, grad_v)


def shards(hidden_in, out_grad, w_query, key_weight, value_weight, w_out):
    rows = hidden_in.shape[0]
    head_size = HEAD_WIDTH
    query_cols = w_query.shape[1]
    key_value_columns = key_weight.shape[1]
    local_heads = query_cols // head_size
    local_groups = key_value_columns // head_size
    group_ratio = local_heads // local_groups
    reach = WINDOW // rows
    first = lax.axis_index("ctx") * rows
    full_query, full_key, full_value, full_out = (
        lax.all_gather(w_query, "ctx", axis=0, tiled=True),
        lax.all_gather(key_weight, "ctx", axis=0, tiled=True),
        lax.all_gather(value_weight, "ctx", axis=0, tiled=True),
        lax.all_gather(w_out, "ctx", axis=0, tiled=True),
    )
    query = jnp.dot(hidden_in, full_query, preferred_element_type=jnp.float32)
    key_projected = jnp.dot(hidden_in, full_key, preferred_element_type=jnp.float32)
    value_projected = jnp.dot(hidden_in, full_value, preferred_element_type=jnp.float32)
    grad_att_f = jnp.dot(out_grad, full_out, preferred_element_type=jnp.float32)
    cosine_table, sine_table = rope_tables(first, rows, head_size)
    query_rows = (
        apply_rotary(query.reshape(rows, local_heads, head_size), cosine_table, sine_table)
        * QUERY_SCALE
    ).astype(jnp.bfloat16)
    keys_here = (
        apply_rotary(key_projected.reshape(rows, local_groups, head_size), cosine_table, sine_table)
        .astype(jnp.bfloat16)
        .reshape(rows, key_value_columns)
    )
    values_here = value_projected.astype(jnp.bfloat16)
    attention_gradient = grad_att_f.astype(jnp.bfloat16)
    key_blocks = []
    value_blocks = []
    for distance in range(reach, 0, -1):
        far_keys, far_values = from_behind((keys_here, values_here), "ctx", distance)
        key_blocks.append(far_keys)
        value_blocks.append(far_values)
    keys_all = jnp.concatenate(key_blocks + [keys_here], axis=0).reshape(
        -1, local_groups, head_size
    )
    values_all = jnp.concatenate(value_blocks + [values_here], axis=0).reshape(
        -1, local_groups, head_size
    )
    query_pos = first + jnp.arange(rows, dtype=jnp.int32)
    key_pos = first - reach * rows + jnp.arange((reach + 1) * rows, dtype=jnp.int32)
    allowed = (
        (key_pos[None, :] <= query_pos[:, None])
        & (key_pos[None, :] > query_pos[:, None] - WINDOW)
        & (key_pos[None, :] >= 0)
    )
    grouped_queries = query_rows.reshape(rows, local_groups, group_ratio, head_size)
    grouped_grads = attention_gradient.reshape(rows, local_groups, group_ratio, head_size)
    prob, prob_b, attended = attend_forward(grouped_queries, keys_all, values_all, allowed)
    attended_flat = attended.reshape(rows, query_cols)
    grad_w_out = jnp.einsum(
        "nd,nc->dc", out_grad, attended_flat, preferred_element_type=jnp.float32
    )
    grad_q, grad_k, grad_v = attend_backward(
        prob, prob_b, attended, grouped_grads, grouped_queries, keys_all, values_all
    )
    grad_k = grad_k.reshape(-1, key_value_columns)
    grad_v = grad_v.reshape(-1, key_value_columns)
    own_keys = grad_k[reach * rows :]
    own_values = grad_v[reach * rows :]
    for distance in range(1, reach + 1):
        lowest = (reach - distance) * rows
        back_keys, back_values = from_behind(
            (grad_k[lowest : lowest + rows], grad_v[lowest : lowest + rows]), "ctx", -distance
        )
        own_keys = own_keys + back_keys
        own_values = own_values + back_values
    dquery = (
        (
            inverse_rotary(grad_q.reshape(rows, local_heads, head_size), cosine_table, sine_table)
            * QUERY_SCALE
        )
        .astype(jnp.bfloat16)
        .reshape(rows, query_cols)
    )
    key_gradient = (
        inverse_rotary(own_keys.reshape(rows, local_groups, head_size), cosine_table, sine_table)
        .astype(jnp.bfloat16)
        .reshape(rows, key_value_columns)
    )
    value_gradient = own_values.astype(jnp.bfloat16)
    partial_in = (
        dot_rows(dquery, full_query)
        + dot_rows(key_gradient, full_key)
        + dot_rows(value_gradient, full_value)
    )
    in_grad = lax.psum_scatter(
        partial_in.astype(jnp.bfloat16), "head", scatter_dimension=1, tiled=True
    )
    grad_q_part = jnp.einsum("nd,nc->dc", hidden_in, dquery, preferred_element_type=jnp.float32)
    grad_k_part = jnp.einsum(
        "nd,nc->dc", hidden_in, key_gradient, preferred_element_type=jnp.float32
    )
    grad_v_part = jnp.einsum(
        "nd,nc->dc", hidden_in, value_gradient, preferred_element_type=jnp.float32
    )
    grad_query, grad_key, grad_value, grad_out_w = (
        lax.psum_scatter(
            grad_q_part.astype(jnp.bfloat16), "ctx", scatter_dimension=0, tiled=True
        ).astype(jnp.float32),
        lax.psum_scatter(
            grad_k_part.astype(jnp.bfloat16), "ctx", scatter_dimension=0, tiled=True
        ).astype(jnp.float32),
        lax.psum_scatter(
            grad_v_part.astype(jnp.bfloat16), "ctx", scatter_dimension=0, tiled=True
        ).astype(jnp.float32),
        lax.psum_scatter(
            grad_w_out.astype(jnp.bfloat16), "ctx", scatter_dimension=0, tiled=True
        ).astype(jnp.float32),
    )
    return (in_grad, grad_query, grad_key, grad_value, grad_out_w)


def solution(mesh):
    in_specs = (
        P("ctx", None),
        P("ctx", None),
        P("ctx", "head"),
        P("ctx", "head"),
        P("ctx", "head"),
        P("ctx", "head"),
    )
    out_specs = (
        P("ctx", "head"),
        P("ctx", "head"),
        P("ctx", "head"),
        P("ctx", "head"),
        P("ctx", "head"),
    )
    return jax.shard_map(shards, mesh=mesh, in_specs=in_specs, out_specs=out_specs, check_vma=False)
```

profile of v0, /device:TPU:3, one launch (start us, length us, event | category | flops | bytes accessed | tf_op | source)
XLA Modules:
  0.0 761.7 jit_solution(6520298563329758971)
XLA Ops:
  11.1 42.6 %all-gather.5.cloned.1.call-done = bf16[5376,512]{1,0:T(8,128)(2,1)} async-done(((bf16[672,512]{1,0:T(8,128)(2,1)}), bf16[5376,512]{1,0:T(8,128)(2,1)}) %all-gather.5.cloned.1.call-update) | async-done | bytes 5505040 | tf_op jit(solution)/shard_map/all_gather | solution.py:95
  53.6 6.7 fusion.38
  61.9 3.0 collective-permute-start.1
  64.9 2.6 collective-permute-start
  69.5 17.4 %collective-permute-done.1 = bf16[512,512]{0,1:T(8,128)(2,1)S(1)} collective-permute-done((bf16[512,512]{0,1:T(8,128)(2,1)S(1)}, bf16[512,512]{0,1:T(8,128)(2,1)S(1)}, u32[]{:S(2)}, u32[]{:S(2)}) %collective-permute-start.1) | collective-permute-done | bytes 524320 | tf_op jit(solution)/shard_map/ppermute | solution.py:18
  87.1 9.3 %collective-permute-done = bf16[512,512]{0,1:T(8,128)(2,1)S(1)} collective-permute-done((bf16[512,512]{0,1:T(8,128)(2,1)S(1)}, bf16[512,512]{0,1:T(8,128)(2,1)S(1)}, u32[]{:S(2)}, u32[]{:S(2)}) %collective-permute-start) | collective-permute-done | bytes 524320 | tf_op jit(solution)/shard_map/ppermute | solution.py:18
  96.7 36.7 %all-gather.11.cloned.1.call-done = bf16[5376,1024]{1,0:T(8,128)(2,1)} async-done(((bf16[672,1024]{1,0:T(8,128)(2,1)}), bf16[5376,1024]{1,0:T(8,128)(2,1)}) %all-gather.11.cloned.1.call-update) | async-done | bytes 11010064 | tf_op jit(solution)/shard_map/all_gather | solution.py:97
  133.4 10.2 %convolution_convert_fusion.4 = bf16[512,1024]{1,0:T(8,128)(2,1)S(1)} fusion(bf16[512,5376]{1,0:T(8,128)(2,1)} %param.7, bf16[5376,1024]{1,0:T(8,128)(2,1)} %all-gather.11.cloned.1.call-done), kind=kOutput, calls=%fused_computation.36 | convolution fusion | flops 5637668864 | bytes 17563648 | tf_op jit(solution)/shard_map/dot_general | solution.py:102
  144.9 55.7 %all-gather.7.cloned.1.call-done = bf16[5376,1024]{1,0:T(8,128)(2,1)} async-done(((bf16[672,1024]{1,0:T(8,128)(2,1)}), bf16[5376,1024]{1,0:T(8,128)(2,1)}) %all-gather.7.cloned.1.call-update) | async-done | bytes 11010064 | tf_op jit(solution)/shard_map/all_gather | solution.py:94
  200.6 10.2 %convolution_bitcast_fusion.2 = f32[64,8,8,128]{3,1,2,0:T(8,128)S(1)} fusion(bf16[512,5376]{1,0:T(8,128)(2,1)} %param.6, bf16[5376,1024]{1,0:T(8,128)(2,1)} %all-gather.7.cloned.1.call-done), kind=kOutput, calls=%fused_computation.33 | convolution fusion | flops 5637144576 | bytes 18612224 | tf_op jit(solution)/shard_map/dot_general | solution.py:99
  213.9 14.7 %fusion.37 = (f32[4,2,512]{2,1,0:T(2,128)S(1)}, f32[4,2,512,1536]{2,3,1,0:T(8,128)}) fusion(pred[512,1536]{0,1:T(8,128)(4,1)} %and_and_fusion, bf16[512,4,2,128]{3,0,2,1:T(8,128)(2,1)S(1)} %fusion.13, bf16[512,4,128]{2,0,1:T(8,128)(2,1)S(1)} %maximum_convert_fusion, bf16[512,4,128]{2,0,1:T(8,128)(2,1)S(1)} %copy.63, bf16[512,4,128]{2,0,1:T(8,128)(2,1)S(1)} %copy.62), kind=kOutput, calls=%fused_computation.74 | convolution fusion | flops 1634207232 | bytes 28590080 | tf_op jit(solution)/shard_map/sub | solution.py:59
  228.6 10.8 %fusion.6 = bf16[4,2,512,1536]{2,3,1,0:T(8,128)(2,1)S(1)} fusion(f32[4,2,512,1536]{2,3,1,0:T(8,128)} %get-tuple-element.43, f32[4,2,512]{2,1,0:T(2,128)S(1)} %get-tuple-element.42), kind=kLoop, calls=%fused_computation.13 | loop fusion | flops 12582912 | bytes 37765120 | tf_op jit(solution)/shard_map/convert_element_type | solution.py:61
  239.5 7.9 %convolution_bitcast_fusion = f32[1536,4,128]{0,2,1:T(8,128)} fusion(bf16[512,4,2,128]{0,3,2,1:T(8,128)(2,1)} %bitcast.124, bf16[4,2,512,1536]{2,3,1,0:T(8,128)(2,1)S(1)} %fusion.6), kind=kOutput, calls=%fused_computation.20 | convolution fusion | flops 1610612736 | bytes 16777216 | tf_op jit(solution)/shard_map/grnm,ngrd->mgd/dot_general | solution.py:79
  247.4 3.6 fusion.32
  250.9 2.2 collective-permute-start.7
  253.1 2.6 collective-permute-start.6
  255.8 8.0 %convolution_convert_fusion.6 = bf16[512,512]{1,0:T(8,128)(2,1)} fusion(bf16[512,5376]{1,0:T(8,128)(2,1)} %param.6, bf16[5376,512]{1,0:T(8,128)(2,1)} %all-gather.9.cloned.1.call-done), kind=kOutput, calls=%fused_computation.38 | convolution fusion | flops 2818834432 | bytes 11534336 | tf_op jit(solution)/shard_map/dot_general | solution.py:101
  263.8 4.0 collective-permute-start.3
  267.8 3.1 collective-permute-start.2
  270.9 7.5 collective-permute-done.7
  278.4 23.0 %collective-permute-done.6 = f32[512,512]{0,1:T(8,128)} collective-permute-done((f32[512,512]{0,1:T(8,128)}, f32[512,512]{0,1:T(8,128)}, u32[]{:S(2)}, u32[]{:S(2)}) %collective-permute-start.6) | collective-permute-done | bytes 1048608 | tf_op jit(solution)/shard_map/ppermute | solution.py:18
  302.9 7.5 fusion.10
  310.5 8.3 %copy.107 = bf16[5376,512]{1,0:T(8,128)(2,1)} copy(bf16[5376,512]{0,1:T(8,128)(2,1)} %fusion.10) | data formatting | bytes 11010048
  322.3 2.8 copy.88
  325.0 8.8 %multiply_reduce_fusion = (f32[512,4,2]{0,2,1:T(2,128)S(1)}, bf16[4,128,2,512]{3,1,2,0:T(8,128)(2,1)}) fusion(bf16[512,1024]{0,1:T(8,128)(2,1)S(1)} %copy-done.1, bf16[1536,4,128,1]{0,2,3,1:T(8,128)(2,1)S(1)} %copy.88, bf16[4,2,512,1536]{2,3,1,0:T(8,128)(2,1)} %copy-done), kind=kOutput, calls=%fused_computation.30 | convolution fusion | flops 1613230080 | bytes 16269312 | tf_op jit(solution)/shard_map/grnm,mgd->ngrd/dot_general | solution.py:62
  333.8 14.6 %fusion.2 = bf16[4,2,512,1536]{2,3,1,0:T(8,128)(2,1)} fusion(bf16[1536,4,128,1]{0,2,3,1:T(8,128)(2,1)S(1)} %copy.88, bf16[512,4,2,128]{0,3,2,1:T(8,128)(2,1)S(1)} %bitcast.125, f32[4,2,512]{2,1,0:T(2,128)S(1)} %bitcast.143, f32[4,2,512,1536]{2,3,1,0:T(8,128)} %get-tuple-element.43, f32[4,2,512]{2,1,0:T(2,128)S(1)} %get-tuple-element.42), kind=kOutput, calls=%fused_computation.3 | convolution fusion | flops 1635778560 | bytes 40402944 | tf_op jit(solution)/shard_map/ngrd,mgd->grnm/dot_general | solution.py:71
  348.5 9.3 %convolution_bitcast_fusion.1 = f32[1536,4,128]{0,2,1:T(8,128)S(1)} fusion(bf16[512,4,2,128]{3,0,2,1:T(8,128)(2,1)} %copy-done.6, bf16[4,2,512,1536]{2,3,1,0:T(8,128)(2,1)} %fusion.2), kind=kOutput, calls=%fused_computation.21 | convolution fusion | flops 1610612736 | bytes 16777216 | tf_op jit(solution)/shard_map/grnm,ngrd->mgd/dot_general | solution.py:76
  358.2 2.1 collective-permute-start.5
  360.2 1.9 collective-permute-start.4
  362.2 31.2 %collective-permute-done.5 = f32[512,512]{0,1:T(8,128)S(1)} collective-permute-done((f32[512,512]{0,1:T(8,128)S(1)}, f32[512,512]{0,1:T(8,128)S(1)}, u32[]{:S(2)}, u32[]{:S(2)}) %collective-permute-start.5) | collective-permute-done | bytes 1048608 | tf_op jit(solution)/shard_map/ppermute | solution.py:18
  393.3 9.5 %collective-permute-done.4 = f32[512,512]{0,1:T(8,128)S(1)} collective-permute-done((f32[512,512]{0,1:T(8,128)S(1)}, f32[512,512]{0,1:T(8,128)S(1)}, u32[]{:S(2)}, u32[]{:S(2)}) %collective-permute-start.4) | collective-permute-done | bytes 1048608 | tf_op jit(solution)/shard_map/ppermute | solution.py:18
  404.7 7.5 fusion.9
  412.2 8.3 %copy.105 = bf16[5376,512]{1,0:T(8,128)(2,1)} copy(bf16[5376,512]{0,1:T(8,128)(2,1)} %fusion.9) | data formatting | bytes 11010048
  421.9 6.6 fusion.24
  430.0 2.2 copy.114
  432.2 3.3 copy.113
  435.5 2.1 multiply_add_fusion
  438.3 11.1 %fusion.7 = bf16[5376,1024]{0,1:T(8,128)(2,1)} fusion(bf16[512,5376]{1,0:T(8,128)(2,1)} %param.6, bf16[64,8,8,128]{3,2,1,0:T(8,128)(2,1)S(1)} %bitcast.134), kind=kOutput, calls=%fused_computation.14 | convolution fusion | flops 5642649600 | bytes 17563648 | tf_op jit(solution)/shard_map/nd,nc->dc/dot_general | solution.py:177
  449.4 14.7 %copy.103 = bf16[5376,1024]{1,0:T(8,128)(2,1)} copy(bf16[5376,1024]{0,1:T(8,128)(2,1)} %fusion.7) | data formatting | bytes 22020096
  465.3 11.0 %fusion.8 = bf16[5376,1024]{0,1:T(8,128)(2,1)} fusion(bf16[512,1024]{0,1:T(8,128)(2,1)S(1)} %bitcast.133, bf16[512,5376]{1,0:T(8,128)(2,1)} %param.7), kind=kOutput, calls=%fused_computation.15 | convolution fusion | flops 5642649600 | bytes 17563648 | tf_op jit(solution)/shard_map/nd,nc->dc/dot_general | solution.py:138
  476.3 14.6 %copy.109 = bf16[5376,1024]{1,0:T(8,128)(2,1)} copy(bf16[5376,1024]{0,1:T(8,128)(2,1)} %fusion.8) | data formatting | bytes 22020096
  491.2 15.4 %fusion.16 = f32[512,5376]{0,1:T(8,128)} fusion(bf16[5376,1024]{1,0:T(8,128)(2,1)} %all-gather.7.cloned.1.call-done, bf16[64,8,8,128]{3,2,1,0:T(8,128)(2,1)S(1)} %bitcast.135), kind=kOutput, calls=%fused_computation.40 | convolution fusion | flops 5637144576 | bytes 23068672 | tf_op jit(solution)/shard_map/dot_general | solution.py:50
  506.7 8.3 %fusion.39 = f32[512,5376]{0,1:T(8,128)} fusion(bf16[5376,512]{1,0:T(8,128)(2,1)} %all-gather.5.cloned.1.call-done, bf16[512,512]{0,1:T(8,128)(2,1)S(1)} %bitcast.132), kind=kOutput, calls=%fused_computation.76 | convolution fusion | flops 2818572288 | bytes 17039360 | tf_op jit(solution)/shard_map/dot_general | solution.py:50
  515.0 14.0 %add_convert_fusion = bf16[512,5376]{0,1:T(8,128)(2,1)} fusion(f32[512,5376]{0,1:T(8,128)} %fusion.16, f32[512,5376]{0,1:T(8,128)} %fusion.39, bf16[5376,512]{1,0:T(8,128)(2,1)} %all-gather.9.cloned.1.call-done, bf16[512,512]{0,1:T(8,128)(2,1)S(1)} %copy-done.9), kind=kOutput, calls=%fused_computation.12 | convolution fusion | flops 2826829824 | bytes 33554432 | tf_op jit(solution)/shard_map/dot_general | solution.py:50
  534.5 31.4 %reduce-scatter.16.cloned.1.call-done = bf16[672,1024]{1,0:T(8,128)(2,1)} async-done(((bf16[5376,1024]{1,0:T(8,128)(2,1)}), bf16[672,1024]{1,0:T(8,128)(2,1)}) %reduce-scatter.16.cloned.1.call-update) | async-done | bytes 1376272
  569.4 84.4 %reduce-scatter.22.cloned.1.call-done = bf16[672,1024]{1,0:T(8,128)(2,1)} async-done(((bf16[5376,1024]{1,0:T(8,128)(2,1)}), bf16[672,1024]{1,0:T(8,128)(2,1)}) %reduce-scatter.22.cloned.1.call-update) | async-done | bytes 1376272
  655.5 1.9 copy.85
  657.5 97.5 %reduce-scatter.14.cloned.1.call-done = bf16[512,1344]{0,1:T(8,128)(2,1)} async-done(((bf16[512,5376]{0,1:T(8,128)(2,1)}), bf16[512,1344]{0,1:T(8,128)(2,1)}) %reduce-scatter.14.cloned.1.call-update) | async-done | bytes 1376272 | tf_op jit(solution)/shard_map/reduce_scatter | solution.py:174
  (98 shorter events, 35.0 us)
Async XLA Ops:
  7.2 46.5 %all-gather.5.cloned.1.call-start = ((), (), s32[]{:S(2)}) async-start(), calls=%async_computation.5 | async-start | bytes 6193152 | tf_op jit(solution)/shard_map/all_gather | solution.py:95
  7.9 125.5 %all-gather.11.cloned.1.call-start = ((), (), s32[]{:S(2)}) async-start(), calls=%async_computation.8 | async-start | bytes 12386304 | tf_op jit(solution)/shard_map/all_gather | solution.py:97
  8.6 192.0 %all-gather.7.cloned.1.call-start = ((), (), s32[]{:S(2)}) async-start(), calls=%async_computation.6 | async-start | bytes 12386304 | tf_op jit(solution)/shard_map/all_gather | solution.py:94
  9.4 246.4 %all-gather.9.cloned.1.call-start = ((), (), s32[]{:S(2)}) async-start(), calls=%async_computation.7 | async-start | bytes 6193152 | tf_op jit(solution)/shard_map/all_gather | solution.py:96
  10.0 519.1 %reduce-scatter.20.cloned.1.call-start = ((), (), s32[]{:S(2)}) async-start(), calls=%async_computation.12 | async-start | bytes 6193152
  11.1 200.3 %copy-start.2 = (f32[512,64]{1,0:T(8,128)}, f32[512,64]{1,0:T(8,128)S(1)}, u32[]{:S(2)}) copy-start(f32[512,64]{1,0:T(8,128)S(1)} %get-tuple-element.41) | copy-start | bytes 393220
  61.7 152.2 %copy-start.4 = (bf16[512,4,128]{2,0,1:T(8,128)(2,1)}, bf16[512,4,128]{2,0,1:T(8,128)(2,1)S(1)}, u32[]{:S(2)}) copy-start(bf16[512,4,128]{2,0,1:T(8,128)(2,1)S(1)} %maximum_convert_fusion) | copy-start | bytes 1572868
  61.9 24.9 %collective-permute-start.1 = (bf16[512,512]{0,1:T(8,128)(2,1)S(1)}, bf16[512,512]{0,1:T(8,128)(2,1)S(1)}, u32[]{:S(2)}, u32[]{:S(2)}) collective-permute-start(bf16[512,512]{0,1:T(8,128)(2,1)S(1)} %bitcast.139), channel_id=1, source_target_pairs={{0,4},{4,8},{8,12},{12,16},{16,20},{20,24},{24,28},{1,5},{5,9},{9,... | collective-permute-start | bytes 1572872 | tf_op jit(solution)/shard_map/ppermute | solution.py:18
  64.9 31.5 %collective-permute-start = (bf16[512,512]{0,1:T(8,128)(2,1)S(1)}, bf16[512,512]{0,1:T(8,128)(2,1)S(1)}, u32[]{:S(2)}, u32[]{:S(2)}) collective-permute-start(bf16[512,512]{0,1:T(8,128)(2,1)S(1)} %bitcast.140), channel_id=1, source_target_pairs={{0,8},{4,12},{8,16},{12,20},{16,24},{20,28},{1,9},{5,13},{9,17},{1... | collective-permute-start | bytes 1572872 | tf_op jit(solution)/shard_map/ppermute | solution.py:18
  87.1 126.8 %copy-start.10 = (bf16[512,4,128]{2,0,1:T(8,128)(2,1)}, bf16[512,4,128]{2,0,1:T(8,128)(2,1)S(1)}, u32[]{:S(2)}) copy-start(bf16[512,4,128]{2,0,1:T(8,128)(2,1)S(1)} %copy.63) | copy-start | bytes 1572868
  96.7 117.2 %copy-start.12 = (bf16[512,4,128]{2,0,1:T(8,128)(2,1)}, bf16[512,4,128]{2,0,1:T(8,128)(2,1)S(1)}, u32[]{:S(2)}) copy-start(bf16[512,4,128]{2,0,1:T(8,128)(2,1)S(1)} %copy.62) | copy-start | bytes 1572868
  213.9 14.7 %copy-start.6 = (bf16[512,4,2,128]{3,0,2,1:T(8,128)(2,1)}, bf16[512,4,2,128]{3,0,2,1:T(8,128)(2,1)S(1)}, u32[]{:S(2)}) copy-start(bf16[512,4,2,128]{3,0,2,1:T(8,128)(2,1)S(1)} %fusion.13) | copy-start | bytes 3145732
  239.5 7.9 %copy-start = (bf16[4,2,512,1536]{2,3,1,0:T(8,128)(2,1)}, bf16[4,2,512,1536]{2,3,1,0:T(8,128)(2,1)S(1)}, u32[]{:S(2)}) copy-start(bf16[4,2,512,1536]{2,3,1,0:T(8,128)(2,1)S(1)} %fusion.6) | copy-start | bytes 37748740
  250.9 27.4 %collective-permute-start.7 = (f32[512,512]{0,1:T(8,128)}, f32[512,512]{0,1:T(8,128)S(1)}, u32[]{:S(2)}, u32[]{:S(2)}) collective-permute-start(f32[512,512]{0,1:T(8,128)} %bitcast.33), channel_id=1, source_target_pairs={{8,0},{12,4},{16,8},{20,12},{24,16},{28,20},{9,1},{13,5},{17,9},{2... | collective-permute-start | bytes 3145736 | tf_op jit(solution)/shard_map/ppermute | solution.py:18
  253.1 48.3 %copy-start.7 = (f32[512,4,128]{0,2,1:T(8,128)S(1)}, f32[512,4,128]{0,2,1:T(8,128)}, u32[]{:S(2)}) copy-start(f32[512,4,128]{0,2,1:T(8,128)} %get-tuple-element.22) | copy-start | bytes 3145732
  253.1 48.3 %collective-permute-start.6 = (f32[512,512]{0,1:T(8,128)}, f32[512,512]{0,1:T(8,128)}, u32[]{:S(2)}, u32[]{:S(2)}) collective-permute-start(f32[512,512]{0,1:T(8,128)} %bitcast.32), channel_id=1, source_target_pairs={{4,0},{8,4},{12,8},{16,12},{20,16},{24,20},{28,24},{5,1},{9,5},{13... | collective-permute-start | bytes 3145736 | tf_op jit(solution)/shard_map/ppermute | solution.py:18
  263.8 55.1 %collective-permute-start.3 = (bf16[512,512]{1,0:T(8,128)(2,1)}, bf16[512,512]{1,0:T(8,128)(2,1)}, u32[]{:S(2)}, u32[]{:S(2)}) collective-permute-start(bf16[512,512]{1,0:T(8,128)(2,1)} %convolution_convert_fusion.6), channel_id=1, source_target_pairs={{0,4},{4,8},{8,12},{12,16},{16,20},{20,24},{24,28},{1,5},{5,9},{9,... | collective-permute-start | bytes 1572872 | tf_op jit(solution)/shard_map/ppermute | solution.py:18
  267.8 51.1 %collective-permute-start.2 = (bf16[512,512]{1,0:T(8,128)(2,1)}, bf16[512,512]{1,0:T(8,128)(2,1)}, u32[]{:S(2)}, u32[]{:S(2)}) collective-permute-start(bf16[512,512]{1,0:T(8,128)(2,1)} %convolution_convert_fusion.6), channel_id=1, source_target_pairs={{0,8},{4,12},{8,16},{12,20},{16,24},{20,28},{1,9},{5,13},{9,17},{1... | collective-permute-start | bytes 1572872 | tf_op jit(solution)/shard_map/ppermute | solution.py:18
  302.9 7.5 copy-start.8
  318.8 6.3 copy-start.1
  318.8 213.0 %reduce-scatter.18.cloned.1.call-start = ((), (), s32[]{:S(2)}) async-start(), calls=%async_computation.11 | async-start | bytes 6193152
  358.2 45.7 %copy-start.3 = (f32[512,64]{1,0:T(8,128)S(1)}, f32[512,64]{1,0:T(8,128)}, u32[]{:S(2)}) copy-start(f32[512,64]{1,0:T(8,128)} %copy-done.2) | copy-start | bytes 393220
  358.2 35.2 %collective-permute-start.5 = (f32[512,512]{0,1:T(8,128)S(1)}, f32[512,512]{0,1:T(8,128)S(1)}, u32[]{:S(2)}, u32[]{:S(2)}) collective-permute-start(f32[512,512]{0,1:T(8,128)S(1)} %bitcast.138), channel_id=1, source_target_pairs={{8,0},{12,4},{16,8},{20,12},{24,16},{28,20},{9,1},{13,5},{17,9},{2... | collective-permute-start | bytes 3145736 | tf_op jit(solution)/shard_map/ppermute | solution.py:18
  360.2 42.6 %collective-permute-start.4 = (f32[512,512]{0,1:T(8,128)S(1)}, f32[512,512]{0,1:T(8,128)S(1)}, u32[]{:S(2)}, u32[]{:S(2)}) collective-permute-start(f32[512,512]{0,1:T(8,128)S(1)} %bitcast.137), channel_id=1, source_target_pairs={{4,0},{8,4},{12,8},{16,12},{20,16},{24,20},{28,24},{5,1},{9,5},{13... | collective-permute-start | bytes 3145736 | tf_op jit(solution)/shard_map/ppermute | solution.py:18
  404.7 7.5 copy-start.14
  420.5 1.0 copy-start.5
  420.5 1.2 copy-start.11
  420.5 1.4 copy-start.13
  420.5 145.3 %reduce-scatter.16.cloned.1.call-start = ((), (), s32[]{:S(2)}) async-start(), calls=%async_computation.10 | async-start | bytes 12386304
  464.1 1.2 copy-start.16
  464.1 189.8 %reduce-scatter.22.cloned.1.call-start = ((), (), s32[]{:S(2)}) async-start(), calls=%async_computation.13 | async-start | bytes 12386304
  491.0 15.7 %copy-start.15 = (bf16[512,4,128]{0,2,1:T(8,128)(2,1)S(1)}, bf16[512,4,128]{0,2,1:T(8,128)(2,1)}, u32[]{:S(2)}) copy-start(bf16[512,4,128]{0,2,1:T(8,128)(2,1)} %copy-done.14) | copy-start | bytes 1572868
  491.0 263.9 %reduce-scatter.14.cloned.1.call-start = ((), (), s32[]{:S(2)}) async-start(), calls=%async_computation.9 | async-start | bytes 6881280 | tf_op jit(solution)/shard_map/reduce_scatter | solution.py:174
  506.7 8.3 %copy-start.9 = (bf16[512,512]{0,1:T(8,128)(2,1)S(1)}, bf16[512,512]{0,1:T(8,128)(2,1)}, u32[]{:S(2)}) copy-start(bf16[512,512]{0,1:T(8,128)(2,1)} %copy-done.8) | copy-start | bytes 1572868
Sparse Core Ops, SparseCore 0:
  9.9 43.7 all-gather.4
  55.5 77.8 all-gather.10
  135.3 65.3 all-gather.6
  202.4 42.0 all-gather.8
  318.9 69.5 reduce-scatter.19
  420.7 57.0 reduce-scatter.17
  481.4 84.4 reduce-scatter.15
  569.4 84.4 reduce-scatter.21
  656.7 98.1 reduce-scatter.13
where the time goes:
time: 769 us; the launch traced here: 762 us
  waiting for transfers between devices  449 us (58%)
  matrix products  172 us (22%)
  local copies, waits for them, and re-layouts  81.4 us (11%)
  other arithmetic  22.7 us (3%)
  starting transfers between devices  22.2 us (3%)
  between operations  14.6 us (2%)
    unnamed x13, waiting for transfers between devices  118 us
    ppermute x8, waiting for transfers between devices, from_behind(): lax.ppermute(value, axis, [(source, source + steps) for source in range(i...  97.8 us
    reduce_scatter x1, waiting for transfers between devices, shards(): lax.psum_scatter(partial_in.astype(jnp.bfloat16), 'head', scatter_dimensi...  97.5 us
    unnamed x53, local copies, waits for them, and re-layouts  68.1 us
    all_gather x1, waiting for transfers between devices, shards(): lax.all_gather(w_query, 'ctx', axis=0, tiled=True)  55.7 us
    all_gather x1, waiting for transfers between devices, shards(): lax.all_gather(key_weight, 'ctx', axis=0, tiled=True)  42.6 us
    dot_general x3, matrix products, dot_rows(): lax.dot_general(left, weight, (((1,), (1,)), ((), ())), preferred_element...  37.8 us
    all_gather x1, waiting for transfers between devices, shards(): lax.all_gather(w_out, 'ctx', axis=0, tiled=True)  36.7 us
  transfers between devices with their start and end apart: 17, of which 12 were waited for; matrix products, arithmetic and copies ran while one was open for 36% of the time, Pallas kernels for 0%

commit v1 on v0

--- a/solution.py
+++ b/solution.py
@@ -51,6 +51,17 @@
         left, weight, (((1,), (1,)), ((), ())), preferred_element_type=jnp.float32
     )
 
+
+def gather_rows(value):
+    return lax.all_gather(value, "ctx", axis=0, tiled=True)
+
+
+def block_sums(left, right, blocks):
+    rows = left.shape[0] // blocks
+    left = left.reshape(blocks, rows, left.shape[1])
+    right = right.reshape(blocks, rows, right.shape[1])
+    parts = jnp.einsum("bnd,bnc->bdc", left, right, preferred_element_type=jnp.float32)
+    return jnp.sum(parts.astype(jnp.bfloat16).astype(jnp.float32), axis=0)
 
 def attend_forward(query_rows, key_rows, value_rows, allowed):
     score = jnp.einsum("ngrd,mgd->grnm", query_rows, key_rows, preferred_element_type=jnp.float32)
@@ -135,9 +146,6 @@
     grouped_grads = attention_gradient.reshape(rows, local_groups, group_ratio, head_size)
     prob, prob_b, attended = attend_forward(grouped_queries, keys_all, values_all, allowed)
     attended_flat = attended.reshape(rows, query_cols)
-    grad_w_out = jnp.einsum(
-        "nd,nc->dc", out_grad, attended_flat, preferred_element_type=jnp.float32
-    )
     grad_q, grad_k, grad_v = attend_backward(
         prob, prob_b, attended, grouped_grads, grouped_queries, keys_all, values_all
     )
@@ -174,27 +182,13 @@
     in_grad = lax.psum_scatter(
         partial_in.astype(jnp.bfloat16), "head", scatter_dimension=1, tiled=True
     )
-    grad_q_part = jnp.einsum("nd,nc->dc", hidden_in, dquery, preferred_element_type=jnp.float32)
-    grad_k_part = jnp.einsum(
-        "nd,nc->dc", hidden_in, key_gradient, preferred_element_type=jnp.float32
-    )
-    grad_v_part = jnp.einsum(
-        "nd,nc->dc", hidden_in, value_gradient, preferred_element_type=jnp.float32
-    )
-    grad_query, grad_key, grad_value, grad_out_w = (
-        lax.psum_scatter(
-            grad_q_part.astype(jnp.bfloat16), "ctx", scatter_dimension=0, tiled=True
-        ).astype(jnp.float32),
-        lax.psum_scatter(
-            grad_k_part.astype(jnp.bfloat16), "ctx", scatter_dimension=0, tiled=True
-        ).astype(jnp.float32),
-        lax.psum_scatter(
-            grad_v_part.astype(jnp.bfloat16), "ctx", scatter_dimension=0, tiled=True
-        ).astype(jnp.float32),
-        lax.psum_scatter(
-            grad_w_out.astype(jnp.bfloat16), "ctx", scatter_dimension=0, tiled=True
-        ).astype(jnp.float32),
-    )
+    n_ctx = lax.axis_size("ctx")
+    hidden_cols = lax.all_to_all(hidden_in, "ctx", 1, 0, tiled=True)
+    out_grad_cols = lax.all_to_all(out_grad, "ctx", 1, 0, tiled=True)
+    grad_query = block_sums(hidden_cols, gather_rows(dquery), n_ctx)
+    grad_key = block_sums(hidden_cols, gather_rows(key_gradient), n_ctx)
+    grad_value = block_sums(hidden_cols, gather_rows(value_gradient), n_ctx)
+    grad_out_w = block_sums(out_grad_cols, gather_rows(attended_flat), n_ctx)
     return (in_grad, grad_query, grad_key, grad_value, grad_out_w)
 
 

time: 769 us -> 746 us (0.970)
  waiting for transfers between devices: 449 us -> 411 us
  starting transfers between devices: 22.2 us -> 48.4 us
  local copies, waits for them, and re-layouts: 81.4 us -> 69.9 us
    unnamed x13 -> x9, waiting for transfers between devices: 118 us -> 3.34 us
    all_gather x0 -> x4, waiting for transfers between devices: none -> 87.9 us  [gather_rows(): return lax.all_gather(value, 'ctx', axis=0, tiled=True)]
    unnamed x53 -> x32, local copies, waits for them, and re-layouts: 68.1 us -> 26.1 us
    all_to_all x0 -> x2, waiting for transfers between devices: none -> 32.1 us  [the longest x1 32.1 us: shards(): hidden_cols = lax.all_to_all(hidden_in, 'ctx', 1, 0, tiled=True)]
    all_gather x0 -> x3, local copies, waits for them, and re-layouts: none -> 25.2 us  [gather_rows(): return lax.all_gather(value, 'ctx', axis=0, tiled=True)]
    reduce_scatter x1, waiting for transfers between devices: 97.5 us -> 76.5 us  [shards(): lax.psum_scatter(partial_in.astype(jnp.bfloat16), 'head', scatter_dimensi...]
    all_to_all x0 -> x2, starting transfers between devices: none -> 19.3 us  [the longest x1 12.8 us: shards(): hidden_cols = lax.all_to_all(hidden_in, 'ctx', 1, 0, tiled=True)]
    all_gather x1, waiting for transfers between devices: 55.7 us -> 36.5 us  [shards(): lax.all_gather(w_query, 'ctx', axis=0, tiled=True)]
  transfers between devices with their start and end apart: 17 -> 19, of which waited for: 12 -> 15; matrix products, arithmetic and copies ran while one was open for 36% -> 36% of each run, Pallas kernels for 0% -> 0%
where the time goes in v1:
time: 746 us; the launch traced here: 739 us
  waiting for transfers between devices  411 us (55%)
  matrix products  169 us (23%)
  local copies, waits for them, and re-layouts  69.9 us (9%)
  starting transfers between devices  48.4 us (6%)
  other arithmetic  25.6 us (3%)
  between operations  14.5 us (2%)
    all_gather x4, waiting for transfers between devices, gather_rows(): return lax.all_gather(value, 'ctx', axis=0, tiled=True)  87.9 us
    ppermute x8, waiting for transfers between devices, from_behind(): lax.ppermute(value, axis, [(source, source + steps) for source in range(i...  79.1 us
    reduce_scatter x1, waiting for transfers between devices, shards(): lax.psum_scatter(partial_in.astype(jnp.bfloat16), 'head', scatter_dimensi...  76.5 us
    all_gather x1, waiting for transfers between devices, shards(): lax.all_gather(w_out, 'ctx', axis=0, tiled=True)  53.3 us
    all_gather x1, waiting for transfers between devices, shards(): lax.all_gather(key_weight, 'ctx', axis=0, tiled=True)  42.6 us
    dot_general x4, matrix products, block_sums(): jnp.einsum('bnd,bnc->bdc', left, right, preferred_element_type=jnp.float32)  39 us
    all_gather x1, waiting for transfers between devices, shards(): lax.all_gather(w_query, 'ctx', axis=0, tiled=True)  36.5 us
    dot_general x3, matrix products, dot_rows(): lax.dot_general(left, weight, (((1,), (1,)), ((), ())), preferred_element...  34.4 us
  transfers between devices with their start and end apart: 19, of which 15 were waited for; matrix products, arithmetic and copies ran while one was open for 36% of the time, Pallas kernels for 0%

profile of v1, /device:TPU:3, one launch (start us, length us, event | category | flops | bytes accessed | tf_op | source)
XLA Modules:
  0.0 739.0 jit_solution(2174743812924072082)
XLA Ops:
  11.1 42.6 %all-gather.9.cloned.1.call-done = bf16[5376,512]{1,0:T(8,128)(2,1)} async-done(((bf16[672,512]{1,0:T(8,128)(2,1)}), bf16[5376,512]{1,0:T(8,128)(2,1)}) %all-gather.9.cloned.1.call-update) | async-done | bytes 5505040 | tf_op jit(solution)/shard_map/all_gather | solution.py:106
  53.6 6.7 fusion.40
  61.9 2.9 collective-permute-start
  64.8 3.0 collective-permute-start.1
  69.7 19.1 %collective-permute-done = bf16[512,512]{0,1:T(8,128)(2,1)S(1)} collective-permute-done((bf16[512,512]{0,1:T(8,128)(2,1)S(1)}, bf16[512,512]{0,1:T(8,128)(2,1)S(1)}, u32[]{:S(2)}, u32[]{:S(2)}) %collective-permute-start) | collective-permute-done | bytes 524320 | tf_op jit(solution)/shard_map/ppermute | solution.py:18
  89.9 6.1 collective-permute-done.1
  96.9 36.5 %all-gather.11.cloned.1.call-done = bf16[5376,1024]{1,0:T(8,128)(2,1)} async-done(((bf16[672,1024]{1,0:T(8,128)(2,1)}), bf16[5376,1024]{1,0:T(8,128)(2,1)}) %all-gather.11.cloned.1.call-update) | async-done | bytes 11010064 | tf_op jit(solution)/shard_map/all_gather | solution.py:105
  133.4 10.2 %convolution_bitcast_fusion.2 = f32[64,8,8,128]{3,1,2,0:T(8,128)S(1)} fusion(bf16[512,5376]{1,0:T(8,128)(2,1)} %param.6, bf16[5376,1024]{1,0:T(8,128)(2,1)} %all-gather.11.cloned.1.call-done), kind=kOutput, calls=%fused_computation.35 | convolution fusion | flops 5637144576 | bytes 18612224 | tf_op jit(solution)/shard_map/dot_general | solution.py:110
  147.4 53.3 %all-gather.15.cloned.1.call-done = bf16[5376,1024]{1,0:T(8,128)(2,1)} async-done(((bf16[672,1024]{1,0:T(8,128)(2,1)}), bf16[5376,1024]{1,0:T(8,128)(2,1)}) %all-gather.15.cloned.1.call-update) | async-done | bytes 11010064 | tf_op jit(solution)/shard_map/all_gather | solution.py:108
  200.7 11.0 %convolution_convert_fusion = bf16[512,1024]{1,0:T(8,128)(2,1)} fusion(bf16[512,5376]{1,0:T(8,128)(2,1)} %param.7, bf16[5376,1024]{1,0:T(8,128)(2,1)} %all-gather.15.cloned.1.call-done), kind=kOutput, calls=%fused_computation.38 | convolution fusion | flops 5637668864 | bytes 17563648 | tf_op jit(solution)/shard_map/dot_general | solution.py:113
  214.0 3.2 fusion.19
  217.1 14.6 %fusion.39 = (f32[4,2,512]{2,1,0:T(2,128)S(1)}, f32[4,2,512,1536]{2,3,1,0:T(8,128)}) fusion(pred[512,1536]{0,1:T(8,128)(4,1)} %and_and_fusion, bf16[512,4,2,128]{3,0,2,1:T(8,128)(2,1)} %fusion.19, bf16[512,4,128]{2,0,1:T(8,128)(2,1)S(1)} %maximum_convert_fusion, bf16[512,4,128]{2,0,1:T(8,128)(2,1)} %copy.36, bf16[512,4,128]{2,0,1:T(8,128)(2,1)} %copy.35), kind=kOutput, calls=%fused_computation.73 | convolution fusion | flops 1634207232 | bytes 28590080 | tf_op jit(solution)/shard_map/sub | solution.py:70
  231.8 10.5 %fusion.6 = bf16[4,2,512,1536]{2,3,1,0:T(8,128)(2,1)S(1)} fusion(f32[4,2,512,1536]{2,3,1,0:T(8,128)} %get-tuple-element.28, f32[4,2,512]{2,1,0:T(2,128)S(1)} %get-tuple-element.27), kind=kLoop, calls=%fused_computation.15 | loop fusion | flops 12582912 | bytes 37765120 | tf_op jit(solution)/shard_map/convert_element_type | solution.py:72
  242.3 7.9 %convolution_bitcast_fusion = f32[1536,4,128]{0,2,1:T(8,128)} fusion(bf16[512,4,2,128]{0,3,2,1:T(8,128)(2,1)} %bitcast.134, bf16[4,2,512,1536]{2,3,1,0:T(8,128)(2,1)S(1)} %fusion.6), kind=kOutput, calls=%fused_computation.22 | convolution fusion | flops 1610612736 | bytes 16777216 | tf_op jit(solution)/shard_map/grnm,ngrd->mgd/dot_general | solution.py:90
  250.2 3.6 fusion.34
  258.4 7.2 convolution_convert_fusion.2
  265.6 4.0 collective-permute-start.2
  269.6 4.8 collective-permute-start.3
  274.5 5.9 collective-permute-done.6
  280.4 4.0 collective-permute-done.7
  286.9 5.9 collective-permute-done.2
  292.8 11.2 %collective-permute-done.3 = bf16[512,512]{1,0:T(8,128)(2,1)} collective-permute-done((bf16[512,512]{1,0:T(8,128)(2,1)S(1)}, bf16[512,512]{1,0:T(8,128)(2,1)}, u32[]{:S(2)}, u32[]{:S(2)}) %collective-permute-start.3) | collective-permute-done | bytes 524320 | tf_op jit(solution)/shard_map/ppermute | solution.py:18
  310.0 7.8 %multiply_reduce_fusion = (f32[512,4,2]{0,2,1:T(2,128)S(1)}, bf16[4,128,2,512]{3,1,2,0:T(8,128)(2,1)}) fusion(bf16[512,1024]{0,1:T(8,128)(2,1)S(1)} %copy-done.1, bf16[1536,4,128,1]{0,2,3,1:T(8,128)(2,1)S(1)} %copy.62, bf16[4,2,512,1536]{2,3,1,0:T(8,128)(2,1)} %copy-done), kind=kOutput, calls=%fused_computation.32 | convolution fusion | flops 1613230080 | bytes 16269312 | tf_op jit(solution)/shard_map/grnm,mgd->ngrd/dot_general | solution.py:73
  317.8 14.4 %fusion.2 = bf16[4,2,512,1536]{2,3,1,0:T(8,128)(2,1)} fusion(bf16[1536,4,128,1]{0,2,3,1:T(8,128)(2,1)S(1)} %copy.62, bf16[512,4,2,128]{0,3,2,1:T(8,128)(2,1)S(1)} %bitcast.135, f32[4,2,512]{2,1,0:T(2,128)S(1)} %bitcast.157, f32[4,2,512,1536]{2,3,1,0:T(8,128)} %get-tuple-element.28, f32[4,2,512]{2,1,0:T(2,128)S(1)} %get-tuple-element.27), kind=kOutput, calls=%fused_computation.3 | convolution fusion | flops 1635778560 | bytes 40402944 | tf_op jit(solution)/shard_map/ngrd,mgd->grnm/dot_general | solution.py:82
  332.1 9.2 %convolution_bitcast_fusion.1 = f32[1536,4,128]{0,2,1:T(8,128)S(1)} fusion(bf16[512,4,2,128]{3,0,2,1:T(8,128)(2,1)} %fusion.19, bf16[4,2,512,1536]{2,3,1,0:T(8,128)(2,1)} %fusion.2), kind=kOutput, calls=%fused_computation.23 | convolution fusion | flops 1610612736 | bytes 16777216 | tf_op jit(solution)/shard_map/grnm,ngrd->mgd/dot_general | solution.py:87
  341.8 6.9 collective-permute-start.4
  351.1 23.0 %collective-permute-done.4 = f32[512,512]{0,1:T(8,128)S(1)} collective-permute-done((f32[512,512]{0,1:T(8,128)S(1)}, f32[512,512]{0,1:T(8,128)S(1)}, u32[]{:S(2)}, u32[]{:S(2)}) %collective-permute-start.4) | collective-permute-done | bytes 1048608 | tf_op jit(solution)/shard_map/ppermute | solution.py:18
  374.1 3.8 collective-permute-done.5
  383.3 6.8 fusion.25
  393.7 3.2 copy.80
  400.8 8.3 %copy.55 = bf16[512,5376]{0,1:T(8,128)(2,1)} copy(bf16[512,5376]{1,0:T(8,128)(2,1)} %param.6) | data formatting | bytes 11010048 | tf_op args[0]
  409.1 12.8 %all-to-all-start = ((bf16[512,8,672]{0,2,1:T(8,128)(2,1)}), bf16[512,8,672]{0,2,1:T(8,128)(2,1)}, u32[]{:S(2)}, u32[]{:S(2)}) async-start(bf16[512,8,672]{0,2,1:T(8,128)(2,1)} %bitcast.132), calls=%async_computation.1 | async-start | bytes 11010048 | tf_op jit(solution)/shard_map/all_to_all | solution.py:186
  422.1 12.8 %fusion.33 = f32[512,5376]{0,1:T(8,128)} fusion(bf16[5376,1024]{1,0:T(8,128)(2,1)} %all-gather.11.cloned.1.call-done, bf16[64,8,8,128]{3,2,1,0:T(8,128)(2,1)S(1)} %bitcast.145), kind=kOutput, calls=%fused_computation.67 | convolution fusion | flops 5637144576 | bytes 23068672 | tf_op jit(solution)/shard_map/dot_general | solution.py:50
  435.0 8.3 %fusion.41 = f32[512,5376]{0,1:T(8,128)} fusion(bf16[5376,512]{1,0:T(8,128)(2,1)} %all-gather.9.cloned.1.call-done, bf16[512,512]{0,1:T(8,128)(2,1)S(1)} %bitcast.142), kind=kOutput, calls=%fused_computation.75 | convolution fusion | flops 2818572288 | bytes 17039360 | tf_op jit(solution)/shard_map/dot_general | solution.py:50
  443.3 13.3 %add_convert_fusion = bf16[512,5376]{0,1:T(8,128)(2,1)} fusion(f32[512,5376]{0,1:T(8,128)} %fusion.33, f32[512,5376]{0,1:T(8,128)} %fusion.41, bf16[5376,512]{1,0:T(8,128)(2,1)} %all-gather.13.cloned.1.call-done, bf16[512,512]{0,1:T(8,128)(2,1)S(1)} %copy-done.4), kind=kOutput, calls=%fused_computation.14 | convolution fusion | flops 2826829824 | bytes 33554432 | tf_op jit(solution)/shard_map/dot_general | solution.py:50
  456.6 8.5 %copy.59 = bf16[512,5376]{0,1:T(8,128)(2,1)} copy(bf16[512,5376]{1,0:T(8,128)(2,1)} %param.7) | data formatting | bytes 11010048 | tf_op args[1]
  465.1 32.1 %all-to-all-done = bf16[512,8,672]{0,2,1:T(8,128)(2,1)} async-done(((bf16[512,8,672]{0,2,1:T(8,128)(2,1)}), bf16[512,8,672]{0,2,1:T(8,128)(2,1)}, u32[]{:S(2)}, u32[]{:S(2)}) %all-to-all-start) | async-done | bytes 5505056 | tf_op jit(solution)/shard_map/all_to_all | solution.py:186
  497.1 6.5 all-to-all-start.1
  503.7 6.5 copy.57
  510.2 6.5 copy.56
  516.7 8.1 %convert_reduce_fusion.2 = f32[512,672]{0,1:T(8,128)} fusion(bf16[8,512,512]{2,1,0:T(8,128)(2,1)} %bitcast.146, bf16[512,8,672]{0,2,1:T(8,128)(2,1)} %all-to-all-done), kind=kOutput, calls=%fused_computation.12 | convolution fusion | flops 2826485760 | bytes 11075584 | tf_op jit(solution)/shard_map/bnd,bnc->bdc/dot_general | solution.py:63
  524.9 6.9 convert_reduce_fusion.3
  531.8 43.2 %all-gather.23.cloned.1.call-done = bf16[4096,1024]{0,1:T(8,128)(2,1)} async-done(((bf16[512,1024]{0,1:T(8,128)(2,1)}), bf16[4096,1024]{0,1:T(8,128)(2,1)}) %all-gather.23.cloned.1.call-update) | async-done | bytes 8388624 | tf_op jit(solution)/shard_map/all_gather | solution.py:56
  575.0 12.1 %copy.58 = bf16[4096,1024]{1,0:T(8,128)(2,1)} copy(bf16[4096,1024]{0,1:T(8,128)(2,1)} %all-gather.23.cloned.1.call-done) | data formatting | bytes 16777216 | tf_op jit(solution)/shard_map/all_gather | solution.py:56
  587.1 44.7 %all-gather.17.cloned.1.call-done = bf16[4096,1024]{1,0:T(8,128)(2,1)} async-done(((bf16[512,1024]{1,0:T(8,128)(2,1)}), bf16[4096,1024]{1,0:T(8,128)(2,1)}) %all-gather.17.cloned.1.call-update) | async-done | bytes 8388624 | tf_op jit(solution)/shard_map/all_gather | solution.py:56
  631.8 12.0 %convert_reduce_fusion.1 = f32[1024,672]{0,1:T(8,128)} fusion(bf16[8,512,1024]{2,1,0:T(8,128)(2,1)} %bitcast.158, bf16[512,8,672]{0,2,1:T(8,128)(2,1)} %all-to-all-done), kind=kOutput, calls=%fused_computation.8 | convolution fusion | flops 5652971520 | bytes 16646144 | tf_op jit(solution)/shard_map/bnd,bnc->bdc/dot_general | solution.py:63
  643.8 12.0 %convert_reduce_fusion = f32[1024,672]{0,1:T(8,128)} fusion(bf16[8,512,1024]{2,1,0:T(8,128)(2,1)} %bitcast.136, bf16[512,8,672]{0,2,1:T(8,128)(2,1)} %all-to-all-done.1), kind=kOutput, calls=%fused_computation.7 | convolution fusion | flops 5652971520 | bytes 16646144 | tf_op jit(solution)/shard_map/bnd,bnc->bdc/dot_general | solution.py:63
  655.7 76.5 %reduce-scatter.2.cloned.1.call-done = bf16[512,1344]{0,1:T(8,128)(2,1)} async-done(((bf16[512,5376]{0,1:T(8,128)(2,1)}), bf16[512,1344]{0,1:T(8,128)(2,1)}) %reduce-scatter.2.cloned.1.call-update) | async-done | bytes 1376272 | tf_op jit(solution)/shard_map/reduce_scatter | solution.py:182
  (84 shorter events, 43.9 us)
Async XLA Ops:
  7.2 46.5 %all-gather.9.cloned.1.call-start = ((), (), s32[]{:S(2)}) async-start(), calls=%async_computation.3 | async-start | bytes 6193152 | tf_op jit(solution)/shard_map/all_gather | solution.py:106
  7.9 125.5 %all-gather.11.cloned.1.call-start = ((), (), s32[]{:S(2)}) async-start(), calls=%async_computation.4 | async-start | bytes 12386304 | tf_op jit(solution)/shard_map/all_gather | solution.py:105
  8.6 192.0 %all-gather.15.cloned.1.call-start = ((), (), s32[]{:S(2)}) async-start(), calls=%async_computation.6 | async-start | bytes 12386304 | tf_op jit(solution)/shard_map/all_gather | solution.py:108
  9.4 249.0 %all-gather.13.cloned.1.call-start = ((), (), s32[]{:S(2)}) async-start(), calls=%async_computation.5 | async-start | bytes 6193152 | tf_op jit(solution)/shard_map/all_gather | solution.py:107
  10.0 493.7 %all-gather.21.cloned.1.call-start = ((), (), s32[]{:S(2)}) async-start(), calls=%async_computation.10 | async-start | bytes 4718592 | tf_op jit(solution)/shard_map/all_gather | solution.py:56
  11.1 133.1 %copy-start.2 = (f32[512,64]{1,0:T(8,128)}, f32[512,64]{1,0:T(8,128)S(1)}, u32[]{:S(2)}) copy-start(f32[512,64]{1,0:T(8,128)S(1)} %get-tuple-element.26) | copy-start | bytes 393220
  61.7 155.5 %copy-start.5 = (bf16[512,4,128]{2,0,1:T(8,128)(2,1)}, bf16[512,4,128]{2,0,1:T(8,128)(2,1)S(1)}, u32[]{:S(2)}) copy-start(bf16[512,4,128]{2,0,1:T(8,128)(2,1)S(1)} %maximum_convert_fusion) | copy-start | bytes 1572868
  61.9 27.0 %collective-permute-start = (bf16[512,512]{0,1:T(8,128)(2,1)S(1)}, bf16[512,512]{0,1:T(8,128)(2,1)S(1)}, u32[]{:S(2)}, u32[]{:S(2)}) collective-permute-start(bf16[512,512]{0,1:T(8,128)(2,1)S(1)} %bitcast.153), channel_id=1, source_target_pairs={{0,8},{4,12},{8,16},{12,20},{16,24},{20,28},{1,9},{5,13},{9,17},{1... | collective-permute-start | bytes 1572872 | tf_op jit(solution)/shard_map/ppermute | solution.py:18
  64.8 31.1 %collective-permute-start.1 = (bf16[512,512]{0,1:T(8,128)(2,1)S(1)}, bf16[512,512]{0,1:T(8,128)(2,1)S(1)}, u32[]{:S(2)}, u32[]{:S(2)}) collective-permute-start(bf16[512,512]{0,1:T(8,128)(2,1)S(1)} %bitcast.154), channel_id=1, source_target_pairs={{0,4},{4,8},{8,12},{12,16},{16,20},{20,24},{24,28},{1,5},{5,9},{9,... | collective-permute-start | bytes 1572872 | tf_op jit(solution)/shard_map/ppermute | solution.py:18
  242.3 7.9 %copy-start = (bf16[4,2,512,1536]{2,3,1,0:T(8,128)(2,1)}, bf16[4,2,512,1536]{2,3,1,0:T(8,128)(2,1)S(1)}, u32[]{:S(2)}) copy-start(bf16[4,2,512,1536]{2,3,1,0:T(8,128)(2,1)S(1)} %fusion.6) | copy-start | bytes 37748740
  253.8 26.6 %collective-permute-start.6 = (f32[512,512]{0,1:T(8,128)}, f32[512,512]{0,1:T(8,128)S(1)}, u32[]{:S(2)}, u32[]{:S(2)}) collective-permute-start(f32[512,512]{0,1:T(8,128)} %bitcast.32), channel_id=1, source_target_pairs={{4,0},{8,4},{12,8},{16,12},{20,16},{24,20},{28,24},{5,1},{9,5},{13... | collective-permute-start | bytes 3145736 | tf_op jit(solution)/shard_map/ppermute | solution.py:18
  256.0 28.4 %copy-start.9 = (f32[512,4,128]{0,2,1:T(8,128)S(1)}, f32[512,4,128]{0,2,1:T(8,128)}, u32[]{:S(2)}) copy-start(f32[512,4,128]{0,2,1:T(8,128)} %get-tuple-element.7) | copy-start | bytes 3145732
  256.0 28.4 %collective-permute-start.7 = (f32[512,512]{0,1:T(8,128)}, f32[512,512]{0,1:T(8,128)}, u32[]{:S(2)}, u32[]{:S(2)}) collective-permute-start(f32[512,512]{0,1:T(8,128)} %bitcast.33), channel_id=1, source_target_pairs={{8,0},{12,4},{16,8},{20,12},{24,16},{28,20},{9,1},{13,5},{17,9},{2... | collective-permute-start | bytes 3145736 | tf_op jit(solution)/shard_map/ppermute | solution.py:18
  265.6 27.2 %copy-start.10 = (bf16[512,512]{1,0:T(8,128)(2,1)}, bf16[512,512]{1,0:T(8,128)(2,1)S(1)}, u32[]{:S(2)}) copy-start(bf16[512,512]{1,0:T(8,128)(2,1)S(1)} %convolution_convert_fusion.2) | copy-start | bytes 1572868
  265.6 27.2 %collective-permute-start.2 = (bf16[512,512]{1,0:T(8,128)(2,1)S(1)}, bf16[512,512]{1,0:T(8,128)(2,1)}, u32[]{:S(2)}, u32[]{:S(2)}) collective-permute-start(bf16[512,512]{1,0:T(8,128)(2,1)S(1)} %convolution_convert_fusion.2), channel_id=1, source_target_pairs={{0,8},{4,12},{8,16},{12,20},{16,24},{20,28},{1,9},{5,13},{9,17},{1... | collective-permute-start | bytes 1572872 | tf_op jit(solution)/shard_map/ppermute | solution.py:18
  269.6 34.4 %collective-permute-start.3 = (bf16[512,512]{1,0:T(8,128)(2,1)S(1)}, bf16[512,512]{1,0:T(8,128)(2,1)}, u32[]{:S(2)}, u32[]{:S(2)}) collective-permute-start(bf16[512,512]{1,0:T(8,128)(2,1)S(1)} %convolution_convert_fusion.2), channel_id=1, source_target_pairs={{0,4},{4,8},{8,12},{12,16},{16,20},{20,24},{24,28},{1,5},{5,9},{9,... | collective-permute-start | bytes 1572872 | tf_op jit(solution)/shard_map/ppermute | solution.py:18
  286.8 23.2 %copy-start.1 = (bf16[512,1024]{0,1:T(8,128)(2,1)S(1)}, bf16[512,1024]{0,1:T(8,128)(2,1)}, u32[]{:S(2)}) copy-start(bf16[512,1024]{0,1:T(8,128)(2,1)} %copy.83) | copy-start | bytes 3145732
  286.8 223.4 %all-gather.19.cloned.1.call-start = ((), (), s32[]{:S(2)}) async-start(), calls=%async_computation.9 | async-start | bytes 4718592 | tf_op jit(solution)/shard_map/all_gather | solution.py:56
  341.8 39.1 %copy-start.3 = (f32[512,64]{1,0:T(8,128)S(1)}, f32[512,64]{1,0:T(8,128)}, u32[]{:S(2)}) copy-start(f32[512,64]{1,0:T(8,128)} %copy-done.2) | copy-start | bytes 393220
  341.8 32.3 %collective-permute-start.4 = (f32[512,512]{0,1:T(8,128)S(1)}, f32[512,512]{0,1:T(8,128)S(1)}, u32[]{:S(2)}, u32[]{:S(2)}) collective-permute-start(f32[512,512]{0,1:T(8,128)S(1)} %bitcast.152), channel_id=1, source_target_pairs={{4,0},{8,4},{12,8},{16,12},{20,16},{24,20},{28,24},{5,1},{9,5},{13... | collective-permute-start | bytes 3145736 | tf_op jit(solution)/shard_map/ppermute | solution.py:18
  348.7 29.2 %collective-permute-start.5 = (f32[512,512]{0,1:T(8,128)S(1)}, f32[512,512]{0,1:T(8,128)S(1)}, u32[]{:S(2)}, u32[]{:S(2)}) collective-permute-start(f32[512,512]{0,1:T(8,128)S(1)} %bitcast.151), channel_id=1, source_target_pairs={{8,0},{12,4},{16,8},{20,12},{24,16},{28,20},{9,1},{13,5},{17,9},{2... | collective-permute-start | bytes 3145736 | tf_op jit(solution)/shard_map/ppermute | solution.py:18
  379.1 4.1 copy-start.6
  382.5 192.5 %all-gather.23.cloned.1.call-start = ((), (), s32[]{:S(2)}) async-start(), calls=%async_computation.11 | async-start | bytes 9437184 | tf_op jit(solution)/shard_map/all_gather | solution.py:56
  383.2 248.6 %all-gather.17.cloned.1.call-start = ((), (), s32[]{:S(2)}) async-start(), calls=%async_computation.8 | async-start | bytes 9437184 | tf_op jit(solution)/shard_map/all_gather | solution.py:56
  409.1 88.0 %all-to-all-start = ((bf16[512,8,672]{0,2,1:T(8,128)(2,1)}), bf16[512,8,672]{0,2,1:T(8,128)(2,1)}, u32[]{:S(2)}, u32[]{:S(2)}) async-start(bf16[512,8,672]{0,2,1:T(8,128)(2,1)} %bitcast.132), calls=%async_computation.1 | async-start | bytes 11010048 | tf_op jit(solution)/shard_map/all_to_all | solution.py:186
  422.0 13.0 %copy-start.7 = (bf16[512,4,128]{0,2,1:T(8,128)(2,1)S(1)}, bf16[512,4,128]{0,2,1:T(8,128)(2,1)}, u32[]{:S(2)}) copy-start(bf16[512,4,128]{0,2,1:T(8,128)(2,1)} %copy.52) | copy-start | bytes 1572868
  422.0 310.3 %reduce-scatter.2.cloned.1.call-start = ((), (), s32[]{:S(2)}) async-start(), calls=%async_computation.7 | async-start | bytes 6881280 | tf_op jit(solution)/shard_map/reduce_scatter | solution.py:182
  435.0 8.3 %copy-start.4 = (bf16[512,512]{0,1:T(8,128)(2,1)S(1)}, bf16[512,512]{0,1:T(8,128)(2,1)}, u32[]{:S(2)}) copy-start(bf16[512,512]{0,1:T(8,128)(2,1)} %fusion.22) | copy-start | bytes 1572868
  497.1 146.6 %all-to-all-start.1 = ((bf16[512,8,672]{0,2,1:T(8,128)(2,1)}), bf16[512,8,672]{0,2,1:T(8,128)(2,1)}, u32[]{:S(2)}, u32[]{:S(2)}) async-start(bf16[512,8,672]{0,2,1:T(8,128)(2,1)} %bitcast.131), calls=%async_computation.2 | async-start | bytes 11010048 | tf_op jit(solution)/shard_map/all_to_all | solution.py:187
  516.7 8.1 %copy-start.8 = (bf16[4096,512]{1,0:T(8,128)(2,1)S(1)}, bf16[4096,512]{1,0:T(8,128)(2,1)}, u32[]{:S(2)}) copy-start(bf16[4096,512]{1,0:T(8,128)(2,1)} %copy.56) | copy-start | bytes 12582916
Sparse Core Ops, SparseCore 0:
  9.9 43.7 all-gather.8
  55.5 77.8 all-gather.10
  135.3 65.3 all-gather.14
  202.4 42.0 all-gather.12
  286.9 56.2 all-gather.20
  382.6 64.1 all-gather.18
  449.2 125.7 all-gather.22
  577.4 54.3 all-gather.16
  634.7 97.5 reduce-scatter.1

commit v2 on v1

--- a/solution.py
+++ b/solution.py
@@ -2,6 +2,7 @@
 import jax.numpy as jnp
 from jax import lax
 from jax.sharding import PartitionSpec as P
+from jax.experimental.layout import Layout, with_layout_constraint
 
 HEAD_WIDTH = 128
 WINDOW = 1024
@@ -53,13 +54,18 @@
 
 
 def gather_rows(value):
-    return lax.all_gather(value, "ctx", axis=0, tiled=True)
-
-
-def block_sums(left, right, blocks):
-    rows = left.shape[0] // blocks
-    left = left.reshape(blocks, rows, left.shape[1])
-    right = right.reshape(blocks, rows, right.shape[1])
+    value = with_layout_constraint(value, Layout((0, 1)))
+    gathered = lax.all_gather(value, "ctx", axis=0, tiled=False)
+    return with_layout_constraint(gathered, Layout((0, 1, 2)))
+
+
+def columns_of(value, blocks):
+    rows, width = value.shape
+    split = jnp.transpose(value.reshape(rows, blocks, width // blocks), (1, 0, 2))
+    return lax.all_to_all(split, "ctx", 0, 0, tiled=False)
+
+
+def block_sums(left, right):
     parts = jnp.einsum("bnd,bnc->bdc", left, right, preferred_element_type=jnp.float32)
     return jnp.sum(parts.astype(jnp.bfloat16).astype(jnp.float32), axis=0)
 
@@ -183,12 +189,15 @@
         partial_in.astype(jnp.bfloat16), "head", scatter_dimension=1, tiled=True
     )
     n_ctx = lax.axis_size("ctx")
-    hidden_cols = lax.all_to_all(hidden_in, "ctx", 1, 0, tiled=True)
-    out_grad_cols = lax.all_to_all(out_grad, "ctx", 1, 0, tiled=True)
-    grad_query = block_sums(hidden_cols, gather_rows(dquery), n_ctx)
-    grad_key = block_sums(hidden_cols, gather_rows(key_gradient), n_ctx)
-    grad_value = block_sums(hidden_cols, gather_rows(value_gradient), n_ctx)
-    grad_out_w = block_sums(out_grad_cols, gather_rows(attended_flat), n_ctx)
+    hidden_cols = columns_of(hidden_in, n_ctx)
+    out_grad_cols = columns_of(out_grad, n_ctx)
+    grad_query = block_sums(hidden_cols, gather_rows(dquery))
+    key_value_sums = block_sums(
+        hidden_cols, gather_rows(jnp.concatenate([key_gradient, value_gradient], axis=1))
+    )
+    grad_key = key_value_sums[:, :key_value_columns]
+    grad_value = key_value_sums[:, key_value_columns:]
+    grad_out_w = block_sums(out_grad_cols, gather_rows(attended_flat))
     return (in_grad, grad_query, grad_key, grad_value, grad_out_w)
 
 

time: 746 us -> 769 us (1.031)
  waiting for transfers between devices: 411 us -> 453 us
  local copies, waits for them, and re-layouts: 69.9 us -> 57.6 us
    all_to_all x2, waiting for transfers between devices: 32.1 us -> 109 us  [columns_of(): return lax.all_to_all(split, 'ctx', 0, 0, tiled=False)]
    all_gather x4 -> x3, waiting for transfers between devices: 87.9 us -> 34.5 us  [gather_rows(): gathered = lax.all_gather(value, 'ctx', axis=0, tiled=False)]
    all_gather x1, waiting for transfers between devices: 0.02 us -> 37.6 us  [shards(): lax.all_gather(value_weight, 'ctx', axis=0, tiled=True)]
    all_gather x3 -> x0, local copies, waits for them, and re-layouts: 25.2 us -> none  [gather_rows(): return lax.all_gather(value, 'ctx', axis=0, tiled=True)]
    ppermute x8, waiting for transfers between devices: 79.1 us -> 55.6 us  [from_behind(): lax.ppermute(value, axis, [(source, source + steps) for source in range(i...]
    reduce_scatter x1, waiting for transfers between devices: 76.5 us -> 88.2 us  [shards(): lax.psum_scatter(partial_in.astype(jnp.bfloat16), 'head', scatter_dimensi...]
    slice x0 -> x4, local copies, waits for them, and re-layouts: none -> 8.65 us  [the longest x3 6.85 us: shards(): grad_v[lowest:lowest + rows]]
    dot_general x4 -> x3, matrix products: 39 us -> 35 us  [block_sums(): jnp.einsum('bnd,bnc->bdc', left, right, preferred_element_type=jnp.float32)]
  transfers between devices with their start and end apart: 19 -> 18, of which waited for: 15 -> 13; matrix products, arithmetic and copies ran while one was open for 36% -> 23% of each run, Pallas kernels for 0% -> 0%
where the time goes in v2:
time: 769 us; the launch traced here: 761 us
  waiting for transfers between devices  453 us (59%)
  matrix products  162 us (21%)
  local copies, waits for them, and re-layouts  57.6 us (7%)
  starting transfers between devices  44.6 us (6%)
  other arithmetic  29.7 us (4%)
  between operations  15 us (2%)
    all_to_all x2, waiting for transfers between devices, columns_of(): return lax.all_to_all(split, 'ctx', 0, 0, tiled=False)  109 us
    reduce_scatter x1, waiting for transfers between devices, shards(): lax.psum_scatter(partial_in.astype(jnp.bfloat16), 'head', scatter_dimensi...  88.2 us
    ppermute x8, waiting for transfers between devices, from_behind(): lax.ppermute(value, axis, [(source, source + steps) for source in range(i...  55.6 us
    all_gather x1, waiting for transfers between devices, shards(): lax.all_gather(w_out, 'ctx', axis=0, tiled=True)  53.1 us
    all_gather x1, waiting for transfers between devices, shards(): lax.all_gather(key_weight, 'ctx', axis=0, tiled=True)  42.6 us
    all_gather x1, waiting for transfers between devices, shards(): lax.all_gather(value_weight, 'ctx', axis=0, tiled=True)  37.6 us
    dot_general x3, matrix products, block_sums(): jnp.einsum('bnd,bnc->bdc', left, right, preferred_element_type=jnp.float32)  35 us
    dot_general x3, matrix products, dot_rows(): lax.dot_general(left, weight, (((1,), (1,)), ((), ())), preferred_element...  34.8 us
  transfers between devices with their start and end apart: 18, of which 13 were waited for; matrix products, arithmetic and copies ran while one was open for 23% of the time, Pallas kernels for 0%

profile of v2, /device:TPU:3, one launch (start us, length us, event | category | flops | bytes accessed | tf_op | source)
XLA Modules:
  0.0 761.4 jit_solution(4668428196909903298)
XLA Ops:
  11.1 42.6 %all-gather.11.cloned.1.call-done = bf16[5376,512]{1,0:T(8,128)(2,1)} async-done(((bf16[672,512]{1,0:T(8,128)(2,1)}), bf16[5376,512]{1,0:T(8,128)(2,1)}) %all-gather.11.cloned.1.call-update) | async-done | bytes 5505040 | tf_op jit(solution)/shard_map/all_gather | solution.py:112
  53.6 6.7 fusion.30
  61.9 2.9 collective-permute-start
  64.8 2.8 collective-permute-start.1
  67.6 37.6 %all-gather.15.cloned.1.call-done = bf16[5376,512]{1,0:T(8,128)(2,1)} async-done(((bf16[672,512]{1,0:T(8,128)(2,1)}), bf16[5376,512]{1,0:T(8,128)(2,1)}) %all-gather.15.cloned.1.call-update) | async-done | bytes 5505040 | tf_op jit(solution)/shard_map/all_gather | solution.py:113
  105.2 7.2 convolution_convert_fusion.2
  112.4 4.4 collective-permute-start.2
  116.8 2.9 collective-permute-start.3
  123.6 15.8 %collective-permute-done.2 = bf16[512,512]{1,0:T(8,128)(2,1)} collective-permute-done((bf16[512,512]{1,0:T(8,128)(2,1)S(1)}, bf16[512,512]{1,0:T(8,128)(2,1)}, u32[]{:S(2)}, u32[]{:S(2)}) %collective-permute-start.2) | collective-permute-done | bytes 524320 | tf_op jit(solution)/shard_map/ppermute | solution.py:19
  139.3 9.5 %collective-permute-done.3 = bf16[512,512]{1,0:T(8,128)(2,1)} collective-permute-done((bf16[512,512]{1,0:T(8,128)(2,1)S(1)}, bf16[512,512]{1,0:T(8,128)(2,1)}, u32[]{:S(2)}, u32[]{:S(2)}) %collective-permute-start.3) | collective-permute-done | bytes 524320 | tf_op jit(solution)/shard_map/ppermute | solution.py:19
  152.0 4.0 copy.66
  156.0 30.2 %all-gather.13.cloned.1.call-done = bf16[5376,1024]{1,0:T(8,128)(2,1)} async-done(((bf16[672,1024]{1,0:T(8,128)(2,1)}), bf16[5376,1024]{1,0:T(8,128)(2,1)}) %all-gather.13.cloned.1.call-update) | async-done | bytes 11010064 | tf_op jit(solution)/shard_map/all_gather | solution.py:111
  186.2 10.3 %convolution_bitcast_fusion.2 = f32[64,8,8,128]{3,1,2,0:T(8,128)S(1)} fusion(bf16[512,5376]{1,0:T(8,128)(2,1)} %param.6, bf16[5376,1024]{1,0:T(8,128)(2,1)} %all-gather.13.cloned.1.call-done), kind=kOutput, calls=%fused_computation.28 | convolution fusion | flops 5637144576 | bytes 18612224 | tf_op jit(solution)/shard_map/dot_general | solution.py:116
  200.2 53.1 %all-gather.17.cloned.1.call-done = bf16[5376,1024]{1,0:T(8,128)(2,1)} async-done(((bf16[672,1024]{1,0:T(8,128)(2,1)}), bf16[5376,1024]{1,0:T(8,128)(2,1)}) %all-gather.17.cloned.1.call-update) | async-done | bytes 11010064 | tf_op jit(solution)/shard_map/all_gather | solution.py:114
  253.3 11.0 %convolution_convert_fusion = bf16[512,1024]{1,0:T(8,128)(2,1)} fusion(bf16[512,5376]{1,0:T(8,128)(2,1)} %param.7, bf16[5376,1024]{1,0:T(8,128)(2,1)} %all-gather.17.cloned.1.call-done), kind=kOutput, calls=%fused_computation.31 | convolution fusion | flops 5637668864 | bytes 17563648 | tf_op jit(solution)/shard_map/dot_general | solution.py:119
  265.8 3.2 fusion.9
  269.0 14.5 %fusion.29 = (f32[4,2,512]{2,1,0:T(2,128)S(1)}, f32[4,2,512,1536]{2,3,1,0:T(8,128)}) fusion(pred[512,1536]{0,1:T(8,128)(4,1)} %and_and_fusion, bf16[512,4,2,128]{3,0,2,1:T(8,128)(2,1)} %fusion.9, bf16[512,4,128]{2,0,1:T(8,128)(2,1)} %copy-done.4, bf16[512,4,128]{2,0,1:T(8,128)(2,1)} %copy.39, bf16[512,4,128]{2,0,1:T(8,128)(2,1)} %copy.38), kind=kOutput, calls=%fused_computation.68 | convolution fusion | flops 1634207232 | bytes 28590080 | tf_op jit(solution)/shard_map/sub | solution.py:76
  283.5 10.5 %fusion.6 = bf16[4,2,512,1536]{2,3,1,0:T(8,128)(2,1)S(1)} fusion(f32[4,2,512,1536]{2,3,1,0:T(8,128)} %get-tuple-element.30, f32[4,2,512]{2,1,0:T(2,128)S(1)} %get-tuple-element.29), kind=kLoop, calls=%fused_computation.14 | loop fusion | flops 12582912 | bytes 37765120 | tf_op jit(solution)/shard_map/convert_element_type | solution.py:78
  294.0 3.3 multiply_reduce_fusion
  298.9 14.5 %fusion.2 = bf16[4,2,512,1536]{2,3,1,0:T(8,128)(2,1)} fusion(bf16[1536,4,128,1]{0,2,3,1:T(8,128)(2,1)S(1)} %copy-done.3, bf16[512,4,2,128]{0,3,2,1:T(8,128)(2,1)S(1)} %bitcast.125, f32[4,2,512]{2,1,0:T(2,128)S(1)} %bitcast.145, f32[4,2,512,1536]{2,3,1,0:T(8,128)} %get-tuple-element.30, f32[4,2,512]{2,1,0:T(2,128)S(1)} %get-tuple-element.29), kind=kOutput, calls=%fused_computation.3 | convolution fusion | flops 1635778560 | bytes 40402944 | tf_op jit(solution)/shard_map/ngrd,mgd->grnm/dot_general | solution.py:88
  313.3 6.8 fusion.13
  323.7 3.2 copy.88
  330.9 2.3 copy.84
  333.3 8.9 %convolution_bitcast_fusion.1 = f32[1536,4,128]{0,2,1:T(8,128)S(1)} fusion(bf16[512,4,2,128]{3,0,2,1:T(8,128)(2,1)S(1)} %copy-done.6, bf16[4,2,512,1536]{2,3,1,0:T(8,128)(2,1)} %fusion.2), kind=kOutput, calls=%fused_computation.16 | convolution fusion | flops 1610612736 | bytes 16777216 | tf_op jit(solution)/shard_map/grnm,ngrd->mgd/dot_general | solution.py:93
  343.9 2.1 collective-permute-start.4
  346.0 2.5 collective-permute-start.5
  348.6 8.7 %convolution_bitcast_fusion = f32[1536,4,128]{0,2,1:T(8,128)S(1)} fusion(bf16[512,4,2,128]{0,3,2,1:T(8,128)(2,1)S(1)} %bitcast.126, bf16[4,2,512,1536]{2,3,1,0:T(8,128)(2,1)} %copy-done), kind=kOutput, calls=%fused_computation.15 | convolution fusion | flops 1610612736 | bytes 16777216 | tf_op jit(solution)/shard_map/grnm,ngrd->mgd/dot_general | solution.py:96
  359.0 2.6 copy.82
  363.6 2.5 copy.83
  369.4 5.0 collective-permute-done.4
  375.6 2.2 fusion.11
  378.7 2.4 copy.89
  384.5 24.1 %collective-permute-done.6 = f32[512,512]{1,0:T(8,128)} collective-permute-done((f32[512,512]{1,0:T(8,128)}, f32[512,512]{1,0:T(8,128)}, u32[]{:S(2)}, u32[]{:S(2)}) %collective-permute-start.6) | collective-permute-done | bytes 1048608 | tf_op jit(solution)/shard_map/ppermute | solution.py:19
  408.6 2.1 add_convert_fusion.1
  411.9 8.3 %copy.61 = bf16[512,5376]{0,1:T(8,128)(2,1)} copy(bf16[512,5376]{1,0:T(8,128)(2,1)} %param.6) | data formatting | bytes 11010048 | tf_op args[0]
  420.2 16.2 %all-to-all-start = ((bf16[8,512,672]{1,2,0:T(8,128)(2,1)}), bf16[8,512,672]{1,2,0:T(8,128)(2,1)}, u32[]{:S(2)}, u32[]{:S(2)}) async-start(bf16[8,512,672]{1,2,0:T(8,128)(2,1)} %bitcast.122), calls=%async_computation.1 | async-start | bytes 11010048 | tf_op jit(solution)/shard_map/all_to_all | solution.py:65
  436.4 13.0 %fusion.22 = f32[512,5376]{0,1:T(8,128)} fusion(bf16[5376,1024]{1,0:T(8,128)(2,1)} %all-gather.13.cloned.1.call-done, bf16[64,8,8,128]{3,2,1,0:T(8,128)(2,1)S(1)} %bitcast.132), kind=kOutput, calls=%fused_computation.61 | convolution fusion | flops 5637144576 | bytes 23068672 | tf_op jit(solution)/shard_map/dot_general | solution.py:51
  449.4 8.5 %fusion.21 = f32[512,5376]{0,1:T(8,128)} fusion(bf16[5376,512]{1,0:T(8,128)(2,1)} %all-gather.11.cloned.1.call-done, bf16[512,4,64]{2,0,1:T(8,128)(2,1)S(1)} %get-tuple-element.16, bf16[512,4,64]{2,0,1:T(8,128)(2,1)S(1)} %get-tuple-element.15), kind=kOutput, calls=%fused_computation.60 | convolution fusion | flops 2819620864 | bytes 17039360 | tf_op jit(solution)/shard_map/dot_general | solution.py:51
  457.9 13.2 %add_convert_fusion = bf16[512,5376]{0,1:T(8,128)(2,1)} fusion(f32[512,5376]{0,1:T(8,128)} %fusion.22, f32[512,5376]{0,1:T(8,128)} %fusion.21, bf16[512,512]{1,0:T(8,128)(2,1)S(1)} %add_convert_fusion.1, bf16[5376,512]{1,0:T(8,128)(2,1)} %all-gather.15.cloned.1.call-done), kind=kOutput, calls=%fused_computation.13 | convolution fusion | flops 2826829824 | bytes 33554432 | tf_op jit(solution)/shard_map/dot_general | solution.py:51
  471.2 8.3 %copy.63 = bf16[512,5376]{0,1:T(8,128)(2,1)} copy(bf16[512,5376]{1,0:T(8,128)(2,1)} %param.7) | data formatting | bytes 11010048 | tf_op args[1]
  479.5 41.3 %all-to-all-done = bf16[8,512,672]{1,2,0:T(8,128)(2,1)} async-done(((bf16[8,512,672]{1,2,0:T(8,128)(2,1)}), bf16[8,512,672]{1,2,0:T(8,128)(2,1)}, u32[]{:S(2)}, u32[]{:S(2)}) %all-to-all-start) | async-done | bytes 5505056 | tf_op jit(solution)/shard_map/all_to_all | solution.py:65
  520.8 6.5 all-to-all-start.1
  527.4 12.0 %convert_reduce_fusion.2 = f32[1024,672]{0,1:T(8,128)} fusion(bf16[8,512,672]{1,2,0:T(8,128)(2,1)} %all-to-all-done, bf16[8,512,1024]{2,1,0:T(8,128)(2,1)} %bitcast.146), kind=kOutput, calls=%fused_computation.9 | convolution fusion | flops 5652971520 | bytes 16646144 | tf_op jit(solution)/shard_map/bnd,bnc->bdc/dot_general | solution.py:69
  539.4 67.3 %all-to-all-done.1 = bf16[8,512,672]{1,2,0:T(8,128)(2,1)} async-done(((bf16[8,512,672]{1,2,0:T(8,128)(2,1)}), bf16[8,512,672]{1,2,0:T(8,128)(2,1)}, u32[]{:S(2)}, u32[]{:S(2)}) %all-to-all-start.1) | async-done | bytes 5505056 | tf_op jit(solution)/shard_map/all_to_all | solution.py:65
  606.6 12.5 %convert_reduce_fusion = f32[1024,672]{0,1:T(8,128)} fusion(bf16[8,512,672]{1,2,0:T(8,128)(2,1)} %all-to-all-done.1, bf16[8,512,1024]{2,1,0:T(8,128)(2,1)} %bitcast.147), kind=kOutput, calls=%fused_computation.7 | convolution fusion | flops 5652971520 | bytes 16646144 | tf_op jit(solution)/shard_map/bnd,bnc->bdc/dot_general | solution.py:69
  619.2 34.5 %all-gather.21.cloned.1.call-done = bf16[4096,1024]{1,0:T(8,128)(2,1)} async-done(((bf16[512,1024]{1,0:T(8,128)(2,1)}), bf16[4096,1024]{1,0:T(8,128)(2,1)}) %all-gather.21.cloned.1.call-update) | async-done | bytes 8388624 | tf_op jit(solution)/shard_map/all_gather | solution.py:58
  653.7 10.5 %convert_reduce_fusion.1 = f32[1024,672]{0,1:T(8,128)S(1)} fusion(bf16[8,512,672]{1,2,0:T(8,128)(2,1)} %all-to-all-done, bf16[8,512,1024]{2,1,0:T(8,128)(2,1)} %bitcast.148), kind=kOutput, calls=%fused_computation.8 | convolution fusion | flops 5652971520 | bytes 16646144 | tf_op jit(solution)/shard_map/bnd,bnc->bdc/dot_general | solution.py:69
  666.0 88.2 %reduce-scatter.2.cloned.1.call-done = bf16[512,1344]{0,1:T(8,128)(2,1)} async-done(((bf16[512,5376]{0,1:T(8,128)(2,1)}), bf16[512,1344]{0,1:T(8,128)(2,1)}) %reduce-scatter.2.cloned.1.call-update) | async-done | bytes 1376272 | tf_op jit(solution)/shard_map/reduce_scatter | solution.py:188
  (74 shorter events, 43.8 us)
Async XLA Ops:
  7.2 46.5 %all-gather.11.cloned.1.call-start = ((), (), s32[]{:S(2)}) async-start(), calls=%async_computation.3 | async-start | bytes 6193152 | tf_op jit(solution)/shard_map/all_gather | solution.py:112
  7.9 97.3 %all-gather.15.cloned.1.call-start = ((), (), s32[]{:S(2)}) async-start(), calls=%async_computation.5 | async-start | bytes 6193152 | tf_op jit(solution)/shard_map/all_gather | solution.py:113
  8.6 177.5 %all-gather.13.cloned.1.call-start = ((), (), s32[]{:S(2)}) async-start(), calls=%async_computation.4 | async-start | bytes 12386304 | tf_op jit(solution)/shard_map/all_gather | solution.py:111
  9.4 243.9 %all-gather.17.cloned.1.call-start = ((), (), s32[]{:S(2)}) async-start(), calls=%async_computation.6 | async-start | bytes 12386304 | tf_op jit(solution)/shard_map/all_gather | solution.py:114
  10.0 517.4 %all-gather.19.cloned.1.call-start = ((), (), s32[]{:S(2)}) async-start(), calls=%async_computation.8 | async-start | bytes 9437184 | tf_op jit(solution)/shard_map/all_gather | solution.py:58
  11.1 185.9 %copy-start.1 = (f32[512,64]{1,0:T(8,128)}, f32[512,64]{1,0:T(8,128)S(1)}, u32[]{:S(2)}) copy-start(f32[512,64]{1,0:T(8,128)S(1)} %get-tuple-element.28) | copy-start | bytes 393220
  61.7 50.7 %copy-start.4 = (bf16[512,4,128]{2,0,1:T(8,128)(2,1)}, bf16[512,4,128]{2,0,1:T(8,128)(2,1)S(1)}, u32[]{:S(2)}) copy-start(bf16[512,4,128]{2,0,1:T(8,128)(2,1)S(1)} %maximum_convert_fusion) | copy-start | bytes 1572868
  61.9 59.7 %collective-permute-start = (bf16[512,512]{0,1:T(8,128)(2,1)S(1)}, bf16[512,512]{0,1:T(8,128)(2,1)S(1)}, u32[]{:S(2)}, u32[]{:S(2)}) collective-permute-start(bf16[512,512]{0,1:T(8,128)(2,1)S(1)} %bitcast.141), channel_id=1, source_target_pairs={{0,8},{4,12},{8,16},{12,20},{16,24},{20,28},{1,9},{5,13},{9,17},{1... | collective-permute-start | bytes 1572872 | tf_op jit(solution)/shard_map/ppermute | solution.py:19
  64.8 57.8 %collective-permute-start.1 = (bf16[512,512]{0,1:T(8,128)(2,1)S(1)}, bf16[512,512]{0,1:T(8,128)(2,1)S(1)}, u32[]{:S(2)}, u32[]{:S(2)}) collective-permute-start(bf16[512,512]{0,1:T(8,128)(2,1)S(1)} %bitcast.142), channel_id=1, source_target_pairs={{0,4},{4,8},{8,12},{12,16},{16,20},{20,24},{24,28},{1,5},{5,9},{9,... | collective-permute-start | bytes 1572872 | tf_op jit(solution)/shard_map/ppermute | solution.py:19
  112.4 27.0 %collective-permute-start.2 = (bf16[512,512]{1,0:T(8,128)(2,1)S(1)}, bf16[512,512]{1,0:T(8,128)(2,1)}, u32[]{:S(2)}, u32[]{:S(2)}) collective-permute-start(bf16[512,512]{1,0:T(8,128)(2,1)S(1)} %convolution_convert_fusion.2), channel_id=1, source_target_pairs={{0,8},{4,12},{8,16},{12,20},{16,24},{20,28},{1,9},{5,13},{9,17},{1... | collective-permute-start | bytes 1572872 | tf_op jit(solution)/shard_map/ppermute | solution.py:19
  116.8 32.0 %collective-permute-start.3 = (bf16[512,512]{1,0:T(8,128)(2,1)S(1)}, bf16[512,512]{1,0:T(8,128)(2,1)}, u32[]{:S(2)}, u32[]{:S(2)}) collective-permute-start(bf16[512,512]{1,0:T(8,128)(2,1)S(1)} %convolution_convert_fusion.2), channel_id=1, source_target_pairs={{0,4},{4,8},{8,12},{12,16},{16,20},{20,24},{24,28},{1,5},{5,9},{9,... | collective-permute-start | bytes 1572872 | tf_op jit(solution)/shard_map/ppermute | solution.py:19
  283.5 10.5 %copy-start.3 = (bf16[1536,4,128,1]{0,2,3,1:T(8,128)(2,1)S(1)}, bf16[1536,4,128,1]{0,2,3,1:T(8,128)(2,1)}, u32[]{:S(2)}) copy-start(bf16[1536,4,128,1]{0,2,3,1:T(8,128)(2,1)} %copy.66) | copy-start | bytes 4718596
  294.0 4.9 copy-start
  298.9 14.5 %copy-start.5 = (bf16[512,4,128]{2,0,1:T(8,128)(2,1)S(1)}, bf16[512,4,128]{2,0,1:T(8,128)(2,1)}, u32[]{:S(2)}) copy-start(bf16[512,4,128]{2,0,1:T(8,128)(2,1)} %copy-done.4) | copy-start | bytes 1572868
  328.9 4.3 copy-start.6
  330.9 275.8 %all-gather.23.cloned.1.call-start = ((), (), s32[]{:S(2)}) async-start(), calls=%async_computation.10 | async-start | bytes 9437184 | tf_op jit(solution)/shard_map/all_gather | solution.py:58
  333.2 320.5 %all-gather.21.cloned.1.call-start = ((), (), s32[]{:S(2)}) async-start(), calls=%async_computation.9 | async-start | bytes 9437184 | tf_op jit(solution)/shard_map/all_gather | solution.py:58
  343.9 30.5 %collective-permute-start.4 = (f32[512,512]{0,1:T(8,128)}, f32[512,512]{0,1:T(8,128)}, u32[]{:S(2)}, u32[]{:S(2)}) collective-permute-start(f32[512,512]{0,1:T(8,128)} %bitcast.23), channel_id=1, source_target_pairs={{4,0},{8,4},{12,8},{16,12},{20,16},{24,20},{28,24},{5,1},{9,5},{13... | collective-permute-start | bytes 3145736 | tf_op jit(solution)/shard_map/ppermute | solution.py:19
  346.0 29.6 %collective-permute-start.5 = (f32[512,512]{0,1:T(8,128)}, f32[512,512]{0,1:T(8,128)}, u32[]{:S(2)}, u32[]{:S(2)}) collective-permute-start(f32[512,512]{0,1:T(8,128)} %bitcast.24), channel_id=1, source_target_pairs={{8,0},{12,4},{16,8},{20,12},{24,16},{28,20},{9,1},{13,5},{17,9},{2... | collective-permute-start | bytes 3145736 | tf_op jit(solution)/shard_map/ppermute | solution.py:19
  361.6 47.0 %collective-permute-start.6 = (f32[512,512]{1,0:T(8,128)}, f32[512,512]{1,0:T(8,128)}, u32[]{:S(2)}, u32[]{:S(2)}) collective-permute-start(f32[512,512]{1,0:T(8,128)} %copy.82), channel_id=1, source_target_pairs={{4,0},{8,4},{12,8},{16,12},{20,16},{24,20},{28,24},{5,1},{9,5},{13... | collective-permute-start | bytes 3145736 | tf_op jit(solution)/shard_map/ppermute | solution.py:19
  366.1 42.5 %collective-permute-start.7 = (f32[512,512]{1,0:T(8,128)}, f32[512,512]{1,0:T(8,128)}, u32[]{:S(2)}, u32[]{:S(2)}) collective-permute-start(f32[512,512]{1,0:T(8,128)} %copy.83), channel_id=1, source_target_pairs={{8,0},{12,4},{16,8},{20,12},{24,16},{28,20},{9,1},{13,5},{17,9},{2... | collective-permute-start | bytes 3145736 | tf_op jit(solution)/shard_map/ppermute | solution.py:19
  368.0 14.4 %copy-start.2 = (f32[512,64]{1,0:T(8,128)S(1)}, f32[512,64]{1,0:T(8,128)}, u32[]{:S(2)}) copy-start(f32[512,64]{1,0:T(8,128)} %copy-done.1) | copy-start | bytes 393220
  420.2 100.7 %all-to-all-start = ((bf16[8,512,672]{1,2,0:T(8,128)(2,1)}), bf16[8,512,672]{1,2,0:T(8,128)(2,1)}, u32[]{:S(2)}, u32[]{:S(2)}) async-start(bf16[8,512,672]{1,2,0:T(8,128)(2,1)} %bitcast.122), calls=%async_computation.1 | async-start | bytes 11010048 | tf_op jit(solution)/shard_map/all_to_all | solution.py:65
  436.4 317.8 %reduce-scatter.2.cloned.1.call-start = ((), (), s32[]{:S(2)}) async-start(), calls=%async_computation.7 | async-start | bytes 6881280 | tf_op jit(solution)/shard_map/reduce_scatter | solution.py:188
  520.8 85.8 %all-to-all-start.1 = ((bf16[8,512,672]{1,2,0:T(8,128)(2,1)}), bf16[8,512,672]{1,2,0:T(8,128)(2,1)}, u32[]{:S(2)}, u32[]{:S(2)}) async-start(bf16[8,512,672]{1,2,0:T(8,128)(2,1)} %bitcast.123), calls=%async_computation.2 | async-start | bytes 11010048 | tf_op jit(solution)/shard_map/all_to_all | solution.py:65
Sparse Core Ops, SparseCore 0:
  9.9 43.7 all-gather.10
  55.5 49.6 all-gather.14
  107.1 79.0 all-gather.12
  187.9 65.3 all-gather.16
  331.0 148.0 all-gather.18
  480.8 116.1 all-gather.22
  599.5 54.1 all-gather.20
  656.6 97.5 reduce-scatter.1

commit v3 on v0

--- a/solution.py
+++ b/solution.py
@@ -1,7 +1,7 @@
 import jax
 import jax.numpy as jnp
 from jax import lax
-from jax.sharding import PartitionSpec as P
+from jax.sharding import Mesh, PartitionSpec as P
 
 HEAD_WIDTH = 128
 WINDOW = 1024
@@ -10,6 +10,9 @@
 QUERY_SCALE = 168.0 ** (-0.5)
 ROPE_BASE = 10000.0
 NEG_LARGE = -1e30
+
+
+CTX = ("chip", "core")
 
 
 def from_behind(value, axis, steps):
@@ -45,6 +48,30 @@
         axis=-1,
     )
 
+
+def gather_weight(weight):
+    mine = lax.all_gather(weight, "chip", axis=0, tiled=False)
+    other = lax.ppermute(mine, "core", [(0, 1), (1, 0)])
+    return (mine, other)
+
+
+def split_columns(value, core, n_chip, width):
+    blocks = value.reshape(value.shape[0], n_chip, 2, width)
+    mine = lax.dynamic_index_in_dim(blocks, core, axis=2, keepdims=False)
+    other = lax.dynamic_index_in_dim(blocks, 1 - core, axis=2, keepdims=False)
+    return (mine, other)
+
+
+def project(halves, weights):
+    total = None
+    for left, right in zip(halves, weights):
+        part = jnp.einsum("nkd,kdc->nc", left, right, preferred_element_type=jnp.float32)
+        total = part if total is None else total + part
+    return total
+
+
+def back_project(grads, weight):
+    return jnp.einsum("nc,kdc->nkd", grads, weight, preferred_element_type=jnp.float32)
 
 def dot_rows(left, weight):
     return lax.dot_general(
@@ -89,17 +116,20 @@
     local_groups = key_value_columns // head_size
     group_ratio = local_heads // local_groups
     reach = WINDOW // rows
-    first = lax.axis_index("ctx") * rows
-    full_query, full_key, full_value, full_out = (
-        lax.all_gather(w_query, "ctx", axis=0, tiled=True),
-        lax.all_gather(key_weight, "ctx", axis=0, tiled=True),
-        lax.all_gather(value_weight, "ctx", axis=0, tiled=True),
-        lax.all_gather(w_out, "ctx", axis=0, tiled=True),
-    )
-    query = jnp.dot(hidden_in, full_query, preferred_element_type=jnp.float32)
-    key_projected = jnp.dot(hidden_in, full_key, preferred_element_type=jnp.float32)
-    value_projected = jnp.dot(hidden_in, full_value, preferred_element_type=jnp.float32)
-    grad_att_f = jnp.dot(out_grad, full_out, preferred_element_type=jnp.float32)
+    core = lax.axis_index("core")
+    first = (lax.axis_index("chip") * lax.axis_size("core") + core) * rows
+    n_chip = lax.axis_size("chip")
+    weight_rows = w_query.shape[0]
+    full_key = gather_weight(key_weight)
+    full_value = gather_weight(value_weight)
+    full_query = gather_weight(w_query)
+    full_out = gather_weight(w_out)
+    hidden_halves = split_columns(hidden_in, core, n_chip, weight_rows)
+    out_grad_halves = split_columns(out_grad, core, n_chip, weight_rows)
+    key_projected = project(hidden_halves, full_key)
+    value_projected = project(hidden_halves, full_value)
+    query = project(hidden_halves, full_query)
+    grad_att_f = project(out_grad_halves, full_out)
     cosine_table, sine_table = rope_tables(first, rows, head_size)
     query_rows = (
         apply_rotary(query.reshape(rows, local_heads, head_size), cosine_table, sine_table)
@@ -115,7 +145,7 @@
     key_blocks = []
     value_blocks = []
     for distance in range(reach, 0, -1):
-        far_keys, far_values = from_behind((keys_here, values_here), "ctx", distance)
+        far_keys, far_values = from_behind((keys_here, values_here), CTX, distance)
         key_blocks.append(far_keys)
         value_blocks.append(far_values)
     keys_all = jnp.concatenate(key_blocks + [keys_here], axis=0).reshape(
@@ -148,7 +178,7 @@
     for distance in range(1, reach + 1):
         lowest = (reach - distance) * rows
         back_keys, back_values = from_behind(
-            (grad_k[lowest : lowest + rows], grad_v[lowest : lowest + rows]), "ctx", -distance
+            (grad_k[lowest : lowest + rows], grad_v[lowest : lowest + rows]), CTX, -distance
         )
         own_keys = own_keys + back_keys
         own_values = own_values + back_values
@@ -166,14 +196,16 @@
         .reshape(rows, key_value_columns)
     )
     value_gradient = own_values.astype(jnp.bfloat16)
-    partial_in = (
-        dot_rows(dquery, full_query)
-        + dot_rows(key_gradient, full_key)
-        + dot_rows(value_gradient, full_value)
-    )
-    in_grad = lax.psum_scatter(
-        partial_in.astype(jnp.bfloat16), "head", scatter_dimension=1, tiled=True
-    )
+    halves = [
+        back_project(dquery, full_query[side])
+        + back_project(key_gradient, full_key[side])
+        + back_project(value_gradient, full_value[side])
+        for side in range(2)
+    ]
+    partial_in = jnp.where(
+        core == 0, jnp.stack(halves, axis=2), jnp.stack(halves[::-1], axis=2)
+    ).astype(jnp.bfloat16).reshape(rows, -1)
+    in_grad = lax.psum_scatter(partial_in, "head", scatter_dimension=1, tiled=True)
     grad_q_part = jnp.einsum("nd,nc->dc", hidden_in, dquery, preferred_element_type=jnp.float32)
     grad_k_part = jnp.einsum(
         "nd,nc->dc", hidden_in, key_gradient, preferred_element_type=jnp.float32
@@ -183,35 +215,24 @@
     )
     grad_query, grad_key, grad_value, grad_out_w = (
         lax.psum_scatter(
-            grad_q_part.astype(jnp.bfloat16), "ctx", scatter_dimension=0, tiled=True
-        ).astype(jnp.float32),
-        lax.psum_scatter(
-            grad_k_part.astype(jnp.bfloat16), "ctx", scatter_dimension=0, tiled=True
-        ).astype(jnp.float32),
-        lax.psum_scatter(
-            grad_v_part.astype(jnp.bfloat16), "ctx", scatter_dimension=0, tiled=True
-        ).astype(jnp.float32),
-        lax.psum_scatter(
-            grad_w_out.astype(jnp.bfloat16), "ctx", scatter_dimension=0, tiled=True
+            grad_q_part.astype(jnp.bfloat16), CTX, scatter_dimension=0, tiled=True
+        ).astype(jnp.float32),
+        lax.psum_scatter(
+            grad_k_part.astype(jnp.bfloat16), CTX, scatter_dimension=0, tiled=True
+        ).astype(jnp.float32),
+        lax.psum_scatter(
+            grad_v_part.astype(jnp.bfloat16), CTX, scatter_dimension=0, tiled=True
+        ).astype(jnp.float32),
+        lax.psum_scatter(
+            grad_w_out.astype(jnp.bfloat16), CTX, scatter_dimension=0, tiled=True
         ).astype(jnp.float32),
     )
     return (in_grad, grad_query, grad_key, grad_value, grad_out_w)
 
 
 def solution(mesh):
-    in_specs = (
-        P("ctx", None),
-        P("ctx", None),
-        P("ctx", "head"),
-        P("ctx", "head"),
-        P("ctx", "head"),
-        P("ctx", "head"),
-    )
-    out_specs = (
-        P("ctx", "head"),
-        P("ctx", "head"),
-        P("ctx", "head"),
-        P("ctx", "head"),
-        P("ctx", "head"),
-    )
-    return jax.shard_map(shards, mesh=mesh, in_specs=in_specs, out_specs=out_specs, check_vma=False)
+    n_ctx, n_head = mesh.shape["ctx"], mesh.shape["head"]
+    split = Mesh(mesh.devices.reshape(n_ctx // 2, 2, n_head), ("chip", "core", "head"))
+    in_specs = (P(CTX, None), P(CTX, None)) + (P(CTX, "head"),) * 4
+    out_specs = (P(CTX, "head"),) * 5
+    return jax.shard_map(shards, mesh=split, in_specs=in_specs, out_specs=out_specs, check_vma=False)

time: 769 us -> 844 us (1.098)
  local copies, waits for them, and re-layouts: 81.4 us -> 117 us
  waiting for transfers between devices: 449 us -> 479 us
  other arithmetic: 22.7 us -> 31.3 us
    all_gather x4, waiting for transfers between devices: 135 us -> 186 us  [gather_weight(): mine = lax.all_gather(weight, 'chip', axis=0, tiled=False)]
    ppermute x8, waiting for transfers between devices: 97.8 us -> 68.2 us  [from_behind(): lax.ppermute(value, axis, [(source, source + steps) for source in range(i...]
    unnamed x53 -> x67, local copies, waits for them, and re-layouts: 68.1 us -> 87.3 us
    unnamed x13, waiting for transfers between devices: 118 us -> 127 us
    dot_general x7 -> x14, matrix products: 72.9 us -> 67.3 us  [the longest x8 40.9 us: project(): jnp.einsum('nkd,kdc->nc', left, right, preferred_element_type=jnp.float32)]
  transfers between devices with their start and end apart: 17 -> 21, of which waited for: 12 -> 11; matrix products, arithmetic and copies ran while one was open for 36% -> 38% of each run, Pallas kernels for 0% -> 0%
where the time goes in v3:
time: 844 us; the launch traced here: 835 us
  waiting for transfers between devices  479 us (57%)
  matrix products  167 us (20%)
  local copies, waits for them, and re-layouts  117 us (14%)
  other arithmetic  31.3 us (4%)
  starting transfers between devices  25 us (3%)
  between operations  14.9 us (2%)
    all_gather x4, waiting for transfers between devices, gather_weight(): mine = lax.all_gather(weight, 'chip', axis=0, tiled=False)  186 us
    unnamed x13, waiting for transfers between devices  127 us
    reduce_scatter x1, waiting for transfers between devices, shards(): lax.psum_scatter(partial_in, 'head', scatter_dimension=1, tiled=True)  97.5 us
    unnamed x67, local copies, waits for them, and re-layouts  87.3 us
    ppermute x8, waiting for transfers between devices, from_behind(): lax.ppermute(value, axis, [(source, source + steps) for source in range(i...  68.2 us
    dot_general x8, matrix products, project(): jnp.einsum('nkd,kdc->nc', left, right, preferred_element_type=jnp.float32)  40.9 us
    dot_general x6, matrix products, back_project(): jnp.einsum('nc,kdc->nkd', grads, weight, preferred_element_type=jnp.float32)  26.4 us
    ppermute x8, starting transfers between devices, from_behind(): lax.ppermute(value, axis, [(source, source + steps) for source in range(i...  21.4 us
  transfers between devices with their start and end apart: 21, of which 11 were waited for; matrix products, arithmetic and copies ran while one was open for 38% of the time, Pallas kernels for 0%

profile of v3, /device:TPU:3, one launch (start us, length us, event | category | flops | bytes accessed | tf_op | source)
XLA Modules:
  0.0 834.7 jit_solution(14530092148994373780)
XLA Ops:
  10.0 41.5 %all-gather.9.cloned.1.call-done = bf16[2688,512]{1,0:T(8,128)(2,1)} async-done(((bf16[672,512]{1,0:T(8,128)(2,1)}), bf16[2688,512]{1,0:T(8,128)(2,1)}) %all-gather.9.cloned.1.call-update) | async-done | bytes 2752528 | tf_op jit(solution)/shard_map/all_gather | solution.py:53
  52.3 64.5 %all-gather.11.cloned.1.call-done = bf16[2688,1024]{1,0:T(8,128)(2,1)} async-done(((bf16[672,1024]{1,0:T(8,128)(2,1)}), bf16[2688,1024]{1,0:T(8,128)(2,1)}) %all-gather.11.cloned.1.call-update) | async-done | bytes 5505040 | tf_op jit(solution)/shard_map/all_gather | solution.py:53
  117.7 8.4 %copy.74 = bf16[512,5376]{0,1:T(8,128)(2,1)} copy(bf16[512,5376]{1,0:T(8,128)(2,1)} %param.6) | data formatting | bytes 11010048 | tf_op args[0]
  127.2 4.2 fusion.46
  131.5 3.5 fusion.61
  137.4 3.0 collective-permute-start.2
  142.8 8.5 %copy.82 = bf16[512,5376]{0,1:T(8,128)(2,1)} copy(bf16[512,5376]{1,0:T(8,128)(2,1)} %param.7) | data formatting | bytes 11010048 | tf_op args[1]
  153.2 18.3 %all-gather.13.cloned.1.call-done = bf16[2688,512]{1,0:T(8,128)(2,1)} async-done(((bf16[672,512]{1,0:T(8,128)(2,1)}), bf16[2688,512]{1,0:T(8,128)(2,1)}) %all-gather.13.cloned.1.call-update) | async-done | bytes 2752528 | tf_op jit(solution)/shard_map/all_gather | solution.py:53
  176.2 61.5 %all-gather.15.cloned.1.call-done = bf16[2688,1024]{1,0:T(8,128)(2,1)} async-done(((bf16[672,1024]{1,0:T(8,128)(2,1)}), bf16[2688,1024]{1,0:T(8,128)(2,1)}) %all-gather.15.cloned.1.call-update) | async-done | bytes 5505040 | tf_op jit(solution)/shard_map/all_gather | solution.py:53
  238.5 6.4 fusion.26
  245.0 4.5 fusion.16
  249.5 5.2 fusion.41
  258.7 14.9 %fusion.97 = (f32[4,2,512]{2,1,0:T(2,128)S(1)}, f32[4,2,512,1536]{2,3,1,0:T(8,128)}) fusion(pred[512,1536]{0,1:T(8,128)(4,1)} %and_and_fusion, bf16[512,4,2,128]{3,0,2,1:T(8,128)(2,1)} %fusion.38, bf16[512,4,128]{2,0,1:T(8,128)(2,1)} %copy-done.4, bf16[512,4,128]{2,0,1:T(8,128)(2,1)} %copy.79, bf16[512,4,128]{2,0,1:T(8,128)(2,1)} %copy.78), kind=kOutput, calls=%fused_computation.115 | convolution fusion | flops 1634207232 | bytes 28590080 | tf_op jit(solution)/shard_map/sub | solution.py:86
  273.6 14.3 %fusion.7 = bf16[4,2,512,1536]{2,3,1,0:T(8,128)(2,1)} fusion(f32[4,2,512,1536]{2,3,1,0:T(8,128)} %get-tuple-element.43, f32[4,2,512]{2,1,0:T(2,128)S(1)} %get-tuple-element.42), kind=kLoop, calls=%fused_computation.14 | loop fusion | flops 12582912 | bytes 37765120 | tf_op jit(solution)/shard_map/convert_element_type | solution.py:88
  287.9 7.5 fusion.40
  297.7 9.0 %convolution_bitcast_fusion = f32[1536,4,128]{0,2,1:T(8,128)S(1)} fusion(bf16[512,4,2,128]{0,3,2,1:T(8,128)(2,1)} %bitcast.223, bf16[4,2,512,1536]{2,3,1,0:T(8,128)(2,1)} %fusion.7), kind=kOutput, calls=%fused_computation.23 | convolution fusion | flops 1610612736 | bytes 16777216 | tf_op jit(solution)/shard_map/grnm,ngrd->mgd/dot_general | solution.py:106
  318.1 4.3 fusion.49
  322.4 5.3 fusion.64
  327.7 4.3 collective-permute-start.6
  332.0 3.1 collective-permute-start.5
  336.7 4.6 collective-permute-done.11
  341.2 22.8 %collective-permute-done.10 = f32[512,512]{1,0:T(8,128)} collective-permute-done((f32[512,512]{1,0:T(8,128)}, f32[512,512]{1,0:T(8,128)}, u32[]{:S(2)}, u32[]{:S(2)}) %collective-permute-start.10) | collective-permute-done | bytes 1048608 | tf_op jit(solution)/shard_map/ppermute | solution.py:21
  365.8 7.4 fusion.11
  373.2 8.3 copy.134
  384.1 3.6 reshape.217
  387.6 3.9 copy.111
  391.5 9.1 %multiply_reduce_fusion = (f32[512,4,2]{0,2,1:T(2,128)S(1)}, bf16[4,128,2,512]{3,1,2,0:T(8,128)(2,1)}) fusion(bf16[512,1024]{0,1:T(8,128)(2,1)S(1)} %copy-done.3, bf16[1536,4,128,1]{0,2,3,1:T(8,128)(2,1)} %copy.111, bf16[4,2,512,1536]{2,3,1,0:T(8,128)(2,1)} %fusion.7), kind=kOutput, calls=%fused_computation.61 | convolution fusion | flops 1613230080 | bytes 16269312 | tf_op jit(solution)/shard_map/grnm,mgd->ngrd/dot_general | solution.py:89
  400.7 16.4 %fusion.2 = bf16[4,2,512,1536]{2,3,1,0:T(8,128)(2,1)} fusion(bf16[1536,4,128,1]{0,2,3,1:T(8,128)(2,1)} %copy.111, bf16[512,4,2,128]{0,3,2,1:T(8,128)(2,1)S(1)} %bitcast.224, f32[4,2,512]{2,1,0:T(2,128)S(1)} %bitcast.248, f32[4,2,512,1536]{2,3,1,0:T(8,128)} %get-tuple-element.43, f32[4,2,512]{2,1,0:T(2,128)S(1)} %get-tuple-element.42), kind=kOutput, calls=%fused_computation.3 | convolution fusion | flops 1635778560 | bytes 40402944 | tf_op jit(solution)/shard_map/ngrd,mgd->grnm/dot_general | solution.py:98
  417.1 9.3 %convolution_bitcast_fusion.1 = f32[1536,4,128]{0,2,1:T(8,128)S(1)} fusion(bf16[512,4,2,128]{3,0,2,1:T(8,128)(2,1)} %fusion.38, bf16[4,2,512,1536]{2,3,1,0:T(8,128)(2,1)} %fusion.2), kind=kOutput, calls=%fused_computation.24 | convolution fusion | flops 1610612736 | bytes 16777216 | tf_op jit(solution)/shard_map/grnm,ngrd->mgd/dot_general | solution.py:103
  430.8 30.5 %collective-permute-done.9 = f32[512,512]{0,1:T(8,128)S(1)} collective-permute-done((f32[512,512]{0,1:T(8,128)S(1)}, f32[512,512]{0,1:T(8,128)S(1)}, u32[]{:S(2)}, u32[]{:S(2)}) %collective-permute-start.9) | collective-permute-done | bytes 1048608 | tf_op jit(solution)/shard_map/ppermute | solution.py:21
  461.4 10.3 %collective-permute-done.8 = f32[512,512]{0,1:T(8,128)S(1)} collective-permute-done((f32[512,512]{0,1:T(8,128)S(1)}, f32[512,512]{0,1:T(8,128)S(1)}, u32[]{:S(2)}, u32[]{:S(2)}) %collective-permute-start.8) | collective-permute-done | bytes 1048608 | tf_op jit(solution)/shard_map/ppermute | solution.py:21
  477.6 7.5 fusion.10
  485.1 8.2 copy.132
  494.7 6.6 fusion.76
  504.5 3.4 copy.140
  507.9 2.9 multiply_add_fusion
  511.5 8.6 %fusion.8 = bf16[5376,1024]{0,1:T(8,128)(2,1)} fusion(bf16[512,5376]{1,0:T(8,128)(2,1)S(1)} %bitcast.217, bf16[64,8,8,128]{3,2,1,0:T(8,128)(2,1)S(1)} %bitcast.236), kind=kOutput, calls=%fused_computation.15 | convolution fusion | flops 5642649600 | bytes 17563648 | tf_op jit(solution)/shard_map/nd,nc->dc/dot_general | solution.py:209
  520.1 14.7 %copy.130 = bf16[5376,1024]{1,0:T(8,128)(2,1)} copy(bf16[5376,1024]{0,1:T(8,128)(2,1)} %fusion.8) | data formatting | bytes 22020096
  536.0 11.0 %fusion.9 = bf16[5376,1024]{0,1:T(8,128)(2,1)} fusion(bf16[512,1024]{0,1:T(8,128)(2,1)S(1)} %bitcast.244, bf16[512,5376]{1,0:T(8,128)(2,1)} %param.7), kind=kOutput, calls=%fused_computation.16 | convolution fusion | flops 5642649600 | bytes 17563648 | tf_op jit(solution)/shard_map/nd,nc->dc/dot_general | solution.py:168
  547.0 14.7 %copy.136 = bf16[5376,1024]{1,0:T(8,128)(2,1)} copy(bf16[5376,1024]{0,1:T(8,128)(2,1)} %fusion.9) | data formatting | bytes 22020096
  562.5 8.9 %fusion.98 = f32[512,4,672]{0,2,1:T(8,128)} fusion(bf16[512,1024,1]{1,0,2:T(8,128)(2,1)S(1)} %reshape.239, bf16[4,672,1024]{2,1,0:T(8,128)(2,1)} %bitcast.251), kind=kOutput, calls=%fused_computation.116 | convolution fusion | flops 2818572288 | bytes 12058624 | tf_op jit(solution)/shard_map/nc,kdc->nkd/dot_general | solution.py:74
  571.4 5.4 fusion.100
  578.4 3.6 fusion.101
  582.0 5.1 add_bitcast_fusion.1
  589.9 2.8 copy.104
  598.3 40.3 %reduce-scatter.16.cloned.1.call-done = bf16[672,1024]{1,0:T(8,128)(2,1)} async-done(((bf16[5376,1024]{1,0:T(8,128)(2,1)}), bf16[672,1024]{1,0:T(8,128)(2,1)}) %reduce-scatter.16.cloned.1.call-update) | async-done | bytes 1376272
  642.2 84.4 %reduce-scatter.22.cloned.1.call-done = bf16[672,1024]{1,0:T(8,128)(2,1)} async-done(((bf16[5376,1024]{1,0:T(8,128)(2,1)}), bf16[672,1024]{1,0:T(8,128)(2,1)}) %reduce-scatter.22.cloned.1.call-update) | async-done | bytes 1376272
  730.2 97.5 %reduce-scatter.14.cloned.1.call-done = bf16[512,1344]{0,1:T(8,128)(2,1)} async-done(((bf16[512,5376]{0,1:T(8,128)(2,1)}), bf16[512,1344]{0,1:T(8,128)(2,1)}) %reduce-scatter.14.cloned.1.call-update) | async-done | bytes 1376272 | tf_op jit(solution)/shard_map/reduce_scatter | solution.py:208
  (137 shorter events, 75.6 us)
Async XLA Ops:
  7.2 44.3 %all-gather.9.cloned.1.call-start = ((), (), s32[]{:S(2)}) async-start(), calls=%async_computation.6 | async-start | bytes 3440640 | tf_op jit(solution)/shard_map/all_gather | solution.py:53
  7.9 109.0 %all-gather.11.cloned.1.call-start = ((), (), s32[]{:S(2)}) async-start(), calls=%async_computation.7 | async-start | bytes 6881280 | tf_op jit(solution)/shard_map/all_gather | solution.py:53
  8.6 162.8 %all-gather.13.cloned.1.call-start = ((), (), s32[]{:S(2)}) async-start(), calls=%async_computation.8 | async-start | bytes 3440640 | tf_op jit(solution)/shard_map/all_gather | solution.py:53
  9.4 228.3 %all-gather.15.cloned.1.call-start = ((), (), s32[]{:S(2)}) async-start(), calls=%async_computation.9 | async-start | bytes 6881280 | tf_op jit(solution)/shard_map/all_gather | solution.py:53
  10.0 582.8 %reduce-scatter.20.cloned.1.call-start = ((), (), s32[]{:S(2)}) async-start(), calls=%async_computation.12 | async-start | bytes 6193152
  51.5 79.9 %collective-permute-start = (bf16[4,672,512]{2,1,0:T(8,128)(2,1)}, bf16[4,672,512]{2,1,0:T(8,128)(2,1)}, u32[]{:S(2)}, u32[]{:S(2)}) collective-permute-start(bf16[4,672,512]{2,1,0:T(8,128)(2,1)} %bitcast.241), channel_id=1, source_target_pairs={{0,4},{4,0},{1,5},{5,1},{2,6},{6,2},{3,7},{7,3},{8,12},{12,8},{9,1... | collective-permute-start | bytes 8257544 | tf_op jit(solution)/shard_map/ppermute | solution.py:54
  116.8 132.6 %collective-permute-start.3 = (bf16[4,672,1024]{2,1,0:T(8,128)(2,1)}, bf16[4,672,1024]{2,1,0:T(8,128)(2,1)}, u32[]{:S(2)}, u32[]{:S(2)}) collective-permute-start(bf16[4,672,1024]{2,1,0:T(8,128)(2,1)} %bitcast.249), channel_id=1, source_target_pairs={{0,4},{4,0},{1,5},{5,1},{2,6},{6,2},{3,7},{7,3},{8,12},{12,8},{9,1... | collective-permute-start | bytes 16515080 | tf_op jit(solution)/shard_map/ppermute | solution.py:54
  117.7 9.5 %copy-start.8 = (bf16[2688,512]{1,0:T(8,128)(2,1)S(1)}, bf16[2688,512]{1,0:T(8,128)(2,1)}, u32[]{:S(2)}) copy-start(bf16[2688,512]{1,0:T(8,128)(2,1)} %all-gather.9.cloned.1.call-done) | copy-start | bytes 8257540
  126.2 5.2 slice-start
  127.2 4.2 slice-start.1
  136.3 15.0 %copy-start.4 = (bf16[512,4,128]{2,0,1:T(8,128)(2,1)}, bf16[512,4,128]{2,0,1:T(8,128)(2,1)S(1)}, u32[]{:S(2)}) copy-start(bf16[512,4,128]{2,0,1:T(8,128)(2,1)S(1)} %maximum_convert_fusion) | copy-start | bytes 1572868
  137.4 34.7 %collective-permute-start.2 = (bf16[512,512]{0,1:T(8,128)(2,1)}, bf16[512,512]{0,1:T(8,128)(2,1)}, u32[]{:S(2)}, u32[]{:S(2)}) collective-permute-start(bf16[512,512]{0,1:T(8,128)(2,1)} %bitcast.7), channel_id=1, source_target_pairs={{0,4},{4,8},{8,12},{12,16},{16,20},{20,24},{24,28},{1,5},{5,9},{9,... | collective-permute-start | bytes 1572872 | tf_op jit(solution)/shard_map/ppermute | solution.py:21
  140.4 33.7 %collective-permute-start.1 = (bf16[512,512]{0,1:T(8,128)(2,1)}, bf16[512,512]{0,1:T(8,128)(2,1)}, u32[]{:S(2)}, u32[]{:S(2)}) collective-permute-start(bf16[512,512]{0,1:T(8,128)(2,1)} %bitcast.7), channel_id=1, source_target_pairs={{0,8},{4,12},{8,16},{12,20},{16,24},{20,28},{1,9},{5,13},{9,17},{1... | collective-permute-start | bytes 1572872 | tf_op jit(solution)/shard_map/ppermute | solution.py:21
  171.5 150.9 %collective-permute-start.4 = (bf16[4,672,512]{2,1,0:T(8,128)(2,1)}, bf16[4,672,512]{2,1,0:T(8,128)(2,1)S(1)}, u32[]{:S(2)}, u32[]{:S(2)}) collective-permute-start(bf16[4,672,512]{2,1,0:T(8,128)(2,1)} %bitcast.220), channel_id=1, source_target_pairs={{0,4},{4,0},{1,5},{5,1},{2,6},{6,2},{3,7},{7,3},{8,12},{12,8},{9,1... | collective-permute-start | bytes 8257544 | tf_op jit(solution)/shard_map/ppermute | solution.py:54
  237.6 7.3 slice-start.6
  237.6 7.3 slice-start.7
  237.6 7.3 copy-start.13
  237.6 50.3 %collective-permute-start.7 = (bf16[4,672,1024]{2,1,0:T(8,128)(2,1)}, bf16[4,672,1024]{2,1,0:T(8,128)(2,1)}, u32[]{:S(2)}, u32[]{:S(2)}) collective-permute-start(bf16[4,672,1024]{2,1,0:T(8,128)(2,1)} %bitcast.252), channel_id=1, source_target_pairs={{0,4},{4,0},{1,5},{5,1},{2,6},{6,2},{3,7},{7,3},{8,12},{12,8},{9,1... | collective-permute-start | bytes 16515080 | tf_op jit(solution)/shard_map/ppermute | solution.py:54
  238.5 11.0 %slice-start.2 = ((s8[5505024]{0:T(1024)(128)(4,1)}), s8[4194304]{0:T(1024)(128)(4,1)S(1)}, s32[]{:S(2)}) async-start(s8[5505024]{0:T(1024)(128)(4,1)} %bitcast.213), calls=%async_computation.16 | async-start | bytes 8388608
  244.9 4.5 slice-start.3
  273.6 14.3 %copy-start.14 = (f32[512,1024,1]{1,0,2:T(8,128)S(1)}, f32[512,1024,1]{1,0,2:T(8,128)}, u32[]{:S(2)}) copy-start(f32[512,1024,1]{1,0,2:T(8,128)} %fusion.16) | copy-start | bytes 6291460
  313.6 27.7 %collective-permute-start.11 = (f32[512,512]{1,0:T(8,128)}, f32[512,512]{1,0:T(8,128)}, u32[]{:S(2)}, u32[]{:S(2)}) collective-permute-start(f32[512,512]{1,0:T(8,128)} %copy.102), channel_id=1, source_target_pairs={{8,0},{12,4},{16,8},{20,12},{24,16},{28,20},{9,1},{13,5},{17,9},{2... | collective-permute-start | bytes 3145736 | tf_op jit(solution)/shard_map/ppermute | solution.py:21
  315.8 48.3 %collective-permute-start.10 = (f32[512,512]{1,0:T(8,128)}, f32[512,512]{1,0:T(8,128)}, u32[]{:S(2)}, u32[]{:S(2)}) collective-permute-start(f32[512,512]{1,0:T(8,128)} %copy.100), channel_id=1, source_target_pairs={{4,0},{8,4},{12,8},{16,12},{20,16},{24,20},{28,24},{5,1},{9,5},{13... | collective-permute-start | bytes 3145736 | tf_op jit(solution)/shard_map/ppermute | solution.py:21
  322.4 5.3 copy-start
  327.7 53.9 %collective-permute-start.6 = (bf16[512,512]{1,0:T(8,128)(2,1)}, bf16[512,512]{1,0:T(8,128)(2,1)}, u32[]{:S(2)}, u32[]{:S(2)}) collective-permute-start(bf16[512,512]{1,0:T(8,128)(2,1)} %fusion.64), channel_id=1, source_target_pairs={{0,4},{4,8},{8,12},{12,16},{16,20},{20,24},{24,28},{1,5},{5,9},{9,... | collective-permute-start | bytes 1572872 | tf_op jit(solution)/shard_map/ppermute | solution.py:21
  332.0 49.6 %collective-permute-start.5 = (bf16[512,512]{1,0:T(8,128)(2,1)}, bf16[512,512]{1,0:T(8,128)(2,1)S(1)}, u32[]{:S(2)}, u32[]{:S(2)}) collective-permute-start(bf16[512,512]{1,0:T(8,128)(2,1)} %fusion.64), channel_id=1, source_target_pairs={{0,8},{4,12},{8,16},{12,20},{16,24},{20,28},{1,9},{5,13},{9,17},{1... | collective-permute-start | bytes 1572872 | tf_op jit(solution)/shard_map/ppermute | solution.py:21
  381.6 214.0 %reduce-scatter.18.cloned.1.call-start = ((), (), s32[]{:S(2)}) async-start(), calls=%async_computation.11 | async-start | bytes 6193152
  384.1 7.5 copy-start.3
  426.8 34.6 %collective-permute-start.9 = (f32[512,512]{0,1:T(8,128)S(1)}, f32[512,512]{0,1:T(8,128)S(1)}, u32[]{:S(2)}, u32[]{:S(2)}) collective-permute-start(f32[512,512]{0,1:T(8,128)S(1)} %bitcast.247), channel_id=1, source_target_pairs={{8,0},{12,4},{16,8},{20,12},{24,16},{28,20},{9,1},{13,5},{17,9},{2... | collective-permute-start | bytes 3145736 | tf_op jit(solution)/shard_map/ppermute | solution.py:21
  428.7 43.0 %collective-permute-start.8 = (f32[512,512]{0,1:T(8,128)S(1)}, f32[512,512]{0,1:T(8,128)S(1)}, u32[]{:S(2)}, u32[]{:S(2)}) collective-permute-start(f32[512,512]{0,1:T(8,128)S(1)} %bitcast.246), channel_id=1, source_target_pairs={{4,0},{8,4},{12,8},{16,12},{20,16},{24,20},{28,24},{5,1},{9,5},{13... | collective-permute-start | bytes 3145736 | tf_op jit(solution)/shard_map/ppermute | solution.py:21
  477.6 7.5 copy-start.6
  493.3 1.0 copy-start.5
  493.3 1.2 copy-start.10
  493.3 1.4 copy-start.11
  493.4 145.3 %reduce-scatter.16.cloned.1.call-start = ((), (), s32[]{:S(2)}) async-start(), calls=%async_computation.10 | async-start | bytes 12386304
  504.5 7.0 slice-start.4
  507.9 3.6 slice-start.5
  534.7 1.2 copy-start.12
  534.8 191.9 %reduce-scatter.22.cloned.1.call-start = ((), (), s32[]{:S(2)}) async-start(), calls=%async_computation.13 | async-start | bytes 12386304
  561.7 266.0 %reduce-scatter.14.cloned.1.call-start = ((), (), s32[]{:S(2)}) async-start(), calls=%async_computation.5 | async-start | bytes 6881280 | tf_op jit(solution)/shard_map/reduce_scatter | solution.py:208
  571.4 5.4 copy-start.7
  571.4 5.4 copy-start.9
  578.4 3.6 copy-start.2
  582.0 5.2 copy-start.1
Sparse Core Ops, SparseCore 0:
  9.8 41.6 all-gather.8
  53.3 63.4 all-gather.10
  118.7 52.7 all-gather.12
  173.2 64.4 all-gather.14
  381.7 65.7 reduce-scatter.19
  493.5 57.0 reduce-scatter.17
  554.2 84.3 reduce-scatter.15
  642.2 84.3 reduce-scatter.21
  729.5 98.1 reduce-scatter.13

commit v4 on v1

--- a/solution.py
+++ b/solution.py
@@ -51,17 +51,6 @@
         left, weight, (((1,), (1,)), ((), ())), preferred_element_type=jnp.float32
     )
 
-
-def gather_rows(value):
-    return lax.all_gather(value, "ctx", axis=0, tiled=True)
-
-
-def block_sums(left, right, blocks):
-    rows = left.shape[0] // blocks
-    left = left.reshape(blocks, rows, left.shape[1])
-    right = right.reshape(blocks, rows, right.shape[1])
-    parts = jnp.einsum("bnd,bnc->bdc", left, right, preferred_element_type=jnp.float32)
-    return jnp.sum(parts.astype(jnp.bfloat16).astype(jnp.float32), axis=0)
 
 def attend_forward(query_rows, key_rows, value_rows, allowed):
     score = jnp.einsum("ngrd,mgd->grnm", query_rows, key_rows, preferred_element_type=jnp.float32)
@@ -101,15 +90,14 @@
     group_ratio = local_heads // local_groups
     reach = WINDOW // rows
     first = lax.axis_index("ctx") * rows
-    full_query, full_key, full_value, full_out = (
-        lax.all_gather(w_query, "ctx", axis=0, tiled=True),
-        lax.all_gather(key_weight, "ctx", axis=0, tiled=True),
-        lax.all_gather(value_weight, "ctx", axis=0, tiled=True),
-        lax.all_gather(w_out, "ctx", axis=0, tiled=True),
-    )
-    query = jnp.dot(hidden_in, full_query, preferred_element_type=jnp.float32)
-    key_projected = jnp.dot(hidden_in, full_key, preferred_element_type=jnp.float32)
-    value_projected = jnp.dot(hidden_in, full_value, preferred_element_type=jnp.float32)
+    full_qkv = lax.all_gather(
+        jnp.concatenate([w_query, key_weight, value_weight], axis=1), "ctx", axis=0, tiled=True
+    )
+    full_out = lax.all_gather(w_out, "ctx", axis=0, tiled=True)
+    projected = jnp.dot(hidden_in, full_qkv, preferred_element_type=jnp.float32)
+    query = projected[:, :query_cols]
+    key_projected = projected[:, query_cols : query_cols + key_value_columns]
+    value_projected = projected[:, query_cols + key_value_columns :]
     grad_att_f = jnp.dot(out_grad, full_out, preferred_element_type=jnp.float32)
     cosine_table, sine_table = rope_tables(first, rows, head_size)
     query_rows = (
@@ -146,6 +134,9 @@
     grouped_grads = attention_gradient.reshape(rows, local_groups, group_ratio, head_size)
     prob, prob_b, attended = attend_forward(grouped_queries, keys_all, values_all, allowed)
     attended_flat = attended.reshape(rows, query_cols)
+    grad_w_out = jnp.einsum(
+        "nd,nc->dc", out_grad, attended_flat, preferred_element_type=jnp.float32
+    )
     grad_q, grad_k, grad_v = attend_backward(
         prob, prob_b, attended, grouped_grads, grouped_queries, keys_all, values_all
     )
@@ -174,21 +165,21 @@
         .reshape(rows, key_value_columns)
     )
     value_gradient = own_values.astype(jnp.bfloat16)
-    partial_in = (
-        dot_rows(dquery, full_query)
-        + dot_rows(key_gradient, full_key)
-        + dot_rows(value_gradient, full_value)
-    )
+    grads_qkv = jnp.concatenate([dquery, key_gradient, value_gradient], axis=1)
+    partial_in = dot_rows(grads_qkv, full_qkv)
     in_grad = lax.psum_scatter(
         partial_in.astype(jnp.bfloat16), "head", scatter_dimension=1, tiled=True
     )
-    n_ctx = lax.axis_size("ctx")
-    hidden_cols = lax.all_to_all(hidden_in, "ctx", 1, 0, tiled=True)
-    out_grad_cols = lax.all_to_all(out_grad, "ctx", 1, 0, tiled=True)
-    grad_query = block_sums(hidden_cols, gather_rows(dquery), n_ctx)
-    grad_key = block_sums(hidden_cols, gather_rows(key_gradient), n_ctx)
-    grad_value = block_sums(hidden_cols, gather_rows(value_gradient), n_ctx)
-    grad_out_w = block_sums(out_grad_cols, gather_rows(attended_flat), n_ctx)
+    grad_qkv_part = jnp.einsum("nd,nc->dc", hidden_in, grads_qkv, preferred_element_type=jnp.float32)
+    grad_out_w = lax.psum_scatter(
+        grad_w_out.astype(jnp.bfloat16), "ctx", scatter_dimension=0, tiled=True
+    ).astype(jnp.float32)
+    grad_qkv = lax.psum_scatter(
+        grad_qkv_part.astype(jnp.bfloat16), "ctx", scatter_dimension=0, tiled=True
+    ).astype(jnp.float32)
+    grad_query = grad_qkv[:, :query_cols]
+    grad_key = grad_qkv[:, query_cols : query_cols + key_value_columns]
+    grad_value = grad_qkv[:, query_cols + key_value_columns :]
     return (in_grad, grad_query, grad_key, grad_value, grad_out_w)
 
 

time: 746 us -> 723 us (0.969)
  matrix products: 169 us -> 129 us
  starting transfers between devices: 48.4 us -> 23.6 us
  local copies, waits for them, and re-layouts: 69.9 us -> 87 us
  waiting for transfers between devices: 411 us -> 428 us
    unnamed x9 -> x7, waiting for transfers between devices: 3.34 us -> 119 us
    all_gather x8 -> x2, waiting for transfers between devices: 220 us -> 158 us  [the longest x1 110 us: shards(): lax.all_gather(jnp.concatenate([w_query, key_weight, value_weight], axis=...]
    unnamed x32 -> x54, local copies, waits for them, and re-layouts: 26.1 us -> 64.8 us
    all_to_all x2 -> x0, waiting for transfers between devices: 32.1 us -> none  [the longest x1 32.1 us: shards(): hidden_cols = lax.all_to_all(hidden_in, 'ctx', 1, 0, tiled=True)]
    all_gather x3 -> x0, local copies, waits for them, and re-layouts: 25.2 us -> none  [gather_rows(): return lax.all_gather(value, 'ctx', axis=0, tiled=True)]
    all_to_all x2 -> x0, starting transfers between devices: 19.3 us -> none  [the longest x1 12.8 us: shards(): hidden_cols = lax.all_to_all(hidden_in, 'ctx', 1, 0, tiled=True)]
    dot_general x7 -> x3, matrix products: 63.1 us -> 45.1 us  [the longest x1 19.9 us: shards(): jnp.einsum('nd,nc->dc', hidden_in, grads_qkv, preferred_element_type=jnp....]
    dot_general x3 -> x1, matrix products: 34.4 us -> 17.6 us  [dot_rows(): lax.dot_general(left, weight, (((1,), (1,)), ((), ())), preferred_element...]
  transfers between devices with their start and end apart: 19 -> 13, of which waited for: 15 -> 7; matrix products, arithmetic and copies ran while one was open for 36% -> 30% of each run, Pallas kernels for 0% -> 0%
where the time goes in v4:
time: 723 us; the launch traced here: 714 us
  waiting for transfers between devices  428 us (59%)
  matrix products  129 us (18%)
  local copies, waits for them, and re-layouts  87 us (12%)
  other arithmetic  31.3 us (4%)
  starting transfers between devices  23.6 us (3%)
  between operations  14.7 us (2%)
    unnamed x7, waiting for transfers between devices  119 us
    all_gather x1, waiting for transfers between devices, shards(): lax.all_gather(jnp.concatenate([w_query, key_weight, value_weight], axis=...  110 us
    reduce_scatter x1, waiting for transfers between devices, shards(): lax.psum_scatter(partial_in.astype(jnp.bfloat16), 'head', scatter_dimensi...  85.7 us
    ppermute x8, waiting for transfers between devices, from_behind(): lax.ppermute(value, axis, [(source, source + steps) for source in range(i...  64.8 us
    unnamed x54, local copies, waits for them, and re-layouts  64.8 us
    all_gather x1, waiting for transfers between devices, shards(): full_out = lax.all_gather(w_out, 'ctx', axis=0, tiled=True)  47.8 us
    ppermute x8, starting transfers between devices, from_behind(): lax.ppermute(value, axis, [(source, source + steps) for source in range(i...  23 us
    dot_general x1, matrix products, shards(): jnp.einsum('nd,nc->dc', hidden_in, grads_qkv, preferred_element_type=jnp....  19.9 us
  transfers between devices with their start and end apart: 13, of which 7 were waited for; matrix products, arithmetic and copies ran while one was open for 30% of the time, Pallas kernels for 0%

profile of v4, /device:TPU:3, one launch (start us, length us, event | category | flops | bytes accessed | tf_op | source)
XLA Modules:
  0.0 713.7 jit_solution(1817643526602952139)
XLA Ops:
  7.2 3.6 pad_maximum_fusion
  12.6 1.9 and_and_fusion
  14.4 110.1 %all-gather.3.cloned.1.call-done = bf16[5376,2048]{1,0:T(8,128)(2,1)} async-done(((bf16[672,2048]{1,0:T(8,128)(2,1)}), bf16[5376,2048]{1,0:T(8,128)(2,1)}) %all-gather.3.cloned.1.call-update) | async-done | bytes 22020112 | tf_op jit(solution)/shard_map/all_gather | solution.py:93
  124.6 16.7 %convolution_bitcast_fusion.2 = f32[512,2048]{0,1:T(8,128)S(1)} fusion(bf16[5376,2048]{1,0:T(8,128)(2,1)} %all-gather.3.cloned.1.call-done, bf16[512,5376]{1,0:T(8,128)(2,1)} %param.6), kind=kOutput, calls=%fused_computation.18 | convolution fusion | flops 11274289152 | bytes 31719424 | tf_op jit(solution)/shard_map/dot_general | solution.py:97
  141.3 2.0 copy-done.2
  145.8 2.2 collective-permute-start.1
  148.1 3.2 collective-permute-start
  151.3 47.8 %all-gather.5.cloned.1.call-done = bf16[5376,1024]{1,0:T(8,128)(2,1)} async-done(((bf16[672,1024]{1,0:T(8,128)(2,1)}), bf16[5376,1024]{1,0:T(8,128)(2,1)}) %all-gather.5.cloned.1.call-update) | async-done | bytes 11010064 | tf_op jit(solution)/shard_map/all_gather | solution.py:96
  199.0 10.2 %convolution_convert_fusion.3 = bf16[512,1024]{1,0:T(8,128)(2,1)S(1)} fusion(bf16[512,5376]{1,0:T(8,128)(2,1)} %param.7, bf16[5376,1024]{1,0:T(8,128)(2,1)} %all-gather.5.cloned.1.call-done), kind=kOutput, calls=%fused_computation.30 | convolution fusion | flops 5637668864 | bytes 17563648 | tf_op jit(solution)/shard_map/dot_general | solution.py:101
  209.8 2.5 slice.134
  212.4 4.8 collective-permute-start.3
  217.2 2.4 collective-permute-start.2
  221.3 1.8 copy.90
  223.1 3.2 copy.91
  226.3 3.2 fusion.11
  232.3 14.5 %fusion.32 = (f32[4,2,512]{2,1,0:T(2,128)S(1)}, f32[4,2,512,1536]{2,3,1,0:T(8,128)}) fusion(pred[512,1536]{0,1:T(8,128)(4,1)} %and_and_fusion, bf16[512,4,2,128]{3,0,2,1:T(8,128)(2,1)} %fusion.11, bf16[512,4,128]{2,0,1:T(8,128)(2,1)} %copy-done.4, bf16[512,4,128]{2,0,1:T(8,128)(2,1)S(1)} %copy.89, bf16[512,4,128]{2,0,1:T(8,128)(2,1)S(1)} %copy.88), kind=kOutput, calls=%fused_computation.69 | convolution fusion | flops 1634207232 | bytes 28590080 | tf_op jit(solution)/shard_map/sub | solution.py:59
  246.8 10.2 %fusion.7 = bf16[4,2,512,1536]{2,3,1,0:T(8,128)(2,1)S(1)} fusion(f32[4,2,512,1536]{2,3,1,0:T(8,128)} %get-tuple-element.48, f32[4,2,512]{2,1,0:T(2,128)S(1)} %get-tuple-element.47), kind=kLoop, calls=%fused_computation.13 | loop fusion | flops 12582912 | bytes 37765120 | tf_op jit(solution)/shard_map/convert_element_type | solution.py:61
  257.1 2.8 pad_maximum_fusion.2
  259.9 1.8 multiply_reduce_fusion
  264.7 8.4 %fusion.8 = bf16[5376,1024]{0,1:T(8,128)(2,1)} fusion(bf16[512,1024]{0,1:T(8,128)(2,1)S(1)} %bitcast.120, bf16[512,5376]{1,0:T(8,128)(2,1)S(1)} %bitcast.125), kind=kOutput, calls=%fused_computation.14 | convolution fusion | flops 5642649600 | bytes 17563648 | tf_op jit(solution)/shard_map/nd,nc->dc/dot_general | solution.py:137
  273.1 14.7 %copy.126 = bf16[5376,1024]{1,0:T(8,128)(2,1)} copy(bf16[5376,1024]{0,1:T(8,128)(2,1)} %fusion.8) | data formatting | bytes 22020096
  288.1 17.0 %fusion.2 = bf16[4,2,512,1536]{2,3,1,0:T(8,128)(2,1)} fusion(bf16[1536,4,128,1]{0,2,3,1:T(8,128)(2,1)S(1)} %bitcast.115, bf16[512,4,2,128]{0,3,2,1:T(8,128)(2,1)S(1)} %bitcast.108, f32[4,2,512]{2,1,0:T(2,128)S(1)} %bitcast.123, f32[4,2,512,1536]{2,3,1,0:T(8,128)} %get-tuple-element.48, f32[4,2,512]{2,1,0:T(2,128)S(1)} %get-tuple-element.47), kind=kOutput, calls=%fused_computation.3 | convolution fusion | flops 1635778560 | bytes 40402944 | tf_op jit(solution)/shard_map/ngrd,mgd->grnm/dot_general | solution.py:71
  305.1 9.9 %convolution_bitcast_fusion.1 = f32[1536,4,128]{0,2,1:T(8,128)S(1)} fusion(bf16[512,4,2,128]{3,0,2,1:T(8,128)(2,1)} %fusion.11, bf16[4,2,512,1536]{2,3,1,0:T(8,128)(2,1)} %fusion.2), kind=kOutput, calls=%fused_computation.17 | convolution fusion | flops 1610612736 | bytes 16777216 | tf_op jit(solution)/shard_map/grnm,ngrd->mgd/dot_general | solution.py:76
  315.0 1.7 fusion.28
  316.7 3.9 collective-permute-start.5
  320.6 2.3 collective-permute-start.4
  322.9 11.1 %convolution_bitcast_fusion = f32[1536,4,128]{0,2,1:T(8,128)} fusion(bf16[512,4,2,128]{0,3,2,1:T(8,128)(2,1)} %bitcast.109, bf16[4,2,512,1536]{2,3,1,0:T(8,128)(2,1)} %copy-done), kind=kOutput, calls=%fused_computation.16 | convolution fusion | flops 1610612736 | bytes 16777216 | tf_op jit(solution)/shard_map/grnm,ngrd->mgd/dot_general | solution.py:79
  334.1 3.7 fusion.29
  337.8 1.9 collective-permute-start.7
  339.7 2.3 collective-permute-start.6
  342.1 2.0 fusion.17
  345.7 21.8 %collective-permute-done.5 = f32[512,512]{0,1:T(8,128)} collective-permute-done((f32[512,512]{0,1:T(8,128)}, f32[512,512]{0,1:T(8,128)}, u32[]{:S(2)}, u32[]{:S(2)}) %collective-permute-start.5) | collective-permute-done | bytes 1048608 | tf_op jit(solution)/shard_map/ppermute | solution.py:18
  367.5 24.9 %collective-permute-done.4 = f32[512,512]{0,1:T(8,128)} collective-permute-done((f32[512,512]{0,1:T(8,128)}, f32[512,512]{0,1:T(8,128)}, u32[]{:S(2)}, u32[]{:S(2)}) %collective-permute-start.4) | collective-permute-done | bytes 1048608 | tf_op jit(solution)/shard_map/ppermute | solution.py:18
  392.5 1.8 fusion.15
  396.9 18.0 %collective-permute-done.6 = f32[512,512]{0,1:T(8,128)} collective-permute-done((f32[512,512]{0,1:T(8,128)}, f32[512,512]{0,1:T(8,128)}, u32[]{:S(2)}, u32[]{:S(2)}) %collective-permute-start.6) | collective-permute-done | bytes 1048608 | tf_op jit(solution)/shard_map/ppermute | solution.py:18
  414.9 1.9 fusion.14
  416.8 19.9 %fusion.4 = bf16[5376,2048]{0,1:T(8,128)(2,1)} fusion(bf16[512,5376]{1,0:T(8,128)(2,1)} %param.6, bf16[512,512]{0,1:T(8,128)(2,1)S(1)} %fusion.14, bf16[512,512]{0,1:T(8,128)(2,1)S(1)} %bitcast.121, bf16[512,1024]{0,1:T(8,128)(2,1)S(1)} %bitcast.118), kind=kOutput, calls=%fused_computation.8 | convolution fusion | flops 11291590656 | bytes 29622272 | tf_op jit(solution)/shard_map/nd,nc->dc/dot_general | solution.py:173
  436.7 28.7 %copy.124 = bf16[5376,2048]{1,0:T(8,128)(2,1)} copy(bf16[5376,2048]{0,1:T(8,128)(2,1)} %fusion.4) | data formatting | bytes 44040192
  465.7 17.6 %convolution_convert_fusion.2 = bf16[512,5376]{0,1:T(8,128)(2,1)} fusion(bf16[5376,2048]{1,0:T(8,128)(2,1)} %all-gather.3.cloned.1.call-done, bf16[512,512]{0,1:T(8,128)(2,1)S(1)} %fusion.14, bf16[512,512]{0,1:T(8,128)(2,1)S(1)} %bitcast.122, bf16[512,1024]{0,1:T(8,128)(2,1)S(1)} %bitcast.119), kind=kOutput, calls=%fused_computation.15 | convolution fusion | flops 11283333120 | bytes 29622272 | tf_op jit(solution)/shard_map/dot_general | solution.py:50
  483.3 1.9 copy.127
  485.3 2.1 copy.108
  487.3 118.6 %reduce-scatter.10.cloned.1.call-done = bf16[672,2048]{1,0:T(8,128)(2,1)} async-done(((bf16[5376,2048]{1,0:T(8,128)(2,1)}), bf16[672,2048]{1,0:T(8,128)(2,1)}) %reduce-scatter.10.cloned.1.call-update) | async-done | bytes 2752528
  606.0 3.1 copy.125
  609.1 1.9 slice.122
  611.0 3.4 copy.105
  614.4 2.2 fusion.27
  616.6 3.1 copy.107
  621.2 85.7 %reduce-scatter.8.cloned.1.call-done = bf16[512,1344]{0,1:T(8,128)(2,1)} async-done(((bf16[512,5376]{0,1:T(8,128)(2,1)}), bf16[512,1344]{0,1:T(8,128)(2,1)}) %reduce-scatter.8.cloned.1.call-update) | async-done | bytes 1376272 | tf_op jit(solution)/shard_map/reduce_scatter | solution.py:170
  (89 shorter events, 18.4 us)
Async XLA Ops:
  7.2 117.4 %all-gather.3.cloned.1.call-start = ((), (), s32[]{:S(2)}) async-start(), calls=%async_computation.3 | async-start | bytes 24772608 | tf_op jit(solution)/shard_map/all_gather | solution.py:93
  10.9 188.1 %all-gather.5.cloned.1.call-start = ((), (), s32[]{:S(2)}) async-start(), calls=%async_computation.4 | async-start | bytes 12386304 | tf_op jit(solution)/shard_map/all_gather | solution.py:96
  11.6 471.7 %reduce-scatter.12.cloned.1.call-start = ((), (), s32[]{:S(2)}) async-start(), calls=%async_computation.7 | async-start | bytes 12386304
  12.2 207.4 %copy-start.9 = (f32[512,64]{0,1:T(8,128)}, f32[512,64]{0,1:T(8,128)S(1)}, u32[]{:S(2)}) copy-start(f32[512,64]{0,1:T(8,128)S(1)} %get-tuple-element.46) | copy-start | bytes 393220
  12.5 131.7 %copy-start.8 = (f32[512,64]{1,0:T(8,128)}, f32[512,64]{1,0:T(8,128)S(1)}, u32[]{:S(2)}) copy-start(f32[512,64]{1,0:T(8,128)S(1)} %copy.86) | copy-start | bytes 393220
  141.3 2.0 copy-start.2
  144.8 54.2 %copy-start.4 = (bf16[512,4,128]{2,0,1:T(8,128)(2,1)}, bf16[512,4,128]{2,0,1:T(8,128)(2,1)S(1)}, u32[]{:S(2)}) copy-start(bf16[512,4,128]{2,0,1:T(8,128)(2,1)S(1)} %maximum_convert_fusion) | copy-start | bytes 1572868
  145.8 83.6 %collective-permute-start.1 = (bf16[512,512]{0,1:T(8,128)(2,1)}, bf16[512,512]{0,1:T(8,128)(2,1)}, u32[]{:S(2)}, u32[]{:S(2)}) collective-permute-start(bf16[512,512]{0,1:T(8,128)(2,1)} %bitcast.2), channel_id=1, source_target_pairs={{0,4},{4,8},{8,12},{12,16},{16,20},{20,24},{24,28},{1,5},{5,9},{9,... | collective-permute-start | bytes 1572872 | tf_op jit(solution)/shard_map/ppermute | solution.py:18
  148.1 82.7 %collective-permute-start = (bf16[512,512]{0,1:T(8,128)(2,1)}, bf16[512,512]{0,1:T(8,128)(2,1)}, u32[]{:S(2)}, u32[]{:S(2)}) collective-permute-start(bf16[512,512]{0,1:T(8,128)(2,1)} %bitcast.2), channel_id=1, source_target_pairs={{0,8},{4,12},{8,16},{12,20},{16,24},{20,28},{1,9},{5,13},{9,17},{1... | collective-permute-start | bytes 1572872 | tf_op jit(solution)/shard_map/ppermute | solution.py:18
  209.8 78.3 %copy-start.1 = (bf16[512,1024]{0,1:T(8,128)(2,1)}, bf16[512,1024]{0,1:T(8,128)(2,1)S(1)}, u32[]{:S(2)}) copy-start(bf16[512,1024]{0,1:T(8,128)(2,1)S(1)} %copy.132) | copy-start | bytes 3145732
  209.8 9.9 %slice-start.3 = ((f32[512,2048]{0,1:T(8,128)}), f32[512,1024]{0,1:T(8,128)S(1)}, s32[]{:S(2)}) async-start(f32[512,2048]{0,1:T(8,128)} %copy-done.2), calls=%async_computation.11 | async-start | bytes 4194304 | tf_op jit(solution)/shard_map/slice | solution.py:98
  212.4 44.7 %collective-permute-start.3 = (bf16[512,512]{0,1:T(8,128)(2,1)}, bf16[512,512]{0,1:T(8,128)(2,1)}, u32[]{:S(2)}, u32[]{:S(2)}) collective-permute-start(bf16[512,512]{0,1:T(8,128)(2,1)} %slice.134), channel_id=1, source_target_pairs={{0,4},{4,8},{8,12},{12,16},{16,20},{20,24},{24,28},{1,5},{5,9},{9,... | collective-permute-start | bytes 1572872 | tf_op jit(solution)/shard_map/ppermute | solution.py:18
  217.2 39.9 %collective-permute-start.2 = (bf16[512,512]{0,1:T(8,128)(2,1)}, bf16[512,512]{0,1:T(8,128)(2,1)}, u32[]{:S(2)}, u32[]{:S(2)}) collective-permute-start(bf16[512,512]{0,1:T(8,128)(2,1)} %slice.134), channel_id=1, source_target_pairs={{0,8},{4,12},{8,16},{12,20},{16,24},{20,28},{1,9},{5,13},{9,17},{1... | collective-permute-start | bytes 1572872 | tf_op jit(solution)/shard_map/ppermute | solution.py:18
  230.8 16.1 %copy-start.11 = (bf16[512,4,128]{2,0,1:T(8,128)(2,1)}, bf16[512,4,128]{2,0,1:T(8,128)(2,1)S(1)}, u32[]{:S(2)}) copy-start(bf16[512,4,128]{2,0,1:T(8,128)(2,1)S(1)} %copy.89) | copy-start | bytes 1572868
  232.3 14.5 %copy-start.13 = (bf16[512,4,128]{2,0,1:T(8,128)(2,1)}, bf16[512,4,128]{2,0,1:T(8,128)(2,1)S(1)}, u32[]{:S(2)}) copy-start(bf16[512,4,128]{2,0,1:T(8,128)(2,1)S(1)} %copy.88) | copy-start | bytes 1572868
  257.1 6.4 copy-start
  257.1 7.0 slice-start.4
  259.9 4.8 slice-start.5
  287.8 318.1 %reduce-scatter.10.cloned.1.call-start = ((), (), s32[]{:S(2)}) async-start(), calls=%async_computation.6 | async-start | bytes 24772608
  315.0 27.0 %slice-start = ((s8[12582912]{0:T(1024)(128)(4,1)}), s8[4194304]{0:T(1024)(128)(4,1)S(1)}, s32[]{:S(2)}) async-start(s8[12582912]{0:T(1024)(128)(4,1)} %bitcast.106), calls=%async_computation.8 | async-start | bytes 8388608
  316.7 50.8 %collective-permute-start.5 = (f32[512,512]{0,1:T(8,128)}, f32[512,512]{0,1:T(8,128)}, u32[]{:S(2)}, u32[]{:S(2)}) collective-permute-start(f32[512,512]{0,1:T(8,128)} %bitcast.29), channel_id=1, source_target_pairs={{8,0},{12,4},{16,8},{20,12},{24,16},{28,20},{9,1},{13,5},{17,9},{2... | collective-permute-start | bytes 3145736 | tf_op jit(solution)/shard_map/ppermute | solution.py:18
  320.6 21.4 %slice-start.1 = ((s8[12582912]{0:T(1024)(128)(4,1)}), s8[4194304]{0:T(1024)(128)(4,1)S(1)}, s32[]{:S(2)}) async-start(s8[12582912]{0:T(1024)(128)(4,1)} %bitcast.106), calls=%async_computation.9 | async-start | bytes 8388608
  320.6 21.4 %slice-start.2 = ((s8[12582912]{0:T(1024)(128)(4,1)}), s8[4194304]{0:T(1024)(128)(4,1)S(1)}, s32[]{:S(2)}) async-start(s8[12582912]{0:T(1024)(128)(4,1)} %bitcast.106), calls=%async_computation.10 | async-start | bytes 8388608
  320.6 71.9 %collective-permute-start.4 = (f32[512,512]{0,1:T(8,128)}, f32[512,512]{0,1:T(8,128)}, u32[]{:S(2)}, u32[]{:S(2)}) collective-permute-start(f32[512,512]{0,1:T(8,128)} %bitcast.28), channel_id=1, source_target_pairs={{4,0},{8,4},{12,8},{16,12},{20,16},{24,20},{28,24},{5,1},{9,5},{13... | collective-permute-start | bytes 3145736 | tf_op jit(solution)/shard_map/ppermute | solution.py:18
  334.1 8.0 %copy-start.5 = (bf16[512,4,128]{2,0,1:T(8,128)(2,1)S(1)}, bf16[512,4,128]{2,0,1:T(8,128)(2,1)}, u32[]{:S(2)}) copy-start(bf16[512,4,128]{2,0,1:T(8,128)(2,1)} %copy-done.4) | copy-start | bytes 1572868
  334.1 8.0 %copy-start.12 = (bf16[512,4,128]{2,0,1:T(8,128)(2,1)S(1)}, bf16[512,4,128]{2,0,1:T(8,128)(2,1)}, u32[]{:S(2)}) copy-start(bf16[512,4,128]{2,0,1:T(8,128)(2,1)} %copy-done.11) | copy-start | bytes 1572868
  334.1 8.0 %copy-start.14 = (bf16[512,4,128]{2,0,1:T(8,128)(2,1)S(1)}, bf16[512,4,128]{2,0,1:T(8,128)(2,1)}, u32[]{:S(2)}) copy-start(bf16[512,4,128]{2,0,1:T(8,128)(2,1)} %copy-done.13) | copy-start | bytes 1572868
  337.8 59.1 %collective-permute-start.7 = (f32[512,512]{0,1:T(8,128)}, f32[512,512]{0,1:T(8,128)}, u32[]{:S(2)}, u32[]{:S(2)}) collective-permute-start(f32[512,512]{0,1:T(8,128)} %bitcast.38), channel_id=1, source_target_pairs={{8,0},{12,4},{16,8},{20,12},{24,16},{28,20},{9,1},{13,5},{17,9},{2... | collective-permute-start | bytes 3145736 | tf_op jit(solution)/shard_map/ppermute | solution.py:18
  339.7 4.4 copy-start.10
  339.7 75.2 %collective-permute-start.6 = (f32[512,512]{0,1:T(8,128)}, f32[512,512]{0,1:T(8,128)}, u32[]{:S(2)}, u32[]{:S(2)}) collective-permute-start(f32[512,512]{0,1:T(8,128)} %bitcast.37), channel_id=1, source_target_pairs={{4,0},{8,4},{12,8},{16,12},{20,16},{24,20},{28,24},{5,1},{9,5},{13... | collective-permute-start | bytes 3145736 | tf_op jit(solution)/shard_map/ppermute | solution.py:18
  344.1 48.4 %copy-start.7 = (f32[512,4,128]{0,2,1:T(8,128)S(1)}, f32[512,4,128]{0,2,1:T(8,128)}, u32[]{:S(2)}) copy-start(f32[512,4,128]{0,2,1:T(8,128)} %get-tuple-element.27) | copy-start | bytes 3145732
  395.0 19.9 %copy-start.6 = (f32[512,4,128]{0,2,1:T(8,128)S(1)}, f32[512,4,128]{0,2,1:T(8,128)}, u32[]{:S(2)}) copy-start(f32[512,4,128]{0,2,1:T(8,128)} %get-tuple-element.30) | copy-start | bytes 3145732
  396.4 20.4 %copy-start.15 = (bf16[512,8,128]{0,2,1:T(8,128)(2,1)S(1)}, bf16[512,8,128]{0,2,1:T(8,128)(2,1)}, u32[]{:S(2)}) copy-start(bf16[512,8,128]{0,2,1:T(8,128)(2,1)} %fusion.12) | copy-start | bytes 3145732
  465.4 241.4 %reduce-scatter.8.cloned.1.call-start = ((), (), s32[]{:S(2)}) async-start(), calls=%async_computation.5 | async-start | bytes 6881280 | tf_op jit(solution)/shard_map/reduce_scatter | solution.py:170
  616.6 3.1 copy-start.3
Sparse Core Ops, SparseCore 0:
  11.0 113.5 all-gather.2
  126.4 72.5 all-gather.4
  287.9 152.1 reduce-scatter.11
  465.5 140.3 reduce-scatter.9
  608.7 98.1 reduce-scatter.7

commit v5 on v4

--- a/solution.py
+++ b/solution.py
@@ -45,6 +45,20 @@
         axis=-1,
     )
 
+
+def sum_over_heads(partial):
+    count = lax.axis_size("head")
+    me = lax.axis_index("head")
+    rows, width = partial.shape
+    blocks = partial.reshape(rows, count, width // count)
+    total = lax.dynamic_index_in_dim(blocks, me, axis=1, keepdims=False).astype(jnp.float32)
+    for shift in range(1, count):
+        outgoing = lax.dynamic_index_in_dim(blocks, (me + shift) % count, axis=1, keepdims=False)
+        incoming = lax.ppermute(
+            outgoing, "head", [(source, (source + shift) % count) for source in range(count)]
+        )
+        total = total + incoming.astype(jnp.float32)
+    return total.astype(jnp.bfloat16)
 
 def dot_rows(left, weight):
     return lax.dot_general(
@@ -167,9 +181,7 @@
     value_gradient = own_values.astype(jnp.bfloat16)
     grads_qkv = jnp.concatenate([dquery, key_gradient, value_gradient], axis=1)
     partial_in = dot_rows(grads_qkv, full_qkv)
-    in_grad = lax.psum_scatter(
-        partial_in.astype(jnp.bfloat16), "head", scatter_dimension=1, tiled=True
-    )
+    in_grad = sum_over_heads(partial_in.astype(jnp.bfloat16))
     grad_qkv_part = jnp.einsum("nd,nc->dc", hidden_in, grads_qkv, preferred_element_type=jnp.float32)
     grad_out_w = lax.psum_scatter(
         grad_w_out.astype(jnp.bfloat16), "ctx", scatter_dimension=0, tiled=True

time: 723 us -> 655 us (0.906)
  waiting for transfers between devices: 428 us -> 342 us
  local copies, waits for them, and re-layouts: 87 us -> 99.2 us
    unnamed x7 -> x6, waiting for transfers between devices: 119 us -> 0.75 us
    ppermute x0 -> x3, waiting for transfers between devices: none -> 118 us  [sum_over_heads(): lax.ppermute(outgoing, 'head', [(source, (source + shift) % count) for so...]
    reduce_scatter x1 -> x0, waiting for transfers between devices: 85.7 us -> none  [shards(): lax.psum_scatter(partial_in.astype(jnp.bfloat16), 'head', scatter_dimensi...]
    convert_element_type x0 -> x1, local copies, waits for them, and re-layouts: none -> 9.02 us  [shards(): in_grad = sum_over_heads(partial_in.astype(jnp.bfloat16))]
    unnamed x54 -> x56, local copies, waits for them, and re-layouts: 64.8 us -> 63.2 us
  transfers between devices with their start and end apart: 13 -> 15, of which waited for: 7 -> 8; matrix products, arithmetic and copies ran while one was open for 30% -> 33% of each run, Pallas kernels for 0% -> 0%
where the time goes in v5:
time: 655 us; the launch traced here: 647 us
  waiting for transfers between devices  342 us (52%)
  matrix products  130 us (20%)
  local copies, waits for them, and re-layouts  99.2 us (15%)
  other arithmetic  34.9 us (5%)
  starting transfers between devices  26.5 us (4%)
  between operations  14.6 us (2%)
    ppermute x3, waiting for transfers between devices, sum_over_heads(): lax.ppermute(outgoing, 'head', [(source, (source + shift) % count) for so...  118 us
    all_gather x1, waiting for transfers between devices, shards(): lax.all_gather(jnp.concatenate([w_query, key_weight, value_weight], axis=...  110 us
    ppermute x8, waiting for transfers between devices, from_behind(): lax.ppermute(value, axis, [(source, source + steps) for source in range(i...  65.1 us
    unnamed x56, local copies, waits for them, and re-layouts  63.2 us
    all_gather x1, waiting for transfers between devices, shards(): full_out = lax.all_gather(w_out, 'ctx', axis=0, tiled=True)  47.8 us
    ppermute x8, starting transfers between devices, from_behind(): lax.ppermute(value, axis, [(source, source + steps) for source in range(i...  22.5 us
    dot_general x1, matrix products, shards(): jnp.einsum('nd,nc->dc', hidden_in, grads_qkv, preferred_element_type=jnp....  20.3 us
    dot_general x1, matrix products, dot_rows(): lax.dot_general(left, weight, (((1,), (1,)), ((), ())), preferred_element...  18 us
  transfers between devices with their start and end apart: 15, of which 8 were waited for; matrix products, arithmetic and copies ran while one was open for 33% of the time, Pallas kernels for 0%

profile of v5, /device:TPU:3, one launch (start us, length us, event | category | flops | bytes accessed | tf_op | source)
XLA Modules:
  0.0 647.3 jit_solution(17923927879507330878)
XLA Ops:
  7.2 3.6 pad_maximum_fusion
  12.6 1.9 and_and_fusion
  14.4 110.1 %all-gather.3.cloned.1.call-done = bf16[5376,2048]{1,0:T(8,128)(2,1)} async-done(((bf16[672,2048]{1,0:T(8,128)(2,1)}), bf16[5376,2048]{1,0:T(8,128)(2,1)}) %all-gather.3.cloned.1.call-update) | async-done | bytes 22020112 | tf_op jit(solution)/shard_map/all_gather | solution.py:107
  124.6 16.6 %convolution_bitcast_fusion.2 = f32[512,2048]{0,1:T(8,128)S(1)} fusion(bf16[5376,2048]{1,0:T(8,128)(2,1)} %all-gather.3.cloned.1.call-done, bf16[512,5376]{1,0:T(8,128)(2,1)} %param.6), kind=kOutput, calls=%fused_computation.18 | convolution fusion | flops 11274289152 | bytes 31719424 | tf_op jit(solution)/shard_map/dot_general | solution.py:111
  141.2 2.0 copy-done.2
  145.7 2.3 collective-permute-start.1
  147.9 3.2 collective-permute-start
  151.1 47.8 %all-gather.5.cloned.1.call-done = bf16[5376,1024]{1,0:T(8,128)(2,1)} async-done(((bf16[672,1024]{1,0:T(8,128)(2,1)}), bf16[5376,1024]{1,0:T(8,128)(2,1)}) %all-gather.5.cloned.1.call-update) | async-done | bytes 11010064 | tf_op jit(solution)/shard_map/all_gather | solution.py:110
  199.0 10.2 %convolution_convert_fusion.3 = bf16[512,1024]{1,0:T(8,128)(2,1)S(1)} fusion(bf16[512,5376]{1,0:T(8,128)(2,1)} %param.7, bf16[5376,1024]{1,0:T(8,128)(2,1)} %all-gather.5.cloned.1.call-done), kind=kOutput, calls=%fused_computation.34 | convolution fusion | flops 5637668864 | bytes 17563648 | tf_op jit(solution)/shard_map/dot_general | solution.py:115
  209.8 2.5 slice.134
  212.3 4.8 collective-permute-start.3
  217.1 2.1 collective-permute-start.2
  222.7 3.2 copy.97
  225.9 3.2 fusion.14
  231.9 14.5 %fusion.35 = (f32[4,2,512]{2,1,0:T(2,128)S(1)}, f32[4,2,512,1536]{2,3,1,0:T(8,128)}) fusion(pred[512,1536]{0,1:T(8,128)(4,1)} %and_and_fusion, bf16[512,4,2,128]{3,0,2,1:T(8,128)(2,1)} %fusion.14, bf16[512,4,128]{2,0,1:T(8,128)(2,1)} %copy-done.5, bf16[512,4,128]{2,0,1:T(8,128)(2,1)S(1)} %copy.95, bf16[512,4,128]{2,0,1:T(8,128)(2,1)S(1)} %copy.94), kind=kOutput, calls=%fused_computation.76 | convolution fusion | flops 1634207232 | bytes 28590080 | tf_op jit(solution)/shard_map/sub | solution.py:73
  246.4 10.2 %fusion.7 = bf16[4,2,512,1536]{2,3,1,0:T(8,128)(2,1)S(1)} fusion(f32[4,2,512,1536]{2,3,1,0:T(8,128)} %get-tuple-element.51, f32[4,2,512]{2,1,0:T(2,128)S(1)} %get-tuple-element.50), kind=kLoop, calls=%fused_computation.13 | loop fusion | flops 12582912 | bytes 37765120 | tf_op jit(solution)/shard_map/convert_element_type | solution.py:75
  256.7 2.8 pad_maximum_fusion.2
  259.5 1.8 multiply_reduce_fusion
  264.3 8.5 %fusion.8 = bf16[5376,1024]{0,1:T(8,128)(2,1)} fusion(bf16[512,1024]{0,1:T(8,128)(2,1)S(1)} %bitcast.132, bf16[512,5376]{1,0:T(8,128)(2,1)S(1)} %bitcast.137), kind=kOutput, calls=%fused_computation.14 | convolution fusion | flops 5642649600 | bytes 17563648 | tf_op jit(solution)/shard_map/nd,nc->dc/dot_general | solution.py:151
  272.7 14.6 %copy.133 = bf16[5376,1024]{1,0:T(8,128)(2,1)} copy(bf16[5376,1024]{0,1:T(8,128)(2,1)} %fusion.8) | data formatting | bytes 22020096
  287.7 17.0 %fusion.2 = bf16[4,2,512,1536]{2,3,1,0:T(8,128)(2,1)} fusion(bf16[1536,4,128,1]{0,2,3,1:T(8,128)(2,1)S(1)} %bitcast.127, bf16[512,4,2,128]{0,3,2,1:T(8,128)(2,1)S(1)} %bitcast.120, f32[4,2,512]{2,1,0:T(2,128)S(1)} %bitcast.135, f32[4,2,512,1536]{2,3,1,0:T(8,128)} %get-tuple-element.51, f32[4,2,512]{2,1,0:T(2,128)S(1)} %get-tuple-element.50), kind=kOutput, calls=%fused_computation.3 | convolution fusion | flops 1635778560 | bytes 40402944 | tf_op jit(solution)/shard_map/ngrd,mgd->grnm/dot_general | solution.py:85
  304.7 9.9 %convolution_bitcast_fusion.1 = f32[1536,4,128]{0,2,1:T(8,128)S(1)} fusion(bf16[512,4,2,128]{3,0,2,1:T(8,128)(2,1)} %fusion.14, bf16[4,2,512,1536]{2,3,1,0:T(8,128)(2,1)} %fusion.2), kind=kOutput, calls=%fused_computation.17 | convolution fusion | flops 1610612736 | bytes 16777216 | tf_op jit(solution)/shard_map/grnm,ngrd->mgd/dot_general | solution.py:90
  316.3 3.9 collective-permute-start.5
  320.2 2.3 collective-permute-start.4
  322.5 11.1 %convolution_bitcast_fusion = f32[1536,4,128]{0,2,1:T(8,128)} fusion(bf16[512,4,2,128]{0,3,2,1:T(8,128)(2,1)} %bitcast.121, bf16[4,2,512,1536]{2,3,1,0:T(8,128)(2,1)} %copy-done), kind=kOutput, calls=%fused_computation.16 | convolution fusion | flops 1610612736 | bytes 16777216 | tf_op jit(solution)/shard_map/grnm,ngrd->mgd/dot_general | solution.py:93
  333.6 3.7 fusion.32
  337.4 1.9 collective-permute-start.7
  339.3 2.1 collective-permute-start.6
  341.4 2.0 fusion.20
  345.0 22.1 %collective-permute-done.5 = f32[512,512]{0,1:T(8,128)} collective-permute-done((f32[512,512]{0,1:T(8,128)}, f32[512,512]{0,1:T(8,128)}, u32[]{:S(2)}, u32[]{:S(2)}) %collective-permute-start.5) | collective-permute-done | bytes 1048608 | tf_op jit(solution)/shard_map/ppermute | solution.py:18
  367.1 24.9 %collective-permute-done.4 = f32[512,512]{0,1:T(8,128)} collective-permute-done((f32[512,512]{0,1:T(8,128)}, f32[512,512]{0,1:T(8,128)}, u32[]{:S(2)}, u32[]{:S(2)}) %collective-permute-start.4) | collective-permute-done | bytes 1048608 | tf_op jit(solution)/shard_map/ppermute | solution.py:18
  396.5 18.0 %collective-permute-done.6 = f32[512,512]{0,1:T(8,128)} collective-permute-done((f32[512,512]{0,1:T(8,128)}, f32[512,512]{0,1:T(8,128)}, u32[]{:S(2)}, u32[]{:S(2)}) %collective-permute-start.6) | collective-permute-done | bytes 1048608 | tf_op jit(solution)/shard_map/ppermute | solution.py:18
  414.5 1.9 fusion.17
  416.4 20.3 %fusion.4 = bf16[5376,2048]{0,1:T(8,128)(2,1)} fusion(bf16[512,5376]{1,0:T(8,128)(2,1)} %param.6, bf16[512,512]{0,1:T(8,128)(2,1)S(1)} %fusion.17, bf16[512,512]{0,1:T(8,128)(2,1)S(1)} %bitcast.133, bf16[512,1024]{0,1:T(8,128)(2,1)S(1)} %bitcast.130), kind=kOutput, calls=%fused_computation.8 | convolution fusion | flops 11291590656 | bytes 29622272 | tf_op jit(solution)/shard_map/nd,nc->dc/dot_general | solution.py:185
  436.7 28.7 %copy.131 = bf16[5376,2048]{1,0:T(8,128)(2,1)} copy(bf16[5376,2048]{0,1:T(8,128)(2,1)} %fusion.4) | data formatting | bytes 44040192
  465.5 18.0 %convolution_convert_fusion.2 = bf16[512,5376]{1,0:T(8,128)(2,1)} fusion(bf16[5376,2048]{1,0:T(8,128)(2,1)} %all-gather.3.cloned.1.call-done, bf16[512,512]{0,1:T(8,128)(2,1)S(1)} %fusion.17, bf16[512,512]{0,1:T(8,128)(2,1)S(1)} %bitcast.134, bf16[512,1024]{0,1:T(8,128)(2,1)S(1)} %bitcast.131), kind=kOutput, calls=%fused_computation.15 | convolution fusion | flops 11283333120 | bytes 29622272 | tf_op jit(solution)/shard_map/dot_general | solution.py:64
  483.5 9.0 %copy.111 = bf16[512,5376]{0,1:T(8,128)(2,1)} copy(bf16[512,5376]{1,0:T(8,128)(2,1)} %convolution_convert_fusion.2) | data formatting | bytes 11010048 | tf_op jit(solution)/shard_map/convert_element_type | solution.py:184
  492.5 5.2 dynamic-slice_bitcast_fusion.2
  498.9 2.1 collective-permute-start.10
  501.3 30.4 %collective-permute-done.8 = bf16[512,1344]{0,1:T(8,128)(2,1)S(1)} collective-permute-done((bf16[512,1344]{0,1:T(8,128)(2,1)}, bf16[512,1344]{0,1:T(8,128)(2,1)S(1)}, u32[]{:S(2)}, u32[]{:S(2)}) %collective-permute-start.8) | collective-permute-done | bytes 1376288 | tf_op jit(solution)/shard_map/ppermute | solution.py:57
  531.7 28.9 %collective-permute-done.10 = bf16[512,1344]{0,1:T(8,128)(2,1)S(1)} collective-permute-done((bf16[512,1344]{0,1:T(8,128)(2,1)}, bf16[512,1344]{0,1:T(8,128)(2,1)S(1)}, u32[]{:S(2)}, u32[]{:S(2)}) %collective-permute-start.10) | collective-permute-done | bytes 1376288 | tf_op jit(solution)/shard_map/ppermute | solution.py:57
  560.5 59.3 %collective-permute-done.9 = bf16[512,1344]{0,1:T(8,128)(2,1)} collective-permute-done((bf16[512,1344]{0,1:T(8,128)(2,1)}, bf16[512,1344]{0,1:T(8,128)(2,1)}, u32[]{:S(2)}, u32[]{:S(2)}) %collective-permute-start.9) | collective-permute-done | bytes 1376288 | tf_op jit(solution)/shard_map/ppermute | solution.py:57
  619.8 3.6 fusion.13
  625.2 1.9 copy.115
  627.1 3.1 copy.132
  630.2 1.9 slice.122
  632.1 1.9 fusion.30
  634.0 3.6 copy.112
  (97 shorter events, 28.3 us)
Async XLA Ops:
  7.2 117.4 %all-gather.3.cloned.1.call-start = ((), (), s32[]{:S(2)}) async-start(), calls=%async_computation.2 | async-start | bytes 24772608 | tf_op jit(solution)/shard_map/all_gather | solution.py:107
  10.9 188.1 %all-gather.5.cloned.1.call-start = ((), (), s32[]{:S(2)}) async-start(), calls=%async_computation.3 | async-start | bytes 12386304 | tf_op jit(solution)/shard_map/all_gather | solution.py:110
  11.6 611.8 %reduce-scatter.9.cloned.1.call-start = ((), (), s32[]{:S(2)}) async-start(), calls=%async_computation.5 | async-start | bytes 12386304
  12.2 207.0 %copy-start.10 = (f32[512,64]{0,1:T(8,128)}, f32[512,64]{0,1:T(8,128)S(1)}, u32[]{:S(2)}) copy-start(f32[512,64]{0,1:T(8,128)S(1)} %get-tuple-element.49) | copy-start | bytes 393220
  12.5 131.5 %copy-start.9 = (f32[512,64]{1,0:T(8,128)}, f32[512,64]{1,0:T(8,128)S(1)}, u32[]{:S(2)}) copy-start(f32[512,64]{1,0:T(8,128)S(1)} %copy.92) | copy-start | bytes 393220
  141.1 2.0 copy-start.2
  144.6 54.3 %copy-start.5 = (bf16[512,4,128]{2,0,1:T(8,128)(2,1)}, bf16[512,4,128]{2,0,1:T(8,128)(2,1)S(1)}, u32[]{:S(2)}) copy-start(bf16[512,4,128]{2,0,1:T(8,128)(2,1)S(1)} %maximum_convert_fusion) | copy-start | bytes 1572868
  145.7 83.4 %collective-permute-start.1 = (bf16[512,512]{0,1:T(8,128)(2,1)}, bf16[512,512]{0,1:T(8,128)(2,1)}, u32[]{:S(2)}, u32[]{:S(2)}) collective-permute-start(bf16[512,512]{0,1:T(8,128)(2,1)} %bitcast.2), channel_id=1, source_target_pairs={{0,4},{4,8},{8,12},{12,16},{16,20},{20,24},{24,28},{1,5},{5,9},{9,... | collective-permute-start | bytes 1572872 | tf_op jit(solution)/shard_map/ppermute | solution.py:18
  147.9 82.4 %collective-permute-start = (bf16[512,512]{0,1:T(8,128)(2,1)}, bf16[512,512]{0,1:T(8,128)(2,1)}, u32[]{:S(2)}, u32[]{:S(2)}) collective-permute-start(bf16[512,512]{0,1:T(8,128)(2,1)} %bitcast.2), channel_id=1, source_target_pairs={{0,8},{4,12},{8,16},{12,20},{16,24},{20,28},{1,9},{5,13},{9,17},{1... | collective-permute-start | bytes 1572872 | tf_op jit(solution)/shard_map/ppermute | solution.py:18
  209.7 77.9 %copy-start.1 = (bf16[512,1024]{0,1:T(8,128)(2,1)}, bf16[512,1024]{0,1:T(8,128)(2,1)S(1)}, u32[]{:S(2)}) copy-start(bf16[512,1024]{0,1:T(8,128)(2,1)S(1)} %copy.139) | copy-start | bytes 3145732
  209.8 9.5 %slice-start.3 = ((f32[512,2048]{0,1:T(8,128)}), f32[512,1024]{0,1:T(8,128)S(1)}, s32[]{:S(2)}) async-start(f32[512,2048]{0,1:T(8,128)} %copy-done.2), calls=%async_computation.9 | async-start | bytes 4194304 | tf_op jit(solution)/shard_map/slice | solution.py:112
  212.3 44.4 %collective-permute-start.3 = (bf16[512,512]{0,1:T(8,128)(2,1)}, bf16[512,512]{0,1:T(8,128)(2,1)}, u32[]{:S(2)}, u32[]{:S(2)}) collective-permute-start(bf16[512,512]{0,1:T(8,128)(2,1)} %slice.134), channel_id=1, source_target_pairs={{0,4},{4,8},{8,12},{12,16},{16,20},{20,24},{24,28},{1,5},{5,9},{9,... | collective-permute-start | bytes 1572872 | tf_op jit(solution)/shard_map/ppermute | solution.py:18
  217.1 39.6 %collective-permute-start.2 = (bf16[512,512]{0,1:T(8,128)(2,1)}, bf16[512,512]{0,1:T(8,128)(2,1)}, u32[]{:S(2)}, u32[]{:S(2)}) collective-permute-start(bf16[512,512]{0,1:T(8,128)(2,1)} %slice.134), channel_id=1, source_target_pairs={{0,8},{4,12},{8,16},{12,20},{16,24},{20,28},{1,9},{5,13},{9,17},{1... | collective-permute-start | bytes 1572872 | tf_op jit(solution)/shard_map/ppermute | solution.py:18
  230.4 16.1 %copy-start.12 = (bf16[512,4,128]{2,0,1:T(8,128)(2,1)}, bf16[512,4,128]{2,0,1:T(8,128)(2,1)S(1)}, u32[]{:S(2)}) copy-start(bf16[512,4,128]{2,0,1:T(8,128)(2,1)S(1)} %copy.95) | copy-start | bytes 1572868
  231.9 14.5 %copy-start.14 = (bf16[512,4,128]{2,0,1:T(8,128)(2,1)}, bf16[512,4,128]{2,0,1:T(8,128)(2,1)S(1)}, u32[]{:S(2)}) copy-start(bf16[512,4,128]{2,0,1:T(8,128)(2,1)S(1)} %copy.94) | copy-start | bytes 1572868
  256.7 6.4 copy-start
  256.7 7.0 %slice-start.4 = ((s8[5505024]{0:T(1024)(128)(4,1)}), s8[4194304]{0:T(1024)(128)(4,1)S(1)}, s32[]{:S(2)}) async-start(s8[5505024]{0:T(1024)(128)(4,1)} %bitcast.136), calls=%async_computation.10 | async-start | bytes 8388608
  259.5 4.8 slice-start.5
  287.4 339.7 %reduce-scatter.7.cloned.1.call-start = ((), (), s32[]{:S(2)}) async-start(), calls=%async_computation.4 | async-start | bytes 24772608
  314.6 26.8 %slice-start = ((s8[12582912]{0:T(1024)(128)(4,1)}), s8[4194304]{0:T(1024)(128)(4,1)S(1)}, s32[]{:S(2)}) async-start(s8[12582912]{0:T(1024)(128)(4,1)} %bitcast.116), calls=%async_computation.6 | async-start | bytes 8388608
  316.3 50.8 %collective-permute-start.5 = (f32[512,512]{0,1:T(8,128)}, f32[512,512]{0,1:T(8,128)}, u32[]{:S(2)}, u32[]{:S(2)}) collective-permute-start(f32[512,512]{0,1:T(8,128)} %bitcast.29), channel_id=1, source_target_pairs={{8,0},{12,4},{16,8},{20,12},{24,16},{28,20},{9,1},{13,5},{17,9},{2... | collective-permute-start | bytes 3145736 | tf_op jit(solution)/shard_map/ppermute | solution.py:18
  320.2 21.2 %slice-start.1 = ((s8[12582912]{0:T(1024)(128)(4,1)}), s8[4194304]{0:T(1024)(128)(4,1)S(1)}, s32[]{:S(2)}) async-start(s8[12582912]{0:T(1024)(128)(4,1)} %bitcast.116), calls=%async_computation.7 | async-start | bytes 8388608
  320.2 21.2 %slice-start.2 = ((s8[12582912]{0:T(1024)(128)(4,1)}), s8[4194304]{0:T(1024)(128)(4,1)S(1)}, s32[]{:S(2)}) async-start(s8[12582912]{0:T(1024)(128)(4,1)} %bitcast.116), calls=%async_computation.8 | async-start | bytes 8388608
  320.2 71.8 %collective-permute-start.4 = (f32[512,512]{0,1:T(8,128)}, f32[512,512]{0,1:T(8,128)}, u32[]{:S(2)}, u32[]{:S(2)}) collective-permute-start(f32[512,512]{0,1:T(8,128)} %bitcast.28), channel_id=1, source_target_pairs={{4,0},{8,4},{12,8},{16,12},{20,16},{24,20},{28,24},{5,1},{9,5},{13... | collective-permute-start | bytes 3145736 | tf_op jit(solution)/shard_map/ppermute | solution.py:18
  333.6 7.7 %copy-start.6 = (bf16[512,4,128]{2,0,1:T(8,128)(2,1)S(1)}, bf16[512,4,128]{2,0,1:T(8,128)(2,1)}, u32[]{:S(2)}) copy-start(bf16[512,4,128]{2,0,1:T(8,128)(2,1)} %copy-done.5) | copy-start | bytes 1572868
  333.6 7.7 %copy-start.13 = (bf16[512,4,128]{2,0,1:T(8,128)(2,1)S(1)}, bf16[512,4,128]{2,0,1:T(8,128)(2,1)}, u32[]{:S(2)}) copy-start(bf16[512,4,128]{2,0,1:T(8,128)(2,1)} %copy-done.12) | copy-start | bytes 1572868
  333.6 7.8 %copy-start.15 = (bf16[512,4,128]{2,0,1:T(8,128)(2,1)S(1)}, bf16[512,4,128]{2,0,1:T(8,128)(2,1)}, u32[]{:S(2)}) copy-start(bf16[512,4,128]{2,0,1:T(8,128)(2,1)} %copy-done.14) | copy-start | bytes 1572868
  337.4 59.1 %collective-permute-start.7 = (f32[512,512]{0,1:T(8,128)}, f32[512,512]{0,1:T(8,128)}, u32[]{:S(2)}, u32[]{:S(2)}) collective-permute-start(f32[512,512]{0,1:T(8,128)} %bitcast.38), channel_id=1, source_target_pairs={{8,0},{12,4},{16,8},{20,12},{24,16},{28,20},{9,1},{13,5},{17,9},{2... | collective-permute-start | bytes 3145736 | tf_op jit(solution)/shard_map/ppermute | solution.py:18
  339.3 4.1 copy-start.11
  339.3 75.2 %collective-permute-start.6 = (f32[512,512]{0,1:T(8,128)}, f32[512,512]{0,1:T(8,128)}, u32[]{:S(2)}, u32[]{:S(2)}) collective-permute-start(f32[512,512]{0,1:T(8,128)} %bitcast.37), channel_id=1, source_target_pairs={{4,0},{8,4},{12,8},{16,12},{20,16},{24,20},{28,24},{5,1},{9,5},{13... | collective-permute-start | bytes 3145736 | tf_op jit(solution)/shard_map/ppermute | solution.py:18
  343.4 48.6 %copy-start.8 = (f32[512,4,128]{0,2,1:T(8,128)S(1)}, f32[512,4,128]{0,2,1:T(8,128)}, u32[]{:S(2)}) copy-start(f32[512,4,128]{0,2,1:T(8,128)} %get-tuple-element.30) | copy-start | bytes 3145732
  394.6 19.9 %copy-start.7 = (f32[512,4,128]{0,2,1:T(8,128)S(1)}, f32[512,4,128]{0,2,1:T(8,128)}, u32[]{:S(2)}) copy-start(f32[512,4,128]{0,2,1:T(8,128)} %get-tuple-element.33) | copy-start | bytes 3145732
  395.9 20.4 %copy-start.16 = (bf16[512,8,128]{0,2,1:T(8,128)(2,1)S(1)}, bf16[512,8,128]{0,2,1:T(8,128)(2,1)}, u32[]{:S(2)}) copy-start(bf16[512,8,128]{0,2,1:T(8,128)(2,1)} %fusion.15) | copy-start | bytes 3145732
  497.7 34.0 %collective-permute-start.8 = (bf16[512,1344]{0,1:T(8,128)(2,1)}, bf16[512,1344]{0,1:T(8,128)(2,1)S(1)}, u32[]{:S(2)}, u32[]{:S(2)}) collective-permute-start(bf16[512,1344]{0,1:T(8,128)(2,1)} %get-tuple-element.25), channel_id=1, source_target_pairs={{0,1},{1,2},{2,3},{3,0},{4,5},{5,6},{6,7},{7,4},{8,9},{9,10},{10,1... | collective-permute-start | bytes 4128776 | tf_op jit(solution)/shard_map/ppermute | solution.py:57
  498.9 61.6 %collective-permute-start.10 = (bf16[512,1344]{0,1:T(8,128)(2,1)}, bf16[512,1344]{0,1:T(8,128)(2,1)S(1)}, u32[]{:S(2)}, u32[]{:S(2)}) collective-permute-start(bf16[512,1344]{0,1:T(8,128)(2,1)} %get-tuple-element.26), channel_id=1, source_target_pairs={{0,3},{1,0},{2,1},{3,2},{4,7},{5,4},{6,5},{7,6},{8,11},{9,8},{10,9... | collective-permute-start | bytes 4128776 | tf_op jit(solution)/shard_map/ppermute | solution.py:57
  501.0 118.8 %collective-permute-start.9 = (bf16[512,1344]{0,1:T(8,128)(2,1)}, bf16[512,1344]{0,1:T(8,128)(2,1)}, u32[]{:S(2)}, u32[]{:S(2)}) collective-permute-start(bf16[512,1344]{0,1:T(8,128)(2,1)} %get-tuple-element.27), channel_id=1, source_target_pairs={{0,2},{1,3},{2,0},{3,1},{4,6},{5,7},{6,4},{7,5},{8,10},{9,11},{10,... | collective-permute-start | bytes 4128776 | tf_op jit(solution)/shard_map/ppermute | solution.py:57
  634.0 3.6 copy-start.4
  634.0 5.1 copy-start.3
Sparse Core Ops, SparseCore 0:
  11.0 113.5 all-gather.2
  126.4 72.4 all-gather.4
  287.5 152.1 reduce-scatter.8
  465.5 140.4 reduce-scatter.6

commit v6 on v5

--- a/solution.py
+++ b/solution.py
@@ -2,6 +2,7 @@
 import jax.numpy as jnp
 from jax import lax
 from jax.sharding import PartitionSpec as P
+from jax.experimental.layout import Layout, with_layout_constraint
 
 HEAD_WIDTH = 128
 WINDOW = 1024
@@ -59,6 +60,10 @@
         )
         total = total + incoming.astype(jnp.float32)
     return total.astype(jnp.bfloat16)
+
+
+def row_major(value):
+    return with_layout_constraint(value, Layout(tuple(range(value.ndim))))
 
 def dot_rows(left, weight):
     return lax.dot_general(
@@ -161,10 +166,15 @@
     for distance in range(1, reach + 1):
         lowest = (reach - distance) * rows
         back_keys, back_values = from_behind(
-            (grad_k[lowest : lowest + rows], grad_v[lowest : lowest + rows]), "ctx", -distance
+            (
+                grad_k[lowest : lowest + rows].astype(jnp.bfloat16),
+                grad_v[lowest : lowest + rows].astype(jnp.bfloat16),
+            ),
+            "ctx",
+            -distance,
         )
-        own_keys = own_keys + back_keys
-        own_values = own_values + back_values
+        own_keys = own_keys + back_keys.astype(jnp.float32)
+        own_values = own_values + back_values.astype(jnp.float32)
     dquery = (
         (
             inverse_rotary(grad_q.reshape(rows, local_heads, head_size), cosine_table, sine_table)
@@ -184,10 +194,10 @@
     in_grad = sum_over_heads(partial_in.astype(jnp.bfloat16))
     grad_qkv_part = jnp.einsum("nd,nc->dc", hidden_in, grads_qkv, preferred_element_type=jnp.float32)
     grad_out_w = lax.psum_scatter(
-        grad_w_out.astype(jnp.bfloat16), "ctx", scatter_dimension=0, tiled=True
+        row_major(grad_w_out.astype(jnp.bfloat16)), "ctx", scatter_dimension=0, tiled=True
     ).astype(jnp.float32)
     grad_qkv = lax.psum_scatter(
-        grad_qkv_part.astype(jnp.bfloat16), "ctx", scatter_dimension=0, tiled=True
+        row_major(grad_qkv_part.astype(jnp.bfloat16)), "ctx", scatter_dimension=0, tiled=True
     ).astype(jnp.float32)
     grad_query = grad_qkv[:, :query_cols]
     grad_key = grad_qkv[:, query_cols : query_cols + key_value_columns]

time: 655 us -> 569 us (0.87)
  local copies, waits for them, and re-layouts: 99.2 us -> 42.3 us
  waiting for transfers between devices: 342 us -> 306 us
    unnamed x56 -> x30, local copies, waits for them, and re-layouts: 63.2 us -> 6.76 us
    ppermute x8, waiting for transfers between devices: 65.1 us -> 29.1 us  [from_behind(): lax.ppermute(value, axis, [(source, source + steps) for source in range(i...]
  transfers between devices with their start and end apart: 15 -> 15, of which waited for: 8 -> 7; matrix products, arithmetic and copies ran while one was open for 33% -> 33% of each run, Pallas kernels for 0% -> 0%
where the time goes in v6:
time: 569 us; the launch traced here: 562 us
  waiting for transfers between devices  306 us (54%)
  matrix products  136 us (24%)
  local copies, waits for them, and re-layouts  42.3 us (7%)
  other arithmetic  37.1 us (7%)
  starting transfers between devices  25.9 us (5%)
  between operations  14.8 us (3%)
    ppermute x3, waiting for transfers between devices, sum_over_heads(): lax.ppermute(outgoing, 'head', [(source, (source + shift) % count) for so...  118 us
    all_gather x1, waiting for transfers between devices, shards(): lax.all_gather(jnp.concatenate([w_query, key_weight, value_weight], axis=...  110 us
    all_gather x1, waiting for transfers between devices, shards(): full_out = lax.all_gather(w_out, 'ctx', axis=0, tiled=True)  47.8 us
    ppermute x8, waiting for transfers between devices, from_behind(): lax.ppermute(value, axis, [(source, source + steps) for source in range(i...  29.1 us
    ppermute x8, starting transfers between devices, from_behind(): lax.ppermute(value, axis, [(source, source + steps) for source in range(i...  21.9 us
    dot_general x1, matrix products, shards(): jnp.einsum('nd,nc->dc', hidden_in, grads_qkv, preferred_element_type=jnp....  20.5 us
    dot_general x1, matrix products, dot_rows(): lax.dot_general(left, weight, (((1,), (1,)), ((), ())), preferred_element...  18.3 us
    dot_general x1, matrix products, attend_backward(): jnp.einsum('ngrd,mgd->grnm', gradient_list, value_rows, preferred_element...  17 us
  transfers between devices with their start and end apart: 15, of which 7 were waited for; matrix products, arithmetic and copies ran while one was open for 33% of the time, Pallas kernels for 0%

profile of v6, /device:TPU:3, one launch (start us, length us, event | category | flops | bytes accessed | tf_op | source)
XLA Modules:
  0.0 562.1 jit_solution(6518865746292911155)
XLA Ops:
  7.2 3.6 pad_maximum_fusion
  12.6 1.9 and_and_fusion
  14.4 110.1 %all-gather.3.cloned.1.call-done = bf16[5376,2048]{1,0:T(8,128)(2,1)} async-done(((bf16[672,2048]{1,0:T(8,128)(2,1)}), bf16[5376,2048]{1,0:T(8,128)(2,1)}) %all-gather.3.cloned.1.call-update) | async-done | bytes 22020112 | tf_op jit(solution)/shard_map/all_gather | solution.py:112
  124.6 16.6 %convolution_bitcast_fusion.2 = f32[512,2048]{0,1:T(8,128)S(1)} fusion(bf16[5376,2048]{1,0:T(8,128)(2,1)} %all-gather.3.cloned.1.call-done, bf16[512,5376]{1,0:T(8,128)(2,1)} %param.6), kind=kOutput, calls=%fused_computation.18 | convolution fusion | flops 11274289152 | bytes 31719424 | tf_op jit(solution)/shard_map/dot_general | solution.py:116
  141.2 2.0 copy-done.2
  145.7 2.3 collective-permute-start.1
  147.9 3.2 collective-permute-start
  151.1 47.8 %all-gather.5.cloned.1.call-done = bf16[5376,1024]{1,0:T(8,128)(2,1)} async-done(((bf16[672,1024]{1,0:T(8,128)(2,1)}), bf16[5376,1024]{1,0:T(8,128)(2,1)}) %all-gather.5.cloned.1.call-update) | async-done | bytes 11010064 | tf_op jit(solution)/shard_map/all_gather | solution.py:115
  199.0 10.2 %convolution_convert_fusion.3 = bf16[512,1024]{1,0:T(8,128)(2,1)S(1)} fusion(bf16[512,5376]{1,0:T(8,128)(2,1)} %param.7, bf16[5376,1024]{1,0:T(8,128)(2,1)} %all-gather.5.cloned.1.call-done), kind=kOutput, calls=%fused_computation.34 | convolution fusion | flops 5637668864 | bytes 17563648 | tf_op jit(solution)/shard_map/dot_general | solution.py:120
  209.7 2.3 slice.126
  212.0 4.8 collective-permute-start.3
  216.8 2.1 collective-permute-start.2
  219.0 1.6 multiply_subtract_fusion.1
  220.6 1.8 copy.61
  222.4 3.2 copy.62
  225.6 3.2 fusion.14
  228.8 1.3 copy.60
  230.1 1.3 copy.59
  231.4 14.5 %fusion.35 = (f32[4,2,512]{2,1,0:T(2,128)S(1)}, f32[4,2,512,1536]{2,3,1,0:T(8,128)}) fusion(pred[512,1536]{0,1:T(8,128)(4,1)} %and_and_fusion, bf16[512,4,2,128]{3,0,2,1:T(8,128)(2,1)} %fusion.14, bf16[512,4,128]{2,0,1:T(8,128)(2,1)} %copy-done.3, bf16[512,4,128]{2,0,1:T(8,128)(2,1)S(1)} %copy.60, bf16[512,4,128]{2,0,1:T(8,128)(2,1)S(1)} %copy.59), kind=kOutput, calls=%fused_computation.76 | convolution fusion | flops 1634207232 | bytes 28590080 | tf_op jit(solution)/shard_map/sub | solution.py:78
  245.9 10.2 %fusion.7 = bf16[4,2,512,1536]{2,3,1,0:T(8,128)(2,1)S(1)} fusion(f32[4,2,512,1536]{2,3,1,0:T(8,128)} %get-tuple-element.29, f32[4,2,512]{2,1,0:T(2,128)S(1)} %get-tuple-element.28), kind=kLoop, calls=%fused_computation.13 | loop fusion | flops 12582912 | bytes 37765120 | tf_op jit(solution)/shard_map/convert_element_type | solution.py:80
  256.2 2.8 pad_maximum_fusion.2
  259.0 2.5 multiply_reduce_fusion
  263.8 8.6 %fusion.8 = bf16[5376,1024]{1,0:T(8,128)(2,1)} fusion(bf16[512,1024]{0,1:T(8,128)(2,1)S(1)} %bitcast.128, bf16[512,5376]{1,0:T(8,128)(2,1)S(1)} %bitcast.135), kind=kOutput, calls=%fused_computation.14 | convolution fusion | flops 5642649600 | bytes 17563648 | tf_op jit(solution)/shard_map/nd,nc->dc/dot_general | solution.py:156
  272.7 17.0 %fusion.2 = bf16[4,2,512,1536]{2,3,1,0:T(8,128)(2,1)} fusion(bf16[1536,4,128,1]{0,2,3,1:T(8,128)(2,1)S(1)} %bitcast.123, bf16[512,4,2,128]{0,3,2,1:T(8,128)(2,1)S(1)} %bitcast.116, f32[4,2,512]{2,1,0:T(2,128)} %bitcast.133, f32[4,2,512,1536]{2,3,1,0:T(8,128)} %get-tuple-element.29, f32[4,2,512]{2,1,0:T(2,128)S(1)} %get-tuple-element.28), kind=kOutput, calls=%fused_computation.3 | convolution fusion | flops 1635778560 | bytes 40402944 | tf_op jit(solution)/shard_map/ngrd,mgd->grnm/dot_general | solution.py:90
  289.7 9.9 %fusion.37 = (bf16[1536,4,128]{0,2,1:T(8,128)(2,1)S(1)}, f32[1536,4,128]{0,2,1:T(8,128)S(1)}) fusion(bf16[512,4,2,128]{3,0,2,1:T(8,128)(2,1)} %fusion.14, bf16[4,2,512,1536]{2,3,1,0:T(8,128)(2,1)} %fusion.2), kind=kOutput, calls=%fused_computation.78 | convolution fusion | flops 1611399168 | bytes 18350080 | tf_op jit(solution)/shard_map/grnm,ngrd->mgd/dot_general | solution.py:95
  299.8 3.8 collective-permute-start.5
  303.6 1.9 collective-permute-start.4
  305.5 6.9 %fusion.20 = f32[4,128,2,512]{3,1,2,0:T(8,128)S(1)} fusion(bf16[4,2,512,1536]{2,3,1,0:T(8,128)(2,1)} %fusion.2, bf16[512,4,128]{2,0,1:T(8,128)(2,1)S(1)} %copy-done.4, bf16[512,4,128]{2,0,1:T(8,128)(2,1)S(1)} %copy.60, bf16[512,4,128]{2,0,1:T(8,128)(2,1)S(1)} %copy-done.9), kind=kOutput, calls=%fused_computation.58 | convolution fusion | flops 1615331328 | bytes 16252928 | tf_op jit(solution)/shard_map/grnm,mgd->ngrd/dot_general | solution.py:94
  312.4 10.7 %fusion.36 = (bf16[1536,4,128]{0,2,1:T(8,128)(2,1)S(1)}, f32[1536,4,128]{0,2,1:T(8,128)}) fusion(bf16[512,4,2,128]{0,3,2,1:T(8,128)(2,1)S(1)} %bitcast.117, bf16[4,2,512,1536]{2,3,1,0:T(8,128)(2,1)} %copy-done), kind=kOutput, calls=%fused_computation.77 | convolution fusion | flops 1611399168 | bytes 18350080 | tf_op jit(solution)/shard_map/grnm,ngrd->mgd/dot_general | solution.py:98
  324.2 1.9 collective-permute-start.7
  326.1 1.9 collective-permute-start.6
  331.1 19.4 %collective-permute-done.4 = bf16[512,512]{0,1:T(8,128)(2,1)} collective-permute-done((bf16[512,512]{0,1:T(8,128)(2,1)S(1)}, bf16[512,512]{0,1:T(8,128)(2,1)}, u32[]{:S(2)}, u32[]{:S(2)}) %collective-permute-start.4) | collective-permute-done | bytes 524320 | tf_op jit(solution)/shard_map/ppermute | solution.py:19
  350.5 1.3 fusion.18
  353.0 1.4 copy.94
  356.2 9.7 %collective-permute-done.6 = bf16[512,512]{0,1:T(8,128)(2,1)} collective-permute-done((bf16[512,512]{0,1:T(8,128)(2,1)}, bf16[512,512]{0,1:T(8,128)(2,1)}, u32[]{:S(2)}, u32[]{:S(2)}) %collective-permute-start.6) | collective-permute-done | bytes 524320 | tf_op jit(solution)/shard_map/ppermute | solution.py:19
  365.9 1.4 fusion.17
  367.3 20.5 %fusion.4 = bf16[5376,2048]{1,0:T(8,128)(2,1)} fusion(bf16[512,5376]{1,0:T(8,128)(2,1)} %param.6, bf16[512,512]{0,1:T(8,128)(2,1)S(1)} %fusion.17, bf16[512,512]{0,1:T(8,128)(2,1)S(1)} %bitcast.129, bf16[512,1024]{0,1:T(8,128)(2,1)S(1)} %bitcast.126), kind=kOutput, calls=%fused_computation.8 | convolution fusion | flops 11291590656 | bytes 29622272 | tf_op jit(solution)/shard_map/nd,nc->dc/dot_general | solution.py:195
  387.9 18.3 %convolution_convert_fusion.2 = bf16[512,5376]{1,0:T(8,128)(2,1)} fusion(bf16[5376,2048]{1,0:T(8,128)(2,1)} %all-gather.3.cloned.1.call-done, bf16[512,512]{0,1:T(8,128)(2,1)S(1)} %fusion.17, bf16[512,512]{0,1:T(8,128)(2,1)S(1)} %bitcast.130, bf16[512,1024]{0,1:T(8,128)(2,1)S(1)} %bitcast.127), kind=kOutput, calls=%fused_computation.15 | convolution fusion | flops 11283333120 | bytes 29622272 | tf_op jit(solution)/shard_map/dot_general | solution.py:69
  406.3 9.0 %copy.76 = bf16[512,5376]{0,1:T(8,128)(2,1)} copy(bf16[512,5376]{1,0:T(8,128)(2,1)} %convolution_convert_fusion.2) | data formatting | bytes 11010048 | tf_op jit(solution)/shard_map/convert_element_type | solution.py:194
  415.3 5.8 %dynamic-slice_bitcast_fusion.2 = (bf16[512,1344]{0,1:T(8,128)(2,1)}, bf16[512,1344]{0,1:T(8,128)(2,1)}, bf16[512,1344]{0,1:T(8,128)(2,1)}) fusion(bf16[512,4,1344]{0,2,1:T(8,128)(2,1)} %bitcast.114, s32[]{:T(128)S(6)} %select_n.35, s32[]{:T(128)S(6)} %select_n.39, s32[]{:T(128)S(6)} %select_n.37), kind=kLoop, calls=%fused_computation.38 | loop fusion | bytes 8257548 | tf_op jit(solution)/shard_map/jit(dynamic_index_in_dim)/squeeze | solution.py:57
  422.2 2.1 collective-permute-start.10
  424.6 30.4 %collective-permute-done.8 = bf16[512,1344]{0,1:T(8,128)(2,1)S(1)} collective-permute-done((bf16[512,1344]{0,1:T(8,128)(2,1)}, bf16[512,1344]{0,1:T(8,128)(2,1)S(1)}, u32[]{:S(2)}, u32[]{:S(2)}) %collective-permute-start.8) | collective-permute-done | bytes 1376288 | tf_op jit(solution)/shard_map/ppermute | solution.py:58
  455.0 28.8 %collective-permute-done.10 = bf16[512,1344]{0,1:T(8,128)(2,1)S(1)} collective-permute-done((bf16[512,1344]{0,1:T(8,128)(2,1)}, bf16[512,1344]{0,1:T(8,128)(2,1)S(1)}, u32[]{:S(2)}, u32[]{:S(2)}) %collective-permute-start.10) | collective-permute-done | bytes 1376288 | tf_op jit(solution)/shard_map/ppermute | solution.py:58
  483.8 59.2 %collective-permute-done.9 = bf16[512,1344]{0,1:T(8,128)(2,1)} collective-permute-done((bf16[512,1344]{0,1:T(8,128)(2,1)}, bf16[512,1344]{0,1:T(8,128)(2,1)}, u32[]{:S(2)}, u32[]{:S(2)}) %collective-permute-start.9) | collective-permute-done | bytes 1376288 | tf_op jit(solution)/shard_map/ppermute | solution.py:58
  543.1 3.6 fusion.13
  546.6 3.2 convert_element_type.158
  549.9 3.4 slice.114
  553.2 1.9 fusion.30
  (73 shorter events, 15.9 us)
Async XLA Ops:
  7.2 117.4 %all-gather.3.cloned.1.call-start = ((), (), s32[]{:S(2)}) async-start(), calls=%async_computation.2 | async-start | bytes 24772608 | tf_op jit(solution)/shard_map/all_gather | solution.py:112
  10.9 188.1 %all-gather.5.cloned.1.call-start = ((), (), s32[]{:S(2)}) async-start(), calls=%async_computation.3 | async-start | bytes 12386304 | tf_op jit(solution)/shard_map/all_gather | solution.py:115
  11.6 535.0 %reduce-scatter.5.cloned.1.call-start = ((), (), s32[]{:S(2)}) async-start(), calls=%async_computation.5 | async-start | bytes 12386304 | tf_op jit(solution)/shard_map/reduce_scatter | solution.py:196
  12.2 206.7 %copy-start.6 = (f32[512,64]{0,1:T(8,128)}, f32[512,64]{0,1:T(8,128)S(1)}, u32[]{:S(2)}) copy-start(f32[512,64]{0,1:T(8,128)S(1)} %get-tuple-element.27) | copy-start | bytes 393220
  12.5 131.5 %copy-start.5 = (f32[512,64]{1,0:T(8,128)}, f32[512,64]{1,0:T(8,128)S(1)}, u32[]{:S(2)}) copy-start(f32[512,64]{1,0:T(8,128)S(1)} %copy.57) | copy-start | bytes 393220
  141.1 2.0 copy-start.2
  144.6 54.3 %copy-start.3 = (bf16[512,4,128]{2,0,1:T(8,128)(2,1)}, bf16[512,4,128]{2,0,1:T(8,128)(2,1)S(1)}, u32[]{:S(2)}) copy-start(bf16[512,4,128]{2,0,1:T(8,128)(2,1)S(1)} %maximum_convert_fusion) | copy-start | bytes 1572868
  145.7 83.1 %collective-permute-start.1 = (bf16[512,512]{0,1:T(8,128)(2,1)}, bf16[512,512]{0,1:T(8,128)(2,1)}, u32[]{:S(2)}, u32[]{:S(2)}) collective-permute-start(bf16[512,512]{0,1:T(8,128)(2,1)} %bitcast.2), channel_id=1, source_target_pairs={{0,4},{4,8},{8,12},{12,16},{16,20},{20,24},{24,28},{1,5},{5,9},{9,... | collective-permute-start | bytes 1572872 | tf_op jit(solution)/shard_map/ppermute | solution.py:19
  147.9 82.1 %collective-permute-start = (bf16[512,512]{0,1:T(8,128)(2,1)}, bf16[512,512]{0,1:T(8,128)(2,1)}, u32[]{:S(2)}, u32[]{:S(2)}) collective-permute-start(bf16[512,512]{0,1:T(8,128)(2,1)} %bitcast.2), channel_id=1, source_target_pairs={{0,8},{4,12},{8,16},{12,20},{16,24},{20,28},{1,9},{5,13},{9,17},{1... | collective-permute-start | bytes 1572872 | tf_op jit(solution)/shard_map/ppermute | solution.py:19
  209.7 9.2 %slice-start = ((f32[512,2048]{0,1:T(8,128)}), f32[512,1024]{0,1:T(8,128)S(1)}, s32[]{:S(2)}) async-start(f32[512,2048]{0,1:T(8,128)} %copy-done.2), calls=%async_computation.6 | async-start | bytes 4194304 | tf_op jit(solution)/shard_map/slice | solution.py:117
  212.0 44.2 %collective-permute-start.3 = (bf16[512,512]{0,1:T(8,128)(2,1)}, bf16[512,512]{0,1:T(8,128)(2,1)}, u32[]{:S(2)}, u32[]{:S(2)}) collective-permute-start(bf16[512,512]{0,1:T(8,128)(2,1)} %slice.126), channel_id=1, source_target_pairs={{0,4},{4,8},{8,12},{12,16},{16,20},{20,24},{24,28},{1,5},{5,9},{9,... | collective-permute-start | bytes 1572872 | tf_op jit(solution)/shard_map/ppermute | solution.py:19
  216.8 39.4 %collective-permute-start.2 = (bf16[512,512]{0,1:T(8,128)(2,1)}, bf16[512,512]{0,1:T(8,128)(2,1)}, u32[]{:S(2)}, u32[]{:S(2)}) collective-permute-start(bf16[512,512]{0,1:T(8,128)(2,1)} %slice.126), channel_id=1, source_target_pairs={{0,8},{4,12},{8,16},{12,20},{16,24},{20,28},{1,9},{5,13},{9,17},{1... | collective-permute-start | bytes 1572872 | tf_op jit(solution)/shard_map/ppermute | solution.py:19
  231.4 14.5 %copy-start.8 = (bf16[512,4,128]{2,0,1:T(8,128)(2,1)}, bf16[512,4,128]{2,0,1:T(8,128)(2,1)S(1)}, u32[]{:S(2)}) copy-start(bf16[512,4,128]{2,0,1:T(8,128)(2,1)S(1)} %copy.59) | copy-start | bytes 1572868
  256.2 6.4 %copy-start = (bf16[4,2,512,1536]{2,3,1,0:T(8,128)(2,1)}, bf16[4,2,512,1536]{2,3,1,0:T(8,128)(2,1)S(1)}, u32[]{:S(2)}) copy-start(bf16[4,2,512,1536]{2,3,1,0:T(8,128)(2,1)S(1)} %fusion.7) | copy-start | bytes 37748740
  256.2 7.0 %slice-start.1 = ((s8[5505024]{0:T(1024)(128)(4,1)}), s8[4194304]{0:T(1024)(128)(4,1)S(1)}, s32[]{:S(2)}) async-start(s8[5505024]{0:T(1024)(128)(4,1)} %bitcast.134), calls=%async_computation.7 | async-start | bytes 8388608
  259.0 4.8 slice-start.2
  272.5 277.4 %reduce-scatter.3.cloned.1.call-start = ((), (), s32[]{:S(2)}) async-start(), calls=%async_computation.4 | async-start | bytes 24772608 | tf_op jit(solution)/shard_map/reduce_scatter | solution.py:199
  289.7 15.8 %copy-start.4 = (bf16[512,4,128]{2,0,1:T(8,128)(2,1)S(1)}, bf16[512,4,128]{2,0,1:T(8,128)(2,1)}, u32[]{:S(2)}) copy-start(bf16[512,4,128]{2,0,1:T(8,128)(2,1)} %copy-done.3) | copy-start | bytes 1572868
  289.7 15.8 %copy-start.9 = (bf16[512,4,128]{2,0,1:T(8,128)(2,1)S(1)}, bf16[512,4,128]{2,0,1:T(8,128)(2,1)}, u32[]{:S(2)}) copy-start(bf16[512,4,128]{2,0,1:T(8,128)(2,1)} %copy-done.8) | copy-start | bytes 1572868
  299.8 31.3 %collective-permute-start.5 = (bf16[512,512]{0,1:T(8,128)(2,1)S(1)}, bf16[512,512]{0,1:T(8,128)(2,1)S(1)}, u32[]{:S(2)}, u32[]{:S(2)}) collective-permute-start(bf16[512,512]{0,1:T(8,128)(2,1)S(1)} %bitcast.132), channel_id=1, source_target_pairs={{8,0},{12,4},{16,8},{20,12},{24,16},{28,20},{9,1},{13,5},{17,9},{2... | collective-permute-start | bytes 1572872 | tf_op jit(solution)/shard_map/ppermute | solution.py:19
  303.6 46.9 %collective-permute-start.4 = (bf16[512,512]{0,1:T(8,128)(2,1)S(1)}, bf16[512,512]{0,1:T(8,128)(2,1)}, u32[]{:S(2)}, u32[]{:S(2)}) collective-permute-start(bf16[512,512]{0,1:T(8,128)(2,1)S(1)} %bitcast.131), channel_id=1, source_target_pairs={{4,0},{8,4},{12,8},{16,12},{20,16},{24,20},{28,24},{5,1},{9,5},{13... | collective-permute-start | bytes 1572872 | tf_op jit(solution)/shard_map/ppermute | solution.py:19
  323.2 6.3 %copy-start.7 = (f32[512,64]{0,1:T(8,128)S(1)}, f32[512,64]{0,1:T(8,128)}, u32[]{:S(2)}) copy-start(f32[512,64]{0,1:T(8,128)} %copy-done.6) | copy-start | bytes 393220
  324.2 31.9 %collective-permute-start.7 = (bf16[512,512]{0,1:T(8,128)(2,1)}, bf16[512,512]{0,1:T(8,128)(2,1)}, u32[]{:S(2)}, u32[]{:S(2)}) collective-permute-start(bf16[512,512]{0,1:T(8,128)(2,1)} %bitcast.38), channel_id=1, source_target_pairs={{8,0},{12,4},{16,8},{20,12},{24,16},{28,20},{9,1},{13,5},{17,9},{2... | collective-permute-start | bytes 1572872 | tf_op jit(solution)/shard_map/ppermute | solution.py:19
  326.1 39.7 %collective-permute-start.6 = (bf16[512,512]{0,1:T(8,128)(2,1)}, bf16[512,512]{0,1:T(8,128)(2,1)}, u32[]{:S(2)}, u32[]{:S(2)}) collective-permute-start(bf16[512,512]{0,1:T(8,128)(2,1)} %bitcast.37), channel_id=1, source_target_pairs={{4,0},{8,4},{12,8},{16,12},{20,16},{24,20},{28,24},{5,1},{9,5},{13... | collective-permute-start | bytes 1572872 | tf_op jit(solution)/shard_map/ppermute | solution.py:19
  355.6 11.7 %copy-start.10 = (bf16[512,8,128]{0,2,1:T(8,128)(2,1)S(1)}, bf16[512,8,128]{0,2,1:T(8,128)(2,1)}, u32[]{:S(2)}) copy-start(bf16[512,8,128]{0,2,1:T(8,128)(2,1)} %fusion.15) | copy-start | bytes 3145732
  421.0 34.0 %collective-permute-start.8 = (bf16[512,1344]{0,1:T(8,128)(2,1)}, bf16[512,1344]{0,1:T(8,128)(2,1)S(1)}, u32[]{:S(2)}, u32[]{:S(2)}) collective-permute-start(bf16[512,1344]{0,1:T(8,128)(2,1)} %get-tuple-element.5), channel_id=1, source_target_pairs={{0,1},{1,2},{2,3},{3,0},{4,5},{5,6},{6,7},{7,4},{8,9},{9,10},{10,1... | collective-permute-start | bytes 4128776 | tf_op jit(solution)/shard_map/ppermute | solution.py:58
  422.2 61.6 %collective-permute-start.10 = (bf16[512,1344]{0,1:T(8,128)(2,1)}, bf16[512,1344]{0,1:T(8,128)(2,1)S(1)}, u32[]{:S(2)}, u32[]{:S(2)}) collective-permute-start(bf16[512,1344]{0,1:T(8,128)(2,1)} %get-tuple-element.6), channel_id=1, source_target_pairs={{0,3},{1,0},{2,1},{3,2},{4,7},{5,4},{6,5},{7,6},{8,11},{9,8},{10,9... | collective-permute-start | bytes 4128776 | tf_op jit(solution)/shard_map/ppermute | solution.py:58
  424.3 118.8 %collective-permute-start.9 = (bf16[512,1344]{0,1:T(8,128)(2,1)}, bf16[512,1344]{0,1:T(8,128)(2,1)}, u32[]{:S(2)}, u32[]{:S(2)}) collective-permute-start(bf16[512,1344]{0,1:T(8,128)(2,1)} %get-tuple-element.7), channel_id=1, source_target_pairs={{0,2},{1,3},{2,0},{3,1},{4,6},{5,7},{6,4},{7,5},{8,10},{9,11},{10,... | collective-permute-start | bytes 4128776 | tf_op jit(solution)/shard_map/ppermute | solution.py:58
  549.8 3.4 copy-start.1
Sparse Core Ops, SparseCore 0:
  11.0 113.5 all-gather.2
  126.4 72.4 all-gather.4
  272.6 118.4 reduce-scatter.4
  394.6 141.0 reduce-scatter.2

commit v7 on v6

--- a/solution.py
+++ b/solution.py
@@ -109,10 +109,14 @@
     group_ratio = local_heads // local_groups
     reach = WINDOW // rows
     first = lax.axis_index("ctx") * rows
-    full_qkv = lax.all_gather(
-        jnp.concatenate([w_query, key_weight, value_weight], axis=1), "ctx", axis=0, tiled=True
-    )
-    full_out = lax.all_gather(w_out, "ctx", axis=0, tiled=True)
+    full_weights = lax.all_gather(
+        jnp.concatenate([w_query, key_weight, value_weight, w_out], axis=1),
+        "ctx",
+        axis=0,
+        tiled=True,
+    )
+    full_qkv = full_weights[:, : query_cols + 2 * key_value_columns]
+    full_out = full_weights[:, query_cols + 2 * key_value_columns :]
     projected = jnp.dot(hidden_in, full_qkv, preferred_element_type=jnp.float32)
     query = projected[:, :query_cols]
     key_projected = projected[:, query_cols : query_cols + key_value_columns]

time: 569 us -> 570 us (level)
    all_gather x2 -> x1, waiting for transfers between devices: 158 us -> 157 us  [shards(): lax.all_gather(jnp.concatenate([w_query, key_weight, value_weight, w_out]...]
  transfers between devices with their start and end apart: 15 -> 14, of which waited for: 7 -> 8; matrix products, arithmetic and copies ran while one was open for 33% -> 30% of each run, Pallas kernels for 0% -> 0%
where the time goes in v7:
time: 570 us; the launch traced here: 562 us
  waiting for transfers between devices  308 us (54%)
  matrix products  139 us (24%)
  local copies, waits for them, and re-layouts  41.1 us (7%)
  other arithmetic  37.4 us (7%)
  starting transfers between devices  22.5 us (4%)
  between operations  14.4 us (3%)
    all_gather x1, waiting for transfers between devices, shards(): lax.all_gather(jnp.concatenate([w_query, key_weight, value_weight, w_out]...  157 us
    ppermute x3, waiting for transfers between devices, sum_over_heads(): lax.ppermute(outgoing, 'head', [(source, (source + shift) % count) for so...  118 us
    ppermute x8, waiting for transfers between devices, from_behind(): lax.ppermute(value, axis, [(source, source + steps) for source in range(i...  31.9 us
    dot_general x1, matrix products, shards(): jnp.einsum('nd,nc->dc', hidden_in, grads_qkv, preferred_element_type=jnp....  20.4 us
    dot_general x1, matrix products, shards(): projected = jnp.dot(hidden_in, full_qkv, preferred_element_type=jnp.float32)  18.9 us
    ppermute x8, starting transfers between devices, from_behind(): lax.ppermute(value, axis, [(source, source + steps) for source in range(i...  18.8 us
    dot_general x1, matrix products, dot_rows(): lax.dot_general(left, weight, (((1,), (1,)), ((), ())), preferred_element...  18.3 us
    dot_general x1, matrix products, attend_backward(): jnp.einsum('ngrd,mgd->grnm', gradient_list, value_rows, preferred_element...  17.8 us
  transfers between devices with their start and end apart: 14, of which 8 were waited for; matrix products, arithmetic and copies ran while one was open for 30% of the time, Pallas kernels for 0%

profile of v7, /device:TPU:3, one launch (start us, length us, event | category | flops | bytes accessed | tf_op | source)
XLA Modules:
  0.0 561.6 jit_solution(3831375151939234530)
XLA Ops:
  7.2 3.7 pad_maximum_fusion
  11.9 1.9 and_and_fusion
  13.8 157.4 %all-gather.2.cloned.1.call-done = bf16[5376,3072]{1,0:T(8,128)(2,1)} async-done(((bf16[672,3072]{1,0:T(8,128)(2,1)}), bf16[5376,3072]{1,0:T(8,128)(2,1)}) %all-gather.2.cloned.1.call-update) | async-done | bytes 33030160 | tf_op jit(solution)/shard_map/all_gather | solution.py:112
  171.2 18.9 %fusion.18 = f32[512,2048]{0,1:T(8,128)} fusion(bf16[512,5376]{1,0:T(8,128)(2,1)} %param.6, bf16[5376,3072]{1,0:T(8,128)(2,1)} %all-gather.2.cloned.1.call-done), kind=kOutput, calls=%fused_computation.25 | convolution fusion | flops 11274289152 | bytes 31719424 | tf_op jit(solution)/shard_map/dot_general | solution.py:120
  190.1 2.2 slice.148
  192.2 2.1 collective-permute-start.3
  194.4 3.3 collective-permute-start.2
  200.0 2.4 collective-permute-start.1
  202.5 2.1 collective-permute-start
  204.6 11.9 %fusion.28 = bf16[1024,512]{1,0:T(8,128)(2,1)} fusion(bf16[512,5376]{1,0:T(8,128)(2,1)} %param.7, bf16[5376,3072]{1,0:T(8,128)(2,1)} %all-gather.2.cloned.1.call-done), kind=kOutput, calls=%fused_computation.40 | convolution fusion | flops 5637668864 | bytes 17563648 | tf_op jit(solution)/shard_map/dot_general | solution.py:124
  216.5 1.6 slice-done.1
  218.1 1.6 multiply_subtract_fusion.1
  219.8 1.8 copy.57
  221.6 3.2 copy.58
  224.7 3.2 fusion.26
  227.9 1.3 copy.56
  229.2 1.5 collective-permute-done
  230.7 1.3 copy.55
  232.0 14.2 %fusion.50 = (f32[4,2,512]{2,1,0:T(2,128)S(1)}, f32[4,2,512,1536]{2,3,1,0:T(8,128)}) fusion(pred[512,1536]{0,1:T(8,128)(4,1)} %and_and_fusion, bf16[512,4,2,128]{3,0,2,1:T(8,128)(2,1)} %fusion.26, bf16[512,4,128]{2,0,1:T(8,128)(2,1)S(1)} %maximum_convert_fusion, bf16[512,4,128]{2,0,1:T(8,128)(2,1)S(1)} %copy.56, bf16[512,4,128]{2,0,1:T(8,128)(2,1)S(1)} %copy.55), kind=kOutput, calls=%fused_computation.82 | convolution fusion | flops 1634207232 | bytes 28590080 | tf_op jit(solution)/shard_map/sub | solution.py:78
  246.3 10.2 %fusion.13 = bf16[4,2,512,1536]{2,3,1,0:T(8,128)(2,1)S(1)} fusion(f32[4,2,512,1536]{2,3,1,0:T(8,128)} %get-tuple-element.29, f32[4,2,512]{2,1,0:T(2,128)S(1)} %get-tuple-element.28), kind=kLoop, calls=%fused_computation.19 | loop fusion | flops 12582912 | bytes 37765120 | tf_op jit(solution)/shard_map/convert_element_type | solution.py:80
  256.5 2.8 pad_maximum_fusion.2
  260.2 2.4 multiply_reduce_fusion
  264.4 9.0 %fusion.14 = bf16[5376,1024]{1,0:T(8,128)(2,1)} fusion(bf16[512,1024]{0,1:T(8,128)(2,1)S(1)} %bitcast.127, bf16[512,5376]{1,0:T(8,128)(2,1)S(1)} %bitcast.132), kind=kOutput, calls=%fused_computation.20 | convolution fusion | flops 5642649600 | bytes 17563648 | tf_op jit(solution)/shard_map/nd,nc->dc/dot_general | solution.py:160
  273.5 17.8 %fusion.2 = bf16[4,2,512,1536]{2,3,1,0:T(8,128)(2,1)} fusion(bf16[1536,4,128,1]{0,2,3,1:T(8,128)(2,1)S(1)} %bitcast.121, bf16[512,4,2,128]{0,3,2,1:T(8,128)(2,1)} %bitcast.122, f32[4,2,512]{2,1,0:T(2,128)} %bitcast.130, f32[4,2,512,1536]{2,3,1,0:T(8,128)} %get-tuple-element.29, f32[4,2,512]{2,1,0:T(2,128)S(1)} %get-tuple-element.28), kind=kOutput, calls=%fused_computation.3 | convolution fusion | flops 1635778560 | bytes 40402944 | tf_op jit(solution)/shard_map/ngrd,mgd->grnm/dot_general | solution.py:90
  291.3 9.4 %fusion.52 = (bf16[1536,4,128]{0,2,1:T(8,128)(2,1)S(1)}, f32[1536,4,128]{0,2,1:T(8,128)S(1)}) fusion(bf16[512,4,2,128]{3,0,2,1:T(8,128)(2,1)} %fusion.26, bf16[4,2,512,1536]{2,3,1,0:T(8,128)(2,1)} %fusion.2), kind=kOutput, calls=%fused_computation.84 | convolution fusion | flops 1611399168 | bytes 18350080 | tf_op jit(solution)/shard_map/grnm,ngrd->mgd/dot_general | solution.py:95
  301.8 2.4 collective-permute-start.5
  304.3 2.4 collective-permute-start.4
  306.7 6.9 %fusion.35 = f32[4,128,2,512]{3,1,2,0:T(8,128)S(1)} fusion(bf16[4,2,512,1536]{2,3,1,0:T(8,128)(2,1)} %fusion.2, bf16[512,4,128]{2,0,1:T(8,128)(2,1)S(1)} %maximum_convert_fusion, bf16[512,4,128]{2,0,1:T(8,128)(2,1)S(1)} %copy.56, bf16[512,4,128]{2,0,1:T(8,128)(2,1)S(1)} %copy.55), kind=kOutput, calls=%fused_computation.64 | convolution fusion | flops 1615331328 | bytes 16252928 | tf_op jit(solution)/shard_map/grnm,mgd->ngrd/dot_general | solution.py:94
  313.5 9.2 %fusion.51 = (bf16[1536,4,128]{0,2,1:T(8,128)(2,1)S(1)}, f32[1536,4,128]{0,2,1:T(8,128)S(1)}) fusion(bf16[512,4,2,128]{0,3,2,1:T(8,128)(2,1)} %bitcast.123, bf16[4,2,512,1536]{2,3,1,0:T(8,128)(2,1)} %copy-done), kind=kOutput, calls=%fused_computation.83 | convolution fusion | flops 1611399168 | bytes 18350080 | tf_op jit(solution)/shard_map/grnm,ngrd->mgd/dot_general | solution.py:98
  323.9 1.9 collective-permute-start.7
  325.8 2.1 collective-permute-start.6
  329.8 21.8 %collective-permute-done.4 = bf16[512,512]{0,1:T(8,128)(2,1)} collective-permute-done((bf16[512,512]{0,1:T(8,128)(2,1)}, bf16[512,512]{0,1:T(8,128)(2,1)}, u32[]{:S(2)}, u32[]{:S(2)}) %collective-permute-start.4) | collective-permute-done | bytes 524320 | tf_op jit(solution)/shard_map/ppermute | solution.py:19
  351.6 1.4 fusion.33
  354.2 1.4 copy.89
  357.4 8.4 %collective-permute-done.6 = bf16[512,512]{0,1:T(8,128)(2,1)} collective-permute-done((bf16[512,512]{0,1:T(8,128)(2,1)}, bf16[512,512]{0,1:T(8,128)(2,1)}, u32[]{:S(2)}, u32[]{:S(2)}) %collective-permute-start.6) | collective-permute-done | bytes 524320 | tf_op jit(solution)/shard_map/ppermute | solution.py:19
  365.8 1.4 fusion.32
  367.3 20.4 %fusion.4 = bf16[5376,2048]{1,0:T(8,128)(2,1)} fusion(bf16[512,5376]{1,0:T(8,128)(2,1)} %param.6, bf16[512,512]{0,1:T(8,128)(2,1)S(1)} %fusion.32, bf16[512,512]{0,1:T(8,128)(2,1)S(1)} %bitcast.128, bf16[512,1024]{0,1:T(8,128)(2,1)S(1)} %bitcast.125), kind=kOutput, calls=%fused_computation.8 | convolution fusion | flops 11291590656 | bytes 29622272 | tf_op jit(solution)/shard_map/nd,nc->dc/dot_general | solution.py:199
  387.8 18.3 %fusion.15 = bf16[512,5376]{1,0:T(8,128)(2,1)} fusion(bf16[5376,3072]{1,0:T(8,128)(2,1)} %all-gather.2.cloned.1.call-done, bf16[512,512]{0,1:T(8,128)(2,1)S(1)} %fusion.32, bf16[512,512]{0,1:T(8,128)(2,1)S(1)} %bitcast.129, bf16[512,1024]{0,1:T(8,128)(2,1)S(1)} %bitcast.126), kind=kOutput, calls=%fused_computation.21 | convolution fusion | flops 11283333120 | bytes 29622272 | tf_op jit(solution)/shard_map/dot_general | solution.py:69
  406.1 9.0 %copy.70 = bf16[512,5376]{0,1:T(8,128)(2,1)} copy(bf16[512,5376]{1,0:T(8,128)(2,1)} %fusion.15) | data formatting | bytes 11010048 | tf_op jit(solution)/shard_map/convert_element_type | solution.py:198
  415.2 5.7 %dynamic-slice_bitcast_fusion.2 = (bf16[512,1344]{0,1:T(8,128)(2,1)}, bf16[512,1344]{0,1:T(8,128)(2,1)}, bf16[512,1344]{0,1:T(8,128)(2,1)}) fusion(bf16[512,4,1344]{0,2,1:T(8,128)(2,1)} %bitcast.113, s32[]{:T(128)S(6)} %select_n.35, s32[]{:T(128)S(6)} %select_n.39, s32[]{:T(128)S(6)} %select_n.37), kind=kLoop, calls=%fused_computation.44 | loop fusion | bytes 8257548 | tf_op jit(solution)/shard_map/jit(dynamic_index_in_dim)/squeeze | solution.py:57
  422.1 2.1 collective-permute-start.10
  424.5 30.4 %collective-permute-done.8 = bf16[512,1344]{0,1:T(8,128)(2,1)S(1)} collective-permute-done((bf16[512,1344]{0,1:T(8,128)(2,1)}, bf16[512,1344]{0,1:T(8,128)(2,1)S(1)}, u32[]{:S(2)}, u32[]{:S(2)}) %collective-permute-start.8) | collective-permute-done | bytes 1376288 | tf_op jit(solution)/shard_map/ppermute | solution.py:58
  454.8 28.7 %collective-permute-done.10 = bf16[512,1344]{0,1:T(8,128)(2,1)S(1)} collective-permute-done((bf16[512,1344]{0,1:T(8,128)(2,1)}, bf16[512,1344]{0,1:T(8,128)(2,1)S(1)}, u32[]{:S(2)}, u32[]{:S(2)}) %collective-permute-start.10) | collective-permute-done | bytes 1376288 | tf_op jit(solution)/shard_map/ppermute | solution.py:58
  483.6 59.2 %collective-permute-done.9 = bf16[512,1344]{0,1:T(8,128)(2,1)} collective-permute-done((bf16[512,1344]{0,1:T(8,128)(2,1)}, bf16[512,1344]{0,1:T(8,128)(2,1)}, u32[]{:S(2)}, u32[]{:S(2)}) %collective-permute-start.9) | collective-permute-done | bytes 1376288 | tf_op jit(solution)/shard_map/ppermute | solution.py:58
  542.8 3.6 fusion.25
  546.3 3.2 convert_element_type.162
  549.6 3.4 slice.124
  552.9 1.9 fusion.45
  (64 shorter events, 14.5 us)
Async XLA Ops:
  7.2 164.0 %all-gather.2.cloned.1.call-start = ((), (), s32[]{:S(2)}) async-start(), calls=%async_computation.2 | async-start | bytes 37158912 | tf_op jit(solution)/shard_map/all_gather | solution.py:112
  10.9 535.4 %reduce-scatter.5.cloned.1.call-start = ((), (), s32[]{:S(2)}) async-start(), calls=%async_computation.4 | async-start | bytes 12386304 | tf_op jit(solution)/shard_map/reduce_scatter | solution.py:200
  11.6 178.5 %copy-start.4 = (f32[512,64]{0,1:T(8,128)}, f32[512,64]{0,1:T(8,128)S(1)}, u32[]{:S(2)}) copy-start(f32[512,64]{0,1:T(8,128)S(1)} %get-tuple-element.27) | copy-start | bytes 393220
  11.8 186.6 %copy-start.3 = (f32[512,64]{1,0:T(8,128)}, f32[512,64]{1,0:T(8,128)S(1)}, u32[]{:S(2)}) copy-start(f32[512,64]{1,0:T(8,128)S(1)} %copy.53) | copy-start | bytes 393220
  190.1 7.6 %slice-start = ((f32[512,2048]{0,1:T(8,128)}), f32[512,512]{0,1:T(8,128)S(1)}, s32[]{:S(2)}) async-start(f32[512,2048]{0,1:T(8,128)} %fusion.18), calls=%async_computation.5 | async-start | bytes 2097152 | tf_op jit(solution)/shard_map/slice | solution.py:122
  192.2 64.3 %collective-permute-start.3 = (bf16[512,512]{0,1:T(8,128)(2,1)}, bf16[512,512]{0,1:T(8,128)(2,1)}, u32[]{:S(2)}, u32[]{:S(2)}) collective-permute-start(bf16[512,512]{0,1:T(8,128)(2,1)} %slice.148), channel_id=1, source_target_pairs={{0,4},{4,8},{8,12},{12,16},{16,20},{20,24},{24,28},{1,5},{5,9},{9,... | collective-permute-start | bytes 1572872 | tf_op jit(solution)/shard_map/ppermute | solution.py:19
  194.4 62.2 %collective-permute-start.2 = (bf16[512,512]{0,1:T(8,128)(2,1)}, bf16[512,512]{0,1:T(8,128)(2,1)}, u32[]{:S(2)}, u32[]{:S(2)}) collective-permute-start(bf16[512,512]{0,1:T(8,128)(2,1)} %slice.148), channel_id=1, source_target_pairs={{0,8},{4,12},{8,16},{12,20},{16,24},{20,28},{1,9},{5,13},{9,17},{1... | collective-permute-start | bytes 1572872 | tf_op jit(solution)/shard_map/ppermute | solution.py:19
  200.0 27.9 %collective-permute-start.1 = (bf16[512,512]{0,1:T(8,128)(2,1)}, bf16[512,512]{0,1:T(8,128)(2,1)}, u32[]{:S(2)}, u32[]{:S(2)}) collective-permute-start(bf16[512,512]{0,1:T(8,128)(2,1)} %bitcast.2), channel_id=1, source_target_pairs={{0,4},{4,8},{8,12},{12,16},{16,20},{20,24},{24,28},{1,5},{5,9},{9,... | collective-permute-start | bytes 1572872 | tf_op jit(solution)/shard_map/ppermute | solution.py:19
  202.5 28.2 %collective-permute-start = (bf16[512,512]{0,1:T(8,128)(2,1)}, bf16[512,512]{0,1:T(8,128)(2,1)}, u32[]{:S(2)}, u32[]{:S(2)}) collective-permute-start(bf16[512,512]{0,1:T(8,128)(2,1)} %bitcast.2), channel_id=1, source_target_pairs={{0,8},{4,12},{8,16},{12,20},{16,24},{20,28},{1,9},{5,13},{9,17},{1... | collective-permute-start | bytes 1572872 | tf_op jit(solution)/shard_map/ppermute | solution.py:19
  216.5 1.6 slice-start.1
  216.5 1.6 copy-start.5
  256.5 6.4 %copy-start = (bf16[4,2,512,1536]{2,3,1,0:T(8,128)(2,1)}, bf16[4,2,512,1536]{2,3,1,0:T(8,128)(2,1)S(1)}, u32[]{:S(2)}) copy-start(bf16[4,2,512,1536]{2,3,1,0:T(8,128)(2,1)S(1)} %fusion.13) | copy-start | bytes 37748740
  256.5 3.7 copy-start.2
  256.5 7.5 %slice-start.2 = ((s8[5505024]{0:T(1024)(128)(4,1)}), s8[4194304]{0:T(1024)(128)(4,1)S(1)}, s32[]{:S(2)}) async-start(s8[5505024]{0:T(1024)(128)(4,1)} %bitcast.131), calls=%async_computation.7 | async-start | bytes 8388608
  260.2 4.2 slice-start.3
  273.5 276.1 %reduce-scatter.3.cloned.1.call-start = ((), (), s32[]{:S(2)}) async-start(), calls=%async_computation.3 | async-start | bytes 24772608 | tf_op jit(solution)/shard_map/reduce_scatter | solution.py:203
  301.8 28.0 %collective-permute-start.5 = (bf16[512,512]{0,1:T(8,128)(2,1)}, bf16[512,512]{0,1:T(8,128)(2,1)}, u32[]{:S(2)}, u32[]{:S(2)}) collective-permute-start(bf16[512,512]{0,1:T(8,128)(2,1)} %bitcast.32), channel_id=1, source_target_pairs={{8,0},{12,4},{16,8},{20,12},{24,16},{28,20},{9,1},{13,5},{17,9},{2... | collective-permute-start | bytes 1572872 | tf_op jit(solution)/shard_map/ppermute | solution.py:19
  304.3 47.3 %collective-permute-start.4 = (bf16[512,512]{0,1:T(8,128)(2,1)}, bf16[512,512]{0,1:T(8,128)(2,1)}, u32[]{:S(2)}, u32[]{:S(2)}) collective-permute-start(bf16[512,512]{0,1:T(8,128)(2,1)} %bitcast.31), channel_id=1, source_target_pairs={{4,0},{8,4},{12,8},{16,12},{20,16},{24,20},{28,24},{5,1},{9,5},{13... | collective-permute-start | bytes 1572872 | tf_op jit(solution)/shard_map/ppermute | solution.py:19
  322.8 5.3 copy-start.6
  323.9 33.5 %collective-permute-start.7 = (bf16[512,512]{0,1:T(8,128)(2,1)}, bf16[512,512]{0,1:T(8,128)(2,1)}, u32[]{:S(2)}, u32[]{:S(2)}) collective-permute-start(bf16[512,512]{0,1:T(8,128)(2,1)} %bitcast.41), channel_id=1, source_target_pairs={{8,0},{12,4},{16,8},{20,12},{24,16},{28,20},{9,1},{13,5},{17,9},{2... | collective-permute-start | bytes 1572872 | tf_op jit(solution)/shard_map/ppermute | solution.py:19
  325.8 40.1 %collective-permute-start.6 = (bf16[512,512]{0,1:T(8,128)(2,1)}, bf16[512,512]{0,1:T(8,128)(2,1)}, u32[]{:S(2)}, u32[]{:S(2)}) collective-permute-start(bf16[512,512]{0,1:T(8,128)(2,1)} %bitcast.40), channel_id=1, source_target_pairs={{4,0},{8,4},{12,8},{16,12},{20,16},{24,20},{28,24},{5,1},{9,5},{13... | collective-permute-start | bytes 1572872 | tf_op jit(solution)/shard_map/ppermute | solution.py:19
  356.9 10.4 %copy-start.7 = (bf16[512,8,128]{0,2,1:T(8,128)(2,1)S(1)}, bf16[512,8,128]{0,2,1:T(8,128)(2,1)}, u32[]{:S(2)}) copy-start(bf16[512,8,128]{0,2,1:T(8,128)(2,1)} %fusion.27) | copy-start | bytes 3145732
  420.9 34.0 %collective-permute-start.8 = (bf16[512,1344]{0,1:T(8,128)(2,1)}, bf16[512,1344]{0,1:T(8,128)(2,1)S(1)}, u32[]{:S(2)}, u32[]{:S(2)}) collective-permute-start(bf16[512,1344]{0,1:T(8,128)(2,1)} %get-tuple-element.5), channel_id=1, source_target_pairs={{0,1},{1,2},{2,3},{3,0},{4,5},{5,6},{6,7},{7,4},{8,9},{9,10},{10,1... | collective-permute-start | bytes 4128776 | tf_op jit(solution)/shard_map/ppermute | solution.py:58
  422.1 61.5 %collective-permute-start.10 = (bf16[512,1344]{0,1:T(8,128)(2,1)}, bf16[512,1344]{0,1:T(8,128)(2,1)S(1)}, u32[]{:S(2)}, u32[]{:S(2)}) collective-permute-start(bf16[512,1344]{0,1:T(8,128)(2,1)} %get-tuple-element.6), channel_id=1, source_target_pairs={{0,3},{1,0},{2,1},{3,2},{4,7},{5,4},{6,5},{7,6},{8,11},{9,8},{10,9... | collective-permute-start | bytes 4128776 | tf_op jit(solution)/shard_map/ppermute | solution.py:58
  424.1 118.6 %collective-permute-start.9 = (bf16[512,1344]{0,1:T(8,128)(2,1)}, bf16[512,1344]{0,1:T(8,128)(2,1)}, u32[]{:S(2)}, u32[]{:S(2)}) collective-permute-start(bf16[512,1344]{0,1:T(8,128)(2,1)} %get-tuple-element.7), channel_id=1, source_target_pairs={{0,2},{1,3},{2,0},{3,1},{4,6},{5,7},{6,4},{7,5},{8,10},{9,11},{10,... | collective-permute-start | bytes 4128776 | tf_op jit(solution)/shard_map/ppermute | solution.py:58
  549.6 3.4 copy-start.1
Sparse Core Ops, SparseCore 0:
  11.1 160.0 all-gather.1
  273.6 117.4 reduce-scatter.4
  394.8 141.0 reduce-scatter.2

commit v8 on v6

--- a/solution.py
+++ b/solution.py
@@ -117,7 +117,6 @@
     query = projected[:, :query_cols]
     key_projected = projected[:, query_cols : query_cols + key_value_columns]
     value_projected = projected[:, query_cols + key_value_columns :]
-    grad_att_f = jnp.dot(out_grad, full_out, preferred_element_type=jnp.float32)
     cosine_table, sine_table = rope_tables(first, rows, head_size)
     query_rows = (
         apply_rotary(query.reshape(rows, local_heads, head_size), cosine_table, sine_table)
@@ -129,7 +128,6 @@
         .reshape(rows, key_value_columns)
     )
     values_here = value_projected.astype(jnp.bfloat16)
-    attention_gradient = grad_att_f.astype(jnp.bfloat16)
     key_blocks = []
     value_blocks = []
     for distance in range(reach, 0, -1):
@@ -150,8 +148,12 @@
         & (key_pos[None, :] >= 0)
     )
     grouped_queries = query_rows.reshape(rows, local_groups, group_ratio, head_size)
+    prob, prob_b, attended = attend_forward(grouped_queries, keys_all, values_all, allowed)
+    attended, late_out_grad = lax.optimization_barrier((attended, out_grad))
+    attention_gradient = jnp.dot(
+        late_out_grad, full_out, preferred_element_type=jnp.float32
+    ).astype(jnp.bfloat16)
     grouped_grads = attention_gradient.reshape(rows, local_groups, group_ratio, head_size)
-    prob, prob_b, attended = attend_forward(grouped_queries, keys_all, values_all, allowed)
     attended_flat = attended.reshape(rows, query_cols)
     grad_w_out = jnp.einsum(
         "nd,nc->dc", out_grad, attended_flat, preferred_element_type=jnp.float32

time: 569 us -> 554 us (0.974)
  waiting for transfers between devices: 306 us -> 292 us
    all_gather x1, waiting for transfers between devices: 47.8 us -> 0.02 us  [shards(): full_out = lax.all_gather(w_out, 'ctx', axis=0, tiled=True)]
    ppermute x8, waiting for transfers between devices: 29.1 us -> 62.1 us  [from_behind(): lax.ppermute(value, axis, [(source, source + steps) for source in range(i...]
  transfers between devices with their start and end apart: 15 -> 15, of which waited for: 7 -> 8; matrix products, arithmetic and copies ran while one was open for 33% -> 38% of each run, Pallas kernels for 0% -> 0%
where the time goes in v8:
time: 554 us; the launch traced here: 547 us
  waiting for transfers between devices  292 us (53%)
  matrix products  137 us (25%)
  local copies, waits for them, and re-layouts  43.8 us (8%)
  other arithmetic  38.4 us (7%)
  starting transfers between devices  21.8 us (4%)
  between operations  14.4 us (3%)
    ppermute x3, waiting for transfers between devices, sum_over_heads(): lax.ppermute(outgoing, 'head', [(source, (source + shift) % count) for so...  117 us
    all_gather x1, waiting for transfers between devices, shards(): lax.all_gather(jnp.concatenate([w_query, key_weight, value_weight], axis=...  111 us
    ppermute x8, waiting for transfers between devices, from_behind(): lax.ppermute(value, axis, [(source, source + steps) for source in range(i...  62.1 us
    dot_general x1, matrix products, shards(): jnp.einsum('nd,nc->dc', hidden_in, grads_qkv, preferred_element_type=jnp....  20.5 us
    dot_general x1, matrix products, dot_rows(): lax.dot_general(left, weight, (((1,), (1,)), ((), ())), preferred_element...  18.3 us
    ppermute x8, starting transfers between devices, from_behind(): lax.ppermute(value, axis, [(source, source + steps) for source in range(i...  18 us
    dot_general x1, matrix products, shards(): projected = jnp.dot(hidden_in, full_qkv, preferred_element_type=jnp.float32)  16.6 us
    dot_general x1, matrix products, attend_backward(): jnp.einsum('ngrd,mgd->grnm', gradient_list, value_rows, preferred_element...  16.4 us
  transfers between devices with their start and end apart: 15, of which 8 were waited for; matrix products, arithmetic and copies ran while one was open for 38% of the time, Pallas kernels for 0%

profile of v8, /device:TPU:3, one launch (start us, length us, event | category | flops | bytes accessed | tf_op | source)
XLA Modules:
  0.0 547.0 jit_solution(14688433591843464405)
XLA Ops:
  7.2 3.6 pad_maximum_fusion
  13.2 111.4 %all-gather.3.cloned.1.call-done = bf16[5376,2048]{1,0:T(8,128)(2,1)} async-done(((bf16[672,2048]{1,0:T(8,128)(2,1)}), bf16[5376,2048]{1,0:T(8,128)(2,1)}) %all-gather.3.cloned.1.call-update) | async-done | bytes 22020112 | tf_op jit(solution)/shard_map/all_gather | solution.py:112
  124.6 16.6 %convolution_bitcast_fusion.2 = f32[512,2048]{0,1:T(8,128)S(1)} fusion(bf16[5376,2048]{1,0:T(8,128)(2,1)} %all-gather.3.cloned.1.call-done, bf16[512,5376]{1,0:T(8,128)(2,1)} %param.6), kind=kOutput, calls=%fused_computation.18 | convolution fusion | flops 11274289152 | bytes 31719424 | tf_op jit(solution)/shard_map/dot_general | solution.py:116
  142.1 2.3 collective-permute-start.3
  144.4 3.2 collective-permute-start.2
  150.0 2.4 collective-permute-start.1
  152.5 2.1 collective-permute-start
  154.6 1.9 and_and_fusion
  156.5 1.8 multiply_subtract_fusion.1
  158.3 1.8 copy.60
  160.1 3.2 copy.59
  163.4 3.6 fusion.14
  167.0 32.2 %collective-permute-done.1 = bf16[512,512]{0,1:T(8,128)(2,1)} collective-permute-done((bf16[512,512]{0,1:T(8,128)(2,1)}, bf16[512,512]{0,1:T(8,128)(2,1)}, u32[]{:S(2)}, u32[]{:S(2)}) %collective-permute-start.1) | collective-permute-done | bytes 524320 | tf_op jit(solution)/shard_map/ppermute | solution.py:19
  199.1 2.0 copy.58
  201.2 12.6 %collective-permute-done = bf16[512,512]{0,1:T(8,128)(2,1)} collective-permute-done((bf16[512,512]{0,1:T(8,128)(2,1)}, bf16[512,512]{0,1:T(8,128)(2,1)}, u32[]{:S(2)}, u32[]{:S(2)}) %collective-permute-start) | collective-permute-done | bytes 524320 | tf_op jit(solution)/shard_map/ppermute | solution.py:19
  213.8 2.0 copy.57
  215.9 1.5 pad_maximum_fusion.2
  217.3 14.3 %fusion.36 = (f32[4,2,512]{2,1,0:T(2,128)S(1)}, f32[4,2,512,1536]{2,3,1,0:T(8,128)}) fusion(pred[512,1536]{0,1:T(8,128)(4,1)} %and_and_fusion, bf16[512,4,2,128]{3,0,2,1:T(8,128)(2,1)S(1)} %copy-done.3, bf16[512,4,128]{2,0,1:T(8,128)(2,1)S(1)} %maximum_convert_fusion, bf16[512,4,128]{2,0,1:T(8,128)(2,1)} %copy.58, bf16[512,4,128]{2,0,1:T(8,128)(2,1)} %copy.57), kind=kOutput, calls=%fused_computation.77 | convolution fusion | flops 1634207232 | bytes 28590080 | tf_op jit(solution)/shard_map/sub | solution.py:78
  231.6 10.2 %fusion.7 = bf16[4,2,512,1536]{2,3,1,0:T(8,128)(2,1)S(1)} fusion(f32[4,2,512,1536]{2,3,1,0:T(8,128)} %get-tuple-element.33, f32[4,2,512]{2,1,0:T(2,128)S(1)} %get-tuple-element.32), kind=kLoop, calls=%fused_computation.13 | loop fusion | flops 12582912 | bytes 37765120 | tf_op jit(solution)/shard_map/convert_element_type | solution.py:80
  241.9 1.8 fusion.16
  243.7 2.7 copy-done
  247.4 11.3 %fusion.8 = bf16[5376,1024]{1,0:T(8,128)(2,1)} fusion(bf16[512,1024]{0,1:T(8,128)(2,1)S(1)} %bitcast.125, bf16[512,5376]{1,0:T(8,128)(2,1)} %param.7), kind=kOutput, calls=%fused_computation.14 | convolution fusion | flops 5642649600 | bytes 17563648 | tf_op jit(solution)/shard_map/nd,nc->dc/dot_general | solution.py:158
  258.8 11.0 %convolution_convert_fusion.3 = bf16[512,1024]{1,0:T(8,128)(2,1)} fusion(bf16[512,5376]{1,0:T(8,128)(2,1)} %param.7, bf16[5376,1024]{1,0:T(8,128)(2,1)} %all-gather.5.cloned.1.call-done), kind=kOutput, calls=%fused_computation.34 | convolution fusion | flops 5637668864 | bytes 17563648 | tf_op jit(solution)/shard_map/dot_general | solution.py:153
  269.8 1.7 copy.62
  271.6 2.4 multiply_reduce_fusion
  274.0 16.4 %fusion.2 = bf16[4,2,512,1536]{2,3,1,0:T(8,128)(2,1)} fusion(bf16[1536,4,128,1]{0,2,3,1:T(8,128)(2,1)S(1)} %bitcast.122, bf16[512,4,2,128]{0,3,2,1:T(8,128)(2,1)S(1)} %bitcast.115, f32[4,2,512]{2,1,0:T(2,128)} %bitcast.133, f32[4,2,512,1536]{2,3,1,0:T(8,128)} %get-tuple-element.33, f32[4,2,512]{2,1,0:T(2,128)S(1)} %get-tuple-element.32), kind=kOutput, calls=%fused_computation.3 | convolution fusion | flops 1635778560 | bytes 40402944 | tf_op jit(solution)/shard_map/ngrd,mgd->grnm/dot_general | solution.py:90
  290.4 9.6 %fusion.38 = (bf16[1536,4,128]{0,2,1:T(8,128)(2,1)S(1)}, f32[1536,4,128]{0,2,1:T(8,128)S(1)}) fusion(bf16[512,4,2,128]{3,0,2,1:T(8,128)(2,1)} %fusion.14, bf16[4,2,512,1536]{2,3,1,0:T(8,128)(2,1)} %fusion.2), kind=kOutput, calls=%fused_computation.79 | convolution fusion | flops 1611399168 | bytes 18350080 | tf_op jit(solution)/shard_map/grnm,ngrd->mgd/dot_general | solution.py:95
  300.8 1.9 collective-permute-start.5
  302.7 2.3 collective-permute-start.4
  305.1 6.9 %fusion.21 = f32[4,128,2,512]{3,1,2,0:T(8,128)S(1)} fusion(bf16[4,2,512,1536]{2,3,1,0:T(8,128)(2,1)} %fusion.2, bf16[512,4,128]{2,0,1:T(8,128)(2,1)S(1)} %maximum_convert_fusion, bf16[512,4,128]{2,0,1:T(8,128)(2,1)S(1)} %copy-done.8, bf16[512,4,128]{2,0,1:T(8,128)(2,1)S(1)} %copy-done.9), kind=kOutput, calls=%fused_computation.59 | convolution fusion | flops 1615331328 | bytes 16252928 | tf_op jit(solution)/shard_map/grnm,mgd->ngrd/dot_general | solution.py:94
  312.0 10.4 %fusion.37 = (bf16[1536,4,128]{0,2,1:T(8,128)(2,1)S(1)}, f32[1536,4,128]{0,2,1:T(8,128)}) fusion(bf16[512,4,2,128]{0,3,2,1:T(8,128)(2,1)S(1)} %bitcast.116, bf16[4,2,512,1536]{2,3,1,0:T(8,128)(2,1)} %copy-done), kind=kOutput, calls=%fused_computation.78 | convolution fusion | flops 1611399168 | bytes 18350080 | tf_op jit(solution)/shard_map/grnm,ngrd->mgd/dot_general | solution.py:98
  324.8 1.9 collective-permute-start.7
  326.7 1.9 collective-permute-start.6
  330.3 6.9 %collective-permute-done.4 = bf16[512,512]{0,1:T(8,128)(2,1)S(1)} collective-permute-done((bf16[512,512]{0,1:T(8,128)(2,1)S(1)}, bf16[512,512]{0,1:T(8,128)(2,1)S(1)}, u32[]{:S(2)}, u32[]{:S(2)}) %collective-permute-start.4) | collective-permute-done | bytes 524320 | tf_op jit(solution)/shard_map/ppermute | solution.py:19
  341.8 3.2 collective-permute-done.7
  345.0 7.2 %collective-permute-done.6 = bf16[512,512]{0,1:T(8,128)(2,1)} collective-permute-done((bf16[512,512]{0,1:T(8,128)(2,1)}, bf16[512,512]{0,1:T(8,128)(2,1)}, u32[]{:S(2)}, u32[]{:S(2)}) %collective-permute-start.6) | collective-permute-done | bytes 524320 | tf_op jit(solution)/shard_map/ppermute | solution.py:19
  352.2 1.4 fusion.18
  353.7 20.5 %fusion.4 = bf16[5376,2048]{1,0:T(8,128)(2,1)} fusion(bf16[512,5376]{1,0:T(8,128)(2,1)} %param.6, bf16[512,512]{0,1:T(8,128)(2,1)S(1)} %fusion.18, bf16[512,512]{0,1:T(8,128)(2,1)S(1)} %bitcast.128, bf16[512,1024]{0,1:T(8,128)(2,1)S(1)} %bitcast.126), kind=kOutput, calls=%fused_computation.8 | convolution fusion | flops 11291590656 | bytes 29622272 | tf_op jit(solution)/shard_map/nd,nc->dc/dot_general | solution.py:197
  374.2 18.3 %convolution_convert_fusion.2 = bf16[512,5376]{1,0:T(8,128)(2,1)} fusion(bf16[5376,2048]{1,0:T(8,128)(2,1)} %all-gather.3.cloned.1.call-done, bf16[512,512]{0,1:T(8,128)(2,1)S(1)} %fusion.18, bf16[512,512]{0,1:T(8,128)(2,1)S(1)} %bitcast.129, bf16[512,1024]{0,1:T(8,128)(2,1)S(1)} %bitcast.127), kind=kOutput, calls=%fused_computation.15 | convolution fusion | flops 11283333120 | bytes 29622272 | tf_op jit(solution)/shard_map/dot_general | solution.py:69
  392.6 9.0 %copy.73 = bf16[512,5376]{0,1:T(8,128)(2,1)} copy(bf16[512,5376]{1,0:T(8,128)(2,1)} %convolution_convert_fusion.2) | data formatting | bytes 11010048 | tf_op jit(solution)/shard_map/convert_element_type | solution.py:196
  401.6 5.7 %dynamic-slice_bitcast_fusion.2 = (bf16[512,1344]{0,1:T(8,128)(2,1)}, bf16[512,1344]{0,1:T(8,128)(2,1)}, bf16[512,1344]{0,1:T(8,128)(2,1)}) fusion(bf16[512,4,1344]{0,2,1:T(8,128)(2,1)} %bitcast.113, s32[]{:T(128)S(6)} %select_n.35, s32[]{:T(128)S(6)} %select_n.39, s32[]{:T(128)S(6)} %select_n.37), kind=kLoop, calls=%fused_computation.38 | loop fusion | bytes 8257548 | tf_op jit(solution)/shard_map/jit(dynamic_index_in_dim)/squeeze | solution.py:57
  407.3 3.0 collective-permute-start.10
  410.9 29.9 %collective-permute-done.10 = bf16[512,1344]{0,1:T(8,128)(2,1)S(1)} collective-permute-done((bf16[512,1344]{0,1:T(8,128)(2,1)}, bf16[512,1344]{0,1:T(8,128)(2,1)S(1)}, u32[]{:S(2)}, u32[]{:S(2)}) %collective-permute-start.10) | collective-permute-done | bytes 1376288 | tf_op jit(solution)/shard_map/ppermute | solution.py:58
  440.8 87.4 %collective-permute-done.9 = bf16[512,1344]{0,1:T(8,128)(2,1)S(1)} collective-permute-done((bf16[512,1344]{0,1:T(8,128)(2,1)}, bf16[512,1344]{0,1:T(8,128)(2,1)S(1)}, u32[]{:S(2)}, u32[]{:S(2)}) %collective-permute-start.9) | collective-permute-done | bytes 1376288 | tf_op jit(solution)/shard_map/ppermute | solution.py:58
  528.2 3.6 fusion.13
  531.7 3.2 convert_element_type.158
  535.0 3.4 slice.114
  538.3 1.9 fusion.31
  (71 shorter events, 16.7 us)
Async XLA Ops:
  7.2 117.4 %all-gather.3.cloned.1.call-start = ((), (), s32[]{:S(2)}) async-start(), calls=%async_computation.2 | async-start | bytes 24772608 | tf_op jit(solution)/shard_map/all_gather | solution.py:112
  10.9 247.9 %all-gather.5.cloned.1.call-start = ((), (), s32[]{:S(2)}) async-start(), calls=%async_computation.3 | async-start | bytes 12386304 | tf_op jit(solution)/shard_map/all_gather | solution.py:115
  11.6 520.1 %reduce-scatter.5.cloned.1.call-start = ((), (), s32[]{:S(2)}) async-start(), calls=%async_computation.5 | async-start | bytes 12386304 | tf_op jit(solution)/shard_map/reduce_scatter | solution.py:198
  12.2 144.2 %copy-start.6 = (f32[512,64]{0,1:T(8,128)}, f32[512,64]{0,1:T(8,128)S(1)}, u32[]{:S(2)}) copy-start(f32[512,64]{0,1:T(8,128)S(1)} %get-tuple-element.31) | copy-start | bytes 393220
  12.5 135.9 %copy-start.5 = (f32[512,64]{1,0:T(8,128)}, f32[512,64]{1,0:T(8,128)S(1)}, u32[]{:S(2)}) copy-start(f32[512,64]{1,0:T(8,128)S(1)} %copy.53) | copy-start | bytes 393220
  141.1 6.4 %copy-start.2 = (f32[512,2048]{0,1:T(8,128)}, f32[512,2048]{0,1:T(8,128)S(1)}, u32[]{:S(2)}) copy-start(f32[512,2048]{0,1:T(8,128)S(1)} %convolution_bitcast_fusion.2) | copy-start | bytes 12582916
  142.1 73.8 %collective-permute-start.3 = (bf16[512,512]{0,1:T(8,128)(2,1)}, bf16[512,512]{0,1:T(8,128)(2,1)}, u32[]{:S(2)}, u32[]{:S(2)}) collective-permute-start(bf16[512,512]{0,1:T(8,128)(2,1)} %slice.126), channel_id=1, source_target_pairs={{0,4},{4,8},{8,12},{12,16},{16,20},{20,24},{24,28},{1,5},{5,9},{9,... | collective-permute-start | bytes 1572872 | tf_op jit(solution)/shard_map/ppermute | solution.py:19
  144.4 71.5 %collective-permute-start.2 = (bf16[512,512]{0,1:T(8,128)(2,1)}, bf16[512,512]{0,1:T(8,128)(2,1)}, u32[]{:S(2)}, u32[]{:S(2)}) collective-permute-start(bf16[512,512]{0,1:T(8,128)(2,1)} %slice.126), channel_id=1, source_target_pairs={{0,8},{4,12},{8,16},{12,20},{16,24},{20,28},{1,9},{5,13},{9,17},{1... | collective-permute-start | bytes 1572872 | tf_op jit(solution)/shard_map/ppermute | solution.py:19
  148.4 6.2 %copy-start.11 = (s32[512]{0:T(512)S(1)}, s32[512]{0:T(512)}, u32[]{:S(2)}) copy-start(s32[512]{0:T(512)} %get-tuple-element.39) | copy-start | bytes 6148
  149.0 7.5 %slice-start = ((f32[512,2048]{0,1:T(8,128)}), f32[512,1024]{0,1:T(8,128)S(1)}, s32[]{:S(2)}) async-start(f32[512,2048]{0,1:T(8,128)} %copy-done.2), calls=%async_computation.6 | async-start | bytes 4194304 | tf_op jit(solution)/shard_map/slice | solution.py:117
  150.0 49.1 %collective-permute-start.1 = (bf16[512,512]{0,1:T(8,128)(2,1)}, bf16[512,512]{0,1:T(8,128)(2,1)}, u32[]{:S(2)}, u32[]{:S(2)}) collective-permute-start(bf16[512,512]{0,1:T(8,128)(2,1)} %bitcast.130), channel_id=1, source_target_pairs={{0,4},{4,8},{8,12},{12,16},{16,20},{20,24},{24,28},{1,5},{5,9},{9,... | collective-permute-start | bytes 1572872 | tf_op jit(solution)/shard_map/ppermute | solution.py:19
  152.5 61.3 %collective-permute-start = (bf16[512,512]{0,1:T(8,128)(2,1)}, bf16[512,512]{0,1:T(8,128)(2,1)}, u32[]{:S(2)}, u32[]{:S(2)}) collective-permute-start(bf16[512,512]{0,1:T(8,128)(2,1)} %bitcast.131), channel_id=1, source_target_pairs={{0,8},{4,12},{8,16},{12,20},{16,24},{20,28},{1,9},{5,13},{9,17},{1... | collective-permute-start | bytes 1572872 | tf_op jit(solution)/shard_map/ppermute | solution.py:19
  167.0 50.3 %copy-start.3 = (bf16[512,4,2,128]{3,0,2,1:T(8,128)(2,1)S(1)}, bf16[512,4,2,128]{3,0,2,1:T(8,128)(2,1)}, u32[]{:S(2)}) copy-start(bf16[512,4,2,128]{3,0,2,1:T(8,128)(2,1)} %fusion.14) | copy-start | bytes 3145732
  241.9 4.6 copy-start
  246.4 1.0 copy-start.4
  258.7 276.2 %reduce-scatter.3.cloned.1.call-start = ((), (), s32[]{:S(2)}) async-start(), calls=%async_computation.4 | async-start | bytes 24772608 | tf_op jit(solution)/shard_map/reduce_scatter | solution.py:201
  290.4 14.7 %copy-start.8 = (bf16[512,4,128]{2,0,1:T(8,128)(2,1)S(1)}, bf16[512,4,128]{2,0,1:T(8,128)(2,1)}, u32[]{:S(2)}) copy-start(bf16[512,4,128]{2,0,1:T(8,128)(2,1)} %copy.58) | copy-start | bytes 1572868
  290.4 14.7 %copy-start.9 = (bf16[512,4,128]{2,0,1:T(8,128)(2,1)S(1)}, bf16[512,4,128]{2,0,1:T(8,128)(2,1)}, u32[]{:S(2)}) copy-start(bf16[512,4,128]{2,0,1:T(8,128)(2,1)} %copy.57) | copy-start | bytes 1572868
  300.8 29.5 %collective-permute-start.5 = (bf16[512,512]{0,1:T(8,128)(2,1)}, bf16[512,512]{0,1:T(8,128)(2,1)S(1)}, u32[]{:S(2)}, u32[]{:S(2)}) collective-permute-start(bf16[512,512]{0,1:T(8,128)(2,1)} %bitcast.30), channel_id=1, source_target_pairs={{8,0},{12,4},{16,8},{20,12},{24,16},{28,20},{9,1},{13,5},{17,9},{2... | collective-permute-start | bytes 1572872 | tf_op jit(solution)/shard_map/ppermute | solution.py:19
  302.7 34.5 %collective-permute-start.4 = (bf16[512,512]{0,1:T(8,128)(2,1)S(1)}, bf16[512,512]{0,1:T(8,128)(2,1)S(1)}, u32[]{:S(2)}, u32[]{:S(2)}) collective-permute-start(bf16[512,512]{0,1:T(8,128)(2,1)S(1)} %bitcast.132), channel_id=1, source_target_pairs={{4,0},{8,4},{12,8},{16,12},{20,16},{24,20},{28,24},{5,1},{9,5},{13... | collective-permute-start | bytes 1572872 | tf_op jit(solution)/shard_map/ppermute | solution.py:19
  322.4 6.3 %copy-start.7 = (f32[512,64]{0,1:T(8,128)S(1)}, f32[512,64]{0,1:T(8,128)}, u32[]{:S(2)}) copy-start(f32[512,64]{0,1:T(8,128)} %copy-done.6) | copy-start | bytes 393220
  324.8 20.2 %collective-permute-start.7 = (bf16[512,512]{0,1:T(8,128)(2,1)}, bf16[512,512]{0,1:T(8,128)(2,1)}, u32[]{:S(2)}, u32[]{:S(2)}) collective-permute-start(bf16[512,512]{0,1:T(8,128)(2,1)} %bitcast.39), channel_id=1, source_target_pairs={{8,0},{12,4},{16,8},{20,12},{24,16},{28,20},{9,1},{13,5},{17,9},{2... | collective-permute-start | bytes 1572872 | tf_op jit(solution)/shard_map/ppermute | solution.py:19
  326.7 25.5 %collective-permute-start.6 = (bf16[512,512]{0,1:T(8,128)(2,1)}, bf16[512,512]{0,1:T(8,128)(2,1)}, u32[]{:S(2)}, u32[]{:S(2)}) collective-permute-start(bf16[512,512]{0,1:T(8,128)(2,1)} %bitcast.38), channel_id=1, source_target_pairs={{4,0},{8,4},{12,8},{16,12},{20,16},{24,20},{28,24},{5,1},{9,5},{13... | collective-permute-start | bytes 1572872 | tf_op jit(solution)/shard_map/ppermute | solution.py:19
  341.3 12.4 %copy-start.10 = (bf16[512,8,128]{0,2,1:T(8,128)(2,1)S(1)}, bf16[512,8,128]{0,2,1:T(8,128)(2,1)}, u32[]{:S(2)}) copy-start(bf16[512,8,128]{0,2,1:T(8,128)(2,1)} %fusion.15) | copy-start | bytes 3145732
  407.3 33.4 %collective-permute-start.10 = (bf16[512,1344]{0,1:T(8,128)(2,1)}, bf16[512,1344]{0,1:T(8,128)(2,1)S(1)}, u32[]{:S(2)}, u32[]{:S(2)}) collective-permute-start(bf16[512,1344]{0,1:T(8,128)(2,1)} %get-tuple-element.10), channel_id=1, source_target_pairs={{0,3},{1,0},{2,1},{3,2},{4,7},{5,4},{6,5},{7,6},{8,11},{9,8},{10,9... | collective-permute-start | bytes 4128776 | tf_op jit(solution)/shard_map/ppermute | solution.py:58
  410.3 117.8 %collective-permute-start.9 = (bf16[512,1344]{0,1:T(8,128)(2,1)}, bf16[512,1344]{0,1:T(8,128)(2,1)S(1)}, u32[]{:S(2)}, u32[]{:S(2)}) collective-permute-start(bf16[512,1344]{0,1:T(8,128)(2,1)} %get-tuple-element.11), channel_id=1, source_target_pairs={{0,2},{1,3},{2,0},{3,1},{4,6},{5,7},{6,4},{7,5},{8,10},{9,11},{10,... | collective-permute-start | bytes 4128776 | tf_op jit(solution)/shard_map/ppermute | solution.py:58
  410.4 117.8 %collective-permute-start.8 = (bf16[512,1344]{0,1:T(8,128)(2,1)}, bf16[512,1344]{0,1:T(8,128)(2,1)}, u32[]{:S(2)}, u32[]{:S(2)}) collective-permute-start(bf16[512,1344]{0,1:T(8,128)(2,1)} %get-tuple-element.9), channel_id=1, source_target_pairs={{0,1},{1,2},{2,3},{3,0},{4,5},{5,6},{6,7},{7,4},{8,9},{9,10},{10,1... | collective-permute-start | bytes 4128776 | tf_op jit(solution)/shard_map/ppermute | solution.py:58
  535.0 3.4 copy-start.1
Sparse Core Ops, SparseCore 0:
  11.0 113.5 all-gather.2
  126.4 87.9 all-gather.4
  258.9 118.5 reduce-scatter.4
  381.0 141.0 reduce-scatter.2

commit v9 on v8

--- a/solution.py
+++ b/solution.py
@@ -84,7 +84,7 @@
     return (prob, prob_b, attended)
 
 
-def attend_backward(prob, prob_b, attended, gradient_list, query_rows, key_rows, value_rows):
+def attend_backward(prob, prob_b, attended, gradient_list, query_rows, key_rows, value_rows, block):
     delta = jnp.sum(gradient_list.astype(jnp.float32) * attended.astype(jnp.float32), axis=-1)
     delta = jnp.transpose(delta, (1, 2, 0))[..., None]
     grad_prob = jnp.einsum(
@@ -92,10 +92,25 @@
     )
     grad_score = (prob * (grad_prob - delta)).astype(jnp.bfloat16)
     grad_q = jnp.einsum("grnm,mgd->ngrd", grad_score, key_rows, preferred_element_type=jnp.float32)
-    grad_k = jnp.einsum(
-        "grnm,ngrd->mgd", grad_score, query_rows, preferred_element_type=jnp.float32
-    )
-    grad_v = jnp.einsum("grnm,ngrd->mgd", prob_b, gradient_list, preferred_element_type=jnp.float32)
+    grad_k = []
+    grad_v = []
+    for lowest in range(0, key_rows.shape[0], block):
+        grad_k.append(
+            jnp.einsum(
+                "grnm,ngrd->mgd",
+                grad_score[..., lowest : lowest + block],
+                query_rows,
+                preferred_element_type=jnp.float32,
+            )
+        )
+        grad_v.append(
+            jnp.einsum(
+                "grnm,ngrd->mgd",
+                prob_b[..., lowest : lowest + block],
+                gradient_list,
+                preferred_element_type=jnp.float32,
+            )
+        )
     return (grad_q, grad_k, grad_v)
 
 
@@ -159,18 +174,17 @@
         "nd,nc->dc", out_grad, attended_flat, preferred_element_type=jnp.float32
     )
     grad_q, grad_k, grad_v = attend_backward(
-        prob, prob_b, attended, grouped_grads, grouped_queries, keys_all, values_all
-    )
-    grad_k = grad_k.reshape(-1, key_value_columns)
-    grad_v = grad_v.reshape(-1, key_value_columns)
-    own_keys = grad_k[reach * rows :]
-    own_values = grad_v[reach * rows :]
+        prob, prob_b, attended, grouped_grads, grouped_queries, keys_all, values_all, rows
+    )
+    grad_k = [part.reshape(rows, key_value_columns) for part in grad_k]
+    grad_v = [part.reshape(rows, key_value_columns) for part in grad_v]
+    own_keys = grad_k[reach]
+    own_values = grad_v[reach]
     for distance in range(1, reach + 1):
-        lowest = (reach - distance) * rows
         back_keys, back_values = from_behind(
             (
-                grad_k[lowest : lowest + rows].astype(jnp.bfloat16),
-                grad_v[lowest : lowest + rows].astype(jnp.bfloat16),
+                grad_k[reach - distance].astype(jnp.bfloat16),
+                grad_v[reach - distance].astype(jnp.bfloat16),
             ),
             "ctx",
             -distance,

time: 554 us -> 545 us (0.984)
    dot_general x2 -> x6, matrix products: 20 us -> 25.1 us  [the longest x3 15.3 us: attend_backward(): jnp.einsum('grnm,ngrd->mgd', prob_b[..., lowest:lowest + block], gradient...]
  transfers between devices with their start and end apart: 15 -> 15, of which waited for: 8 -> 7; matrix products, arithmetic and copies ran while one was open for 38% -> 37% of each run, Pallas kernels for 0% -> 0%
where the time goes in v9:
time: 545 us; the launch traced here: 538 us
  waiting for transfers between devices  290 us (53%)
  matrix products  137 us (25%)
  local copies, waits for them, and re-layouts  39.5 us (7%)
  other arithmetic  34.9 us (6%)
  starting transfers between devices  21.9 us (4%)
  between operations  14.5 us (3%)
    ppermute x3, waiting for transfers between devices, sum_over_heads(): lax.ppermute(outgoing, 'head', [(source, (source + shift) % count) for so...  116 us
    all_gather x1, waiting for transfers between devices, shards(): lax.all_gather(jnp.concatenate([w_query, key_weight, value_weight], axis=...  112 us
    ppermute x8, waiting for transfers between devices, from_behind(): lax.ppermute(value, axis, [(source, source + steps) for source in range(i...  61 us
    dot_general x1, matrix products, shards(): jnp.einsum('nd,nc->dc', hidden_in, grads_qkv, preferred_element_type=jnp....  20.3 us
    dot_general x1, matrix products, dot_rows(): lax.dot_general(left, weight, (((1,), (1,)), ((), ())), preferred_element...  18.2 us
    ppermute x8, starting transfers between devices, from_behind(): lax.ppermute(value, axis, [(source, source + steps) for source in range(i...  18.1 us
    dot_general x1, matrix products, shards(): projected = jnp.dot(hidden_in, full_qkv, preferred_element_type=jnp.float32)  16.7 us
    dot_general x1, matrix products, attend_backward(): jnp.einsum('ngrd,mgd->grnm', gradient_list, value_rows, preferred_element...  15.7 us
  transfers between devices with their start and end apart: 15, of which 7 were waited for; matrix products, arithmetic and copies ran while one was open for 37% of the time, Pallas kernels for 0%

profile of v9, /device:TPU:3, one launch (start us, length us, event | category | flops | bytes accessed | tf_op | source)
XLA Modules:
  0.0 537.6 jit_solution(10227466494219794678)
XLA Ops:
  7.2 3.6 pad_maximum_fusion
  12.5 112.0 %all-gather.3.cloned.1.call-done = bf16[5376,2048]{1,0:T(8,128)(2,1)} async-done(((bf16[672,2048]{1,0:T(8,128)(2,1)}), bf16[5376,2048]{1,0:T(8,128)(2,1)}) %all-gather.3.cloned.1.call-update) | async-done | bytes 22020112 | tf_op jit(solution)/shard_map/all_gather | solution.py:127
  124.6 16.7 %convolution_bitcast_fusion = f32[512,2048]{0,1:T(8,128)S(1)} fusion(bf16[5376,2048]{1,0:T(8,128)(2,1)} %all-gather.3.cloned.1.call-done, bf16[512,5376]{1,0:T(8,128)(2,1)} %param.6), kind=kOutput, calls=%fused_computation.28 | convolution fusion | flops 11274289152 | bytes 31719424 | tf_op jit(solution)/shard_map/dot_general | solution.py:131
  142.3 2.2 collective-permute-start.3
  144.5 3.2 collective-permute-start.2
  150.2 2.4 collective-permute-start.1
  152.6 2.1 collective-permute-start
  154.7 1.9 and_and_fusion
  156.6 1.8 multiply_subtract_fusion.1
  158.4 1.8 copy.72
  160.2 3.2 copy.71
  163.5 3.5 fusion.26
  167.0 32.3 %collective-permute-done.1 = bf16[512,512]{0,1:T(8,128)(2,1)} collective-permute-done((bf16[512,512]{0,1:T(8,128)(2,1)}, bf16[512,512]{0,1:T(8,128)(2,1)}, u32[]{:S(2)}, u32[]{:S(2)}) %collective-permute-start.1) | collective-permute-done | bytes 524320 | tf_op jit(solution)/shard_map/ppermute | solution.py:19
  200.6 13.3 %collective-permute-done = bf16[512,512]{0,1:T(8,128)(2,1)} collective-permute-done((bf16[512,512]{0,1:T(8,128)(2,1)}, bf16[512,512]{0,1:T(8,128)(2,1)}, u32[]{:S(2)}, u32[]{:S(2)}) %collective-permute-start) | collective-permute-done | bytes 524320 | tf_op jit(solution)/shard_map/ppermute | solution.py:19
  213.9 2.1 copy.69
  217.4 14.4 %fusion.70 = (f32[4,2,512]{2,1,0:T(2,128)S(1)}, f32[4,2,512,1536]{2,3,1,0:T(8,128)}) fusion(pred[512,1536]{0,1:T(8,128)(4,1)} %and_and_fusion, bf16[512,4,2,128]{3,0,2,1:T(8,128)(2,1)} %fusion.26, bf16[512,4,128]{2,0,1:T(8,128)(2,1)S(1)} %maximum_convert_fusion, bf16[512,4,128]{2,0,1:T(8,128)(2,1)S(1)} %copy.70, bf16[512,4,128]{2,0,1:T(8,128)(2,1)} %copy.69), kind=kOutput, calls=%fused_computation.93 | convolution fusion | flops 1634207232 | bytes 28590080 | tf_op jit(solution)/shard_map/sub | solution.py:78
  231.8 10.2 %fusion.7 = bf16[4,2,512,1536]{2,3,1,0:T(8,128)(2,1)S(1)} fusion(f32[4,2,512,1536]{2,3,1,0:T(8,128)} %get-tuple-element.29, f32[4,2,512]{2,1,0:T(2,128)S(1)} %get-tuple-element.28), kind=kLoop, calls=%fused_computation.13 | loop fusion | flops 12582912 | bytes 37765120 | tf_op jit(solution)/shard_map/convert_element_type | solution.py:80
  242.0 1.8 fusion.28
  243.9 2.7 copy-done
  247.5 11.5 %fusion.8 = bf16[5376,1024]{1,0:T(8,128)(2,1)} fusion(bf16[512,1024]{0,1:T(8,128)(2,1)S(1)} %bitcast.157, bf16[512,5376]{1,0:T(8,128)(2,1)} %param.7), kind=kOutput, calls=%fused_computation.14 | convolution fusion | flops 5642649600 | bytes 17563648 | tf_op jit(solution)/shard_map/nd,nc->dc/dot_general | solution.py:173
  259.2 11.0 %convolution_convert_fusion.3 = bf16[512,1024]{1,0:T(8,128)(2,1)} fusion(bf16[512,5376]{1,0:T(8,128)(2,1)} %param.7, bf16[5376,1024]{1,0:T(8,128)(2,1)} %all-gather.5.cloned.1.call-done), kind=kOutput, calls=%fused_computation.44 | convolution fusion | flops 5637668864 | bytes 17563648 | tf_op jit(solution)/shard_map/dot_general | solution.py:168
  270.2 2.5 copy.74
  272.7 6.1 %fusion.41 = bf16[4,128,512]{2,1,0:T(8,128)(2,1)} fusion(bf16[512,4,2,128]{0,3,2,1:T(8,128)(2,1)} %bitcast.152, bf16[4,2,512,1536]{2,3,1,0:T(8,128)(2,1)} %copy-done), kind=kOutput, calls=%fused_computation.54 | convolution fusion | flops 537133056 | bytes 5767168 | tf_op jit(solution)/shard_map/grnm,ngrd->mgd/dot_general | solution.py:107
  278.8 2.0 collective-permute-start.7
  280.9 4.5 fusion.44
  285.4 1.9 collective-permute-start.6
  287.6 15.7 %fusion.2 = bf16[4,2,512,1536]{2,3,1,0:T(8,128)(2,1)} fusion(bf16[1536,4,128,1]{0,2,3,1:T(8,128)(2,1)S(1)} %bitcast.150, bf16[512,4,2,128]{0,3,2,1:T(8,128)(2,1)} %bitcast.153, f32[4,2,512]{2,1,0:T(2,128)S(1)} %bitcast.164, f32[4,2,512,1536]{2,3,1,0:T(8,128)} %get-tuple-element.29, f32[4,2,512]{2,1,0:T(2,128)S(1)} %get-tuple-element.28), kind=kOutput, calls=%fused_computation.3 | convolution fusion | flops 1635778560 | bytes 40402944 | tf_op jit(solution)/shard_map/ngrd,mgd->grnm/dot_general | solution.py:90
  303.3 4.2 fusion.47
  307.5 2.2 collective-permute-start.5
  309.7 4.1 fusion.50
  313.8 2.1 collective-permute-start.4
  315.9 2.0 fusion.57
  319.1 1.5 fusion.19
  321.9 4.7 fusion.13
  326.6 9.2 %collective-permute-done.5 = bf16[512,512]{0,1:T(8,128)(2,1)S(1)} collective-permute-done((bf16[512,512]{0,1:T(8,128)(2,1)S(1)}, bf16[512,512]{0,1:T(8,128)(2,1)S(1)}, u32[]{:S(2)}, u32[]{:S(2)}) %collective-permute-start.5) | collective-permute-done | bytes 524320 | tf_op jit(solution)/shard_map/ppermute | solution.py:19
  335.9 6.1 %collective-permute-done.4 = bf16[512,512]{0,1:T(8,128)(2,1)S(1)} collective-permute-done((bf16[512,512]{0,1:T(8,128)(2,1)S(1)}, bf16[512,512]{0,1:T(8,128)(2,1)S(1)}, u32[]{:S(2)}, u32[]{:S(2)}) %collective-permute-start.4) | collective-permute-done | bytes 524320 | tf_op jit(solution)/shard_map/ppermute | solution.py:19
  343.8 1.7 fusion.54
  345.6 20.3 %fusion.4 = bf16[5376,2048]{1,0:T(8,128)(2,1)} fusion(bf16[512,5376]{1,0:T(8,128)(2,1)} %param.6, bf16[512,512]{0,1:T(8,128)(2,1)S(1)} %fusion.54, bf16[512,512]{0,1:T(8,128)(2,1)S(1)} %bitcast.160, bf16[512,1024]{0,1:T(8,128)(2,1)S(1)} %bitcast.158), kind=kOutput, calls=%fused_computation.8 | convolution fusion | flops 11291590656 | bytes 29622272 | tf_op jit(solution)/shard_map/nd,nc->dc/dot_general | solution.py:211
  365.9 18.2 %convolution_convert_fusion.2 = bf16[512,5376]{1,0:T(8,128)(2,1)} fusion(bf16[5376,2048]{1,0:T(8,128)(2,1)} %all-gather.3.cloned.1.call-done, bf16[512,512]{0,1:T(8,128)(2,1)S(1)} %fusion.54, bf16[512,512]{0,1:T(8,128)(2,1)S(1)} %bitcast.161, bf16[512,1024]{0,1:T(8,128)(2,1)S(1)} %bitcast.159), kind=kOutput, calls=%fused_computation.15 | convolution fusion | flops 11283333120 | bytes 29622272 | tf_op jit(solution)/shard_map/dot_general | solution.py:69
  384.1 8.9 %copy.91 = bf16[512,5376]{0,1:T(8,128)(2,1)} copy(bf16[512,5376]{1,0:T(8,128)(2,1)} %convolution_convert_fusion.2) | data formatting | bytes 11010048 | tf_op jit(solution)/shard_map/convert_element_type | solution.py:210
  393.1 5.7 %dynamic-slice_bitcast_fusion.2 = (bf16[512,1344]{0,1:T(8,128)(2,1)}, bf16[512,1344]{0,1:T(8,128)(2,1)}, bf16[512,1344]{0,1:T(8,128)(2,1)}) fusion(bf16[512,4,1344]{0,2,1:T(8,128)(2,1)} %bitcast.143, s32[]{:T(128)S(6)} %select_n.35, s32[]{:T(128)S(6)} %select_n.39, s32[]{:T(128)S(6)} %select_n.37), kind=kLoop, calls=%fused_computation.48 | loop fusion | bytes 8257548 | tf_op jit(solution)/shard_map/jit(dynamic_index_in_dim)/squeeze | solution.py:57
  398.8 3.1 collective-permute-start.10
  402.4 29.8 %collective-permute-done.10 = bf16[512,1344]{0,1:T(8,128)(2,1)S(1)} collective-permute-done((bf16[512,1344]{0,1:T(8,128)(2,1)}, bf16[512,1344]{0,1:T(8,128)(2,1)S(1)}, u32[]{:S(2)}, u32[]{:S(2)}) %collective-permute-start.10) | collective-permute-done | bytes 1376288 | tf_op jit(solution)/shard_map/ppermute | solution.py:58
  432.2 86.6 %collective-permute-done.9 = bf16[512,1344]{0,1:T(8,128)(2,1)S(1)} collective-permute-done((bf16[512,1344]{0,1:T(8,128)(2,1)}, bf16[512,1344]{0,1:T(8,128)(2,1)S(1)}, u32[]{:S(2)}, u32[]{:S(2)}) %collective-permute-start.9) | collective-permute-done | bytes 1376288 | tf_op jit(solution)/shard_map/ppermute | solution.py:58
  518.8 3.6 fusion.25
  522.4 3.2 convert_element_type.186
  525.6 3.4 slice.98
  529.0 1.9 fusion.67
  (69 shorter events, 14.0 us)
Async XLA Ops:
  7.2 117.4 %all-gather.3.cloned.1.call-start = ((), (), s32[]{:S(2)}) async-start(), calls=%async_computation.2 | async-start | bytes 24772608 | tf_op jit(solution)/shard_map/all_gather | solution.py:127
  10.9 248.3 %all-gather.5.cloned.1.call-start = ((), (), s32[]{:S(2)}) async-start(), calls=%async_computation.3 | async-start | bytes 12386304 | tf_op jit(solution)/shard_map/all_gather | solution.py:130
  11.6 510.8 %reduce-scatter.5.cloned.1.call-start = ((), (), s32[]{:S(2)}) async-start(), calls=%async_computation.5 | async-start | bytes 12386304 | tf_op jit(solution)/shard_map/reduce_scatter | solution.py:212
  141.3 6.4 %copy-start.3 = (f32[512,2048]{0,1:T(8,128)}, f32[512,2048]{0,1:T(8,128)S(1)}, u32[]{:S(2)}) copy-start(f32[512,2048]{0,1:T(8,128)S(1)} %convolution_bitcast_fusion) | copy-start | bytes 12582916
  142.3 73.7 %collective-permute-start.3 = (bf16[512,512]{0,1:T(8,128)(2,1)}, bf16[512,512]{0,1:T(8,128)(2,1)}, u32[]{:S(2)}, u32[]{:S(2)}) collective-permute-start(bf16[512,512]{0,1:T(8,128)(2,1)} %slice.138), channel_id=1, source_target_pairs={{0,4},{4,8},{8,12},{12,16},{16,20},{20,24},{24,28},{1,5},{5,9},{9,... | collective-permute-start | bytes 1572872 | tf_op jit(solution)/shard_map/ppermute | solution.py:19
  144.5 71.4 %collective-permute-start.2 = (bf16[512,512]{0,1:T(8,128)(2,1)}, bf16[512,512]{0,1:T(8,128)(2,1)}, u32[]{:S(2)}, u32[]{:S(2)}) collective-permute-start(bf16[512,512]{0,1:T(8,128)(2,1)} %slice.138), channel_id=1, source_target_pairs={{0,8},{4,12},{8,16},{12,20},{16,24},{20,28},{1,9},{5,13},{9,17},{1... | collective-permute-start | bytes 1572872 | tf_op jit(solution)/shard_map/ppermute | solution.py:19
  149.1 7.4 %slice-start = ((f32[512,2048]{0,1:T(8,128)}), f32[512,1024]{0,1:T(8,128)S(1)}, s32[]{:S(2)}) async-start(f32[512,2048]{0,1:T(8,128)} %copy-done.3), calls=%async_computation.6 | async-start | bytes 4194304 | tf_op jit(solution)/shard_map/slice | solution.py:132
  150.2 49.1 %collective-permute-start.1 = (bf16[512,512]{0,1:T(8,128)(2,1)}, bf16[512,512]{0,1:T(8,128)(2,1)}, u32[]{:S(2)}, u32[]{:S(2)}) collective-permute-start(bf16[512,512]{0,1:T(8,128)(2,1)} %bitcast.162), channel_id=1, source_target_pairs={{0,4},{4,8},{8,12},{12,16},{16,20},{20,24},{24,28},{1,5},{5,9},{9,... | collective-permute-start | bytes 1572872 | tf_op jit(solution)/shard_map/ppermute | solution.py:19
  152.6 61.3 %collective-permute-start = (bf16[512,512]{0,1:T(8,128)(2,1)}, bf16[512,512]{0,1:T(8,128)(2,1)}, u32[]{:S(2)}, u32[]{:S(2)}) collective-permute-start(bf16[512,512]{0,1:T(8,128)(2,1)} %bitcast.163), channel_id=1, source_target_pairs={{0,8},{4,12},{8,16},{12,20},{16,24},{20,28},{1,9},{5,13},{9,17},{1... | collective-permute-start | bytes 1572872 | tf_op jit(solution)/shard_map/ppermute | solution.py:19
  242.0 4.5 copy-start
  246.6 1.0 copy-start.6
  259.1 266.5 %reduce-scatter.3.cloned.1.call-start = ((), (), s32[]{:S(2)}) async-start(), calls=%async_computation.4 | async-start | bytes 24772608 | tf_op jit(solution)/shard_map/reduce_scatter | solution.py:215
  272.7 8.2 %copy-start.4 = (bf16[512,1024]{0,1:T(8,128)(2,1)S(1)}, bf16[512,1024]{0,1:T(8,128)(2,1)}, u32[]{:S(2)}) copy-start(bf16[512,1024]{0,1:T(8,128)(2,1)} %copy.74) | copy-start | bytes 3145732
  278.8 8.5 %copy-start.7 = (bf16[512,4,2,128]{0,3,2,1:T(8,128)(2,1)S(1)}, bf16[512,4,2,128]{0,3,2,1:T(8,128)(2,1)}, u32[]{:S(2)}) copy-start(bf16[512,4,2,128]{0,3,2,1:T(8,128)(2,1)} %copy-done.6) | copy-start | bytes 3145732
  278.8 65.0 %collective-permute-start.7 = (bf16[512,512]{0,1:T(8,128)(2,1)}, bf16[512,512]{0,1:T(8,128)(2,1)}, u32[]{:S(2)}, u32[]{:S(2)}) collective-permute-start(bf16[512,512]{0,1:T(8,128)(2,1)} %bitcast.49), channel_id=1, source_target_pairs={{8,0},{12,4},{16,8},{20,12},{24,16},{28,20},{9,1},{13,5},{17,9},{2... | collective-permute-start | bytes 1572872 | tf_op jit(solution)/shard_map/ppermute | solution.py:19
  285.4 58.5 %collective-permute-start.6 = (bf16[512,512]{0,1:T(8,128)(2,1)}, bf16[512,512]{0,1:T(8,128)(2,1)}, u32[]{:S(2)}, u32[]{:S(2)}) collective-permute-start(bf16[512,512]{0,1:T(8,128)(2,1)} %bitcast.45), channel_id=1, source_target_pairs={{4,0},{8,4},{12,8},{16,12},{20,16},{24,20},{28,24},{5,1},{9,5},{13... | collective-permute-start | bytes 1572872 | tf_op jit(solution)/shard_map/ppermute | solution.py:19
  303.3 12.6 %copy-start.1 = (bf16[4,2,512,1536]{2,3,1,0:T(8,128)(2,1)S(1)}, bf16[4,2,512,1536]{2,3,1,0:T(8,128)(2,1)}, u32[]{:S(2)}) copy-start(bf16[4,2,512,1536]{2,3,1,0:T(8,128)(2,1)} %fusion.2) | copy-start | bytes 37748740
  307.5 8.4 %copy-start.8 = (bf16[512,4,128]{2,0,1:T(8,128)(2,1)S(1)}, bf16[512,4,128]{2,0,1:T(8,128)(2,1)}, u32[]{:S(2)}) copy-start(bf16[512,4,128]{2,0,1:T(8,128)(2,1)} %copy.69) | copy-start | bytes 1572868
  307.5 28.3 %collective-permute-start.5 = (bf16[512,512]{0,1:T(8,128)(2,1)S(1)}, bf16[512,512]{0,1:T(8,128)(2,1)S(1)}, u32[]{:S(2)}, u32[]{:S(2)}) collective-permute-start(bf16[512,512]{0,1:T(8,128)(2,1)S(1)} %bitcast.165), channel_id=1, source_target_pairs={{8,0},{12,4},{16,8},{20,12},{24,16},{28,20},{9,1},{13,5},{17,9},{2... | collective-permute-start | bytes 1572872 | tf_op jit(solution)/shard_map/ppermute | solution.py:19
  313.8 28.2 %collective-permute-start.4 = (bf16[512,512]{0,1:T(8,128)(2,1)S(1)}, bf16[512,512]{0,1:T(8,128)(2,1)S(1)}, u32[]{:S(2)}, u32[]{:S(2)}) collective-permute-start(bf16[512,512]{0,1:T(8,128)(2,1)S(1)} %bitcast.166), channel_id=1, source_target_pairs={{4,0},{8,4},{12,8},{16,12},{20,16},{24,20},{28,24},{5,1},{9,5},{13... | collective-permute-start | bytes 1572872 | tf_op jit(solution)/shard_map/ppermute | solution.py:19
  317.9 1.2 copy-start.10
  320.7 1.3 copy-start.5
  343.3 2.3 copy-start.9
  398.8 33.4 %collective-permute-start.10 = (bf16[512,1344]{0,1:T(8,128)(2,1)}, bf16[512,1344]{0,1:T(8,128)(2,1)S(1)}, u32[]{:S(2)}, u32[]{:S(2)}) collective-permute-start(bf16[512,1344]{0,1:T(8,128)(2,1)} %get-tuple-element.10), channel_id=1, source_target_pairs={{0,3},{1,0},{2,1},{3,2},{4,7},{5,4},{6,5},{7,6},{8,11},{9,8},{10,9... | collective-permute-start | bytes 4128776 | tf_op jit(solution)/shard_map/ppermute | solution.py:58
  401.8 117.0 %collective-permute-start.9 = (bf16[512,1344]{0,1:T(8,128)(2,1)}, bf16[512,1344]{0,1:T(8,128)(2,1)S(1)}, u32[]{:S(2)}, u32[]{:S(2)}) collective-permute-start(bf16[512,1344]{0,1:T(8,128)(2,1)} %get-tuple-element.11), channel_id=1, source_target_pairs={{0,2},{1,3},{2,0},{3,1},{4,6},{5,7},{6,4},{7,5},{8,10},{9,11},{10,... | collective-permute-start | bytes 4128776 | tf_op jit(solution)/shard_map/ppermute | solution.py:58
  401.8 117.0 %collective-permute-start.8 = (bf16[512,1344]{0,1:T(8,128)(2,1)}, bf16[512,1344]{0,1:T(8,128)(2,1)}, u32[]{:S(2)}, u32[]{:S(2)}) collective-permute-start(bf16[512,1344]{0,1:T(8,128)(2,1)} %get-tuple-element.9), channel_id=1, source_target_pairs={{0,1},{1,2},{2,3},{3,0},{4,5},{5,6},{6,7},{7,4},{8,9},{9,10},{10,1... | collective-permute-start | bytes 4128776 | tf_op jit(solution)/shard_map/ppermute | solution.py:58
  525.6 3.4 copy-start.2
Sparse Core Ops, SparseCore 0:
  11.0 113.5 all-gather.2
  126.4 87.9 all-gather.4
  259.2 108.0 reduce-scatter.4
  370.8 141.0 reduce-scatter.2

commit v10 on v9

--- a/solution.py
+++ b/solution.py
@@ -146,9 +146,9 @@
     key_blocks = []
     value_blocks = []
     for distance in range(reach, 0, -1):
-        far_keys, far_values = from_behind((keys_here, values_here), "ctx", distance)
-        key_blocks.append(far_keys)
-        value_blocks.append(far_values)
+        far = from_behind(jnp.concatenate([keys_here, values_here], axis=1), "ctx", distance)
+        key_blocks.append(far[:, :key_value_columns])
+        value_blocks.append(far[:, key_value_columns:])
     keys_all = jnp.concatenate(key_blocks + [keys_here], axis=0).reshape(
         -1, local_groups, head_size
     )
@@ -181,14 +181,15 @@
     own_keys = grad_k[reach]
     own_values = grad_v[reach]
     for distance in range(1, reach + 1):
-        back_keys, back_values = from_behind(
-            (
-                grad_k[reach - distance].astype(jnp.bfloat16),
-                grad_v[reach - distance].astype(jnp.bfloat16),
+        back = from_behind(
+            jnp.concatenate([grad_k[reach - distance], grad_v[reach - distance]], axis=1).astype(
+                jnp.bfloat16
             ),
             "ctx",
             -distance,
         )
+        back_keys = back[:, :key_value_columns]
+        back_values = back[:, key_value_columns:]
         own_keys = own_keys + back_keys.astype(jnp.float32)
         own_values = own_values + back_values.astype(jnp.float32)
     dquery = (

time: 545 us -> 546 us (level)
  matrix products: 137 us -> 129 us
  waiting for transfers between devices: 290 us -> 296 us
  starting transfers between devices: 21.9 us -> 16.2 us
    ppermute x3, waiting for transfers between devices: 116 us -> 88.7 us  [sum_over_heads(): lax.ppermute(outgoing, 'head', [(source, (source + shift) % count) for so...]
    reduce_scatter x1, waiting for transfers between devices: 0.01 us -> 24.8 us  [shards(): lax.psum_scatter(row_major(grad_qkv_part.astype(jnp.bfloat16)), 'ctx', sc...]
    ppermute x8 -> x4, waiting for transfers between devices: 61 us -> 70.2 us  [from_behind(): lax.ppermute(value, axis, [(source, source + steps) for source in range(i...]
    ppermute x8 -> x4, starting transfers between devices: 18.1 us -> 11.5 us  [from_behind(): lax.ppermute(value, axis, [(source, source + steps) for source in range(i...]
  transfers between devices with their start and end apart: 15 -> 11, of which waited for: 7 -> 8; matrix products, arithmetic and copies ran while one was open for 37% -> 36% of each run, Pallas kernels for 0% -> 0%
where the time goes in v10:
time: 546 us; the launch traced here: 536 us
  waiting for transfers between devices  296 us (54%)
  matrix products  129 us (24%)
  local copies, waits for them, and re-layouts  43.5 us (8%)
  other arithmetic  36.7 us (7%)
  starting transfers between devices  16.2 us (3%)
  between operations  14.5 us (3%)
    all_gather x1, waiting for transfers between devices, shards(): lax.all_gather(jnp.concatenate([w_query, key_weight, value_weight], axis=...  112 us
    ppermute x3, waiting for transfers between devices, sum_over_heads(): lax.ppermute(outgoing, 'head', [(source, (source + shift) % count) for so...  88.7 us
    ppermute x4, waiting for transfers between devices, from_behind(): lax.ppermute(value, axis, [(source, source + steps) for source in range(i...  70.2 us
    reduce_scatter x1, waiting for transfers between devices, shards(): lax.psum_scatter(row_major(grad_qkv_part.astype(jnp.bfloat16)), 'ctx', sc...  24.8 us
    dot_general x1, matrix products, dot_rows(): lax.dot_general(left, weight, (((1,), (1,)), ((), ())), preferred_element...  18.2 us
    dot_general x1, matrix products, attend_backward(): jnp.einsum('ngrd,mgd->grnm', gradient_list, value_rows, preferred_element...  17.1 us
    dot_general x1, matrix products, shards(): jnp.einsum('nd,nc->dc', hidden_in, grads_qkv, preferred_element_type=jnp....  17 us
    dot_general x1, matrix products, shards(): projected = jnp.dot(hidden_in, full_qkv, preferred_element_type=jnp.float32)  16.6 us
  transfers between devices with their start and end apart: 11, of which 8 were waited for; matrix products, arithmetic and copies ran while one was open for 36% of the time, Pallas kernels for 0%

profile of v10, /device:TPU:3, one launch (start us, length us, event | category | flops | bytes accessed | tf_op | source)
XLA Modules:
  0.0 536.3 jit_solution(11053036205945918029)
XLA Ops:
  7.2 3.6 pad_maximum_fusion
  12.5 112.0 %all-gather.3.cloned.1.call-done = bf16[5376,2048]{1,0:T(8,128)(2,1)} async-done(((bf16[672,2048]{1,0:T(8,128)(2,1)}), bf16[5376,2048]{1,0:T(8,128)(2,1)}) %all-gather.3.cloned.1.call-update) | async-done | bytes 22020112 | tf_op jit(solution)/shard_map/all_gather | solution.py:127
  124.6 16.6 %convolution_bitcast_fusion = f32[512,2048]{0,1:T(8,128)S(1)} fusion(bf16[5376,2048]{1,0:T(8,128)(2,1)} %all-gather.3.cloned.1.call-done, bf16[512,5376]{1,0:T(8,128)(2,1)} %param.6), kind=kOutput, calls=%fused_computation.28 | convolution fusion | flops 11274289152 | bytes 31719424 | tf_op jit(solution)/shard_map/dot_general | solution.py:131
  141.2 1.8 copy-done.3
  144.4 1.4 copy.122
  147.6 2.1 collective-permute-start
  149.8 3.7 collective-permute-start.1
  153.6 1.9 and_and_fusion
  155.5 1.6 multiply_subtract_fusion.1
  157.1 1.8 copy.75
  158.9 3.5 copy.74
  162.4 3.2 fusion.26
  165.6 24.0 %collective-permute-done = bf16[512,1024]{0,1:T(8,128)(2,1)} collective-permute-done((bf16[512,1024]{0,1:T(8,128)(2,1)}, bf16[512,1024]{0,1:T(8,128)(2,1)}, u32[]{:S(2)}, u32[]{:S(2)}) %collective-permute-start) | collective-permute-done | bytes 1048608 | tf_op jit(solution)/shard_map/ppermute | solution.py:19
  189.6 2.1 fusion.69
  191.9 21.8 %collective-permute-done.1 = bf16[512,1024]{0,1:T(8,128)(2,1)} collective-permute-done((bf16[512,1024]{0,1:T(8,128)(2,1)}, bf16[512,1024]{0,1:T(8,128)(2,1)}, u32[]{:S(2)}, u32[]{:S(2)}) %collective-permute-start.1) | collective-permute-done | bytes 1048608 | tf_op jit(solution)/shard_map/ppermute | solution.py:19
  213.8 2.1 fusion.70
  218.1 14.4 %fusion.72 = (f32[4,2,512]{2,1,0:T(2,128)S(1)}, f32[4,2,512,1536]{2,3,1,0:T(8,128)}) fusion(pred[512,1536]{0,1:T(8,128)(4,1)} %and_and_fusion, bf16[512,4,2,128]{3,0,2,1:T(8,128)(2,1)} %fusion.26, bf16[512,4,128]{2,0,1:T(8,128)(2,1)S(1)} %maximum_convert_fusion, bf16[512,4,128]{2,0,1:T(8,128)(2,1)} %copy.73, bf16[512,4,128]{2,0,1:T(8,128)(2,1)S(1)} %copy.72), kind=kOutput, calls=%fused_computation.98 | convolution fusion | flops 1634207232 | bytes 28590080 | tf_op jit(solution)/shard_map/sub | solution.py:78
  232.5 10.2 %fusion.7 = bf16[4,2,512,1536]{2,3,1,0:T(8,128)(2,1)S(1)} fusion(f32[4,2,512,1536]{2,3,1,0:T(8,128)} %get-tuple-element.35, f32[4,2,512]{2,1,0:T(2,128)S(1)} %get-tuple-element.34), kind=kLoop, calls=%fused_computation.13 | loop fusion | flops 12582912 | bytes 37765120 | tf_op jit(solution)/shard_map/convert_element_type | solution.py:80
  242.8 1.8 fusion.28
  244.6 2.7 copy-done
  248.3 11.5 %fusion.8 = bf16[5376,1024]{1,0:T(8,128)(2,1)} fusion(bf16[512,1024]{0,1:T(8,128)(2,1)S(1)} %bitcast.157, bf16[512,5376]{1,0:T(8,128)(2,1)} %param.7), kind=kOutput, calls=%fused_computation.14 | convolution fusion | flops 5642649600 | bytes 17563648 | tf_op jit(solution)/shard_map/nd,nc->dc/dot_general | solution.py:173
  259.9 11.0 %convolution_convert_fusion.3 = bf16[512,1024]{1,0:T(8,128)(2,1)} fusion(bf16[512,5376]{1,0:T(8,128)(2,1)} %param.7, bf16[5376,1024]{1,0:T(8,128)(2,1)} %all-gather.5.cloned.1.call-done), kind=kOutput, calls=%fused_computation.44 | convolution fusion | flops 5637668864 | bytes 17563648 | tf_op jit(solution)/shard_map/dot_general | solution.py:168
  270.9 2.4 copy.77
  273.3 2.3 multiply_reduce_fusion
  275.6 17.1 %fusion.2 = bf16[4,2,512,1536]{2,3,1,0:T(8,128)(2,1)} fusion(bf16[1536,4,128,1]{0,2,3,1:T(8,128)(2,1)S(1)} %bitcast.150, bf16[512,4,2,128]{0,3,2,1:T(8,128)(2,1)} %bitcast.151, f32[4,2,512]{2,1,0:T(2,128)S(1)} %bitcast.169, f32[4,2,512,1536]{2,3,1,0:T(8,128)} %get-tuple-element.35, f32[4,2,512]{2,1,0:T(2,128)S(1)} %get-tuple-element.34), kind=kOutput, calls=%fused_computation.3 | convolution fusion | flops 1635778560 | bytes 40402944 | tf_op jit(solution)/shard_map/ngrd,mgd->grnm/dot_general | solution.py:90
  292.7 4.2 fusion.50
  296.9 4.8 fusion.47
  301.8 3.4 collective-permute-start.2
  305.3 1.5 fusion.44
  306.8 3.9 fusion.41
  310.9 2.2 collective-permute-start.3
  313.1 2.0 fusion.57
  316.7 1.5 fusion.19
  318.2 3.7 fusion.9
  321.9 18.5 %collective-permute-done.2 = bf16[512,1024]{0,1:T(8,128)(2,1)S(1)} collective-permute-done((bf16[512,1024]{0,1:T(8,128)(2,1)S(1)}, bf16[512,1024]{0,1:T(8,128)(2,1)S(1)}, u32[]{:S(2)}, u32[]{:S(2)}) %collective-permute-start.2) | collective-permute-done | bytes 1048608 | tf_op jit(solution)/shard_map/ppermute | solution.py:19
  340.4 5.8 %collective-permute-done.3 = bf16[512,1024]{0,1:T(8,128)(2,1)S(1)} collective-permute-done((bf16[512,1024]{0,1:T(8,128)(2,1)S(1)}, bf16[512,1024]{0,1:T(8,128)(2,1)S(1)}, u32[]{:S(2)}, u32[]{:S(2)}) %collective-permute-start.3) | collective-permute-done | bytes 1048608 | tf_op jit(solution)/shard_map/ppermute | solution.py:19
  349.1 17.0 %fusion.4 = bf16[5376,2048]{1,0:T(8,128)(2,1)} fusion(bf16[512,5376]{1,0:T(8,128)(2,1)} %param.6, bf16[512,512]{0,1:T(8,128)(2,1)} %get-tuple-element.23, bf16[512,512]{0,1:T(8,128)(2,1)S(1)} %bitcast.163, bf16[512,1024]{0,1:T(8,128)(2,1)} %bitcast.161), kind=kOutput, calls=%fused_computation.8 | convolution fusion | flops 11291590656 | bytes 29622272 | tf_op jit(solution)/shard_map/nd,nc->dc/dot_general | solution.py:212
  367.5 18.2 %convolution_convert_fusion.2 = bf16[512,5376]{1,0:T(8,128)(2,1)} fusion(bf16[5376,2048]{1,0:T(8,128)(2,1)} %all-gather.3.cloned.1.call-done, bf16[512,512]{0,1:T(8,128)(2,1)S(1)} %copy-done.14, bf16[512,512]{0,1:T(8,128)(2,1)S(1)} %bitcast.164, bf16[512,1024]{0,1:T(8,128)(2,1)S(1)} %bitcast.162), kind=kOutput, calls=%fused_computation.15 | convolution fusion | flops 11283333120 | bytes 29622272 | tf_op jit(solution)/shard_map/dot_general | solution.py:69
  385.7 8.4 %copy.94 = bf16[512,5376]{0,1:T(8,128)(2,1)} copy(bf16[512,5376]{1,0:T(8,128)(2,1)} %convolution_convert_fusion.2) | data formatting | bytes 11010048 | tf_op jit(solution)/shard_map/convert_element_type | solution.py:211
  394.1 5.5 %dynamic-slice_bitcast_fusion.2 = (bf16[512,1344]{0,1:T(8,128)(2,1)}, bf16[512,1344]{0,1:T(8,128)(2,1)}, bf16[512,1344]{0,1:T(8,128)(2,1)}) fusion(bf16[512,4,1344]{0,2,1:T(8,128)(2,1)} %bitcast.143, s32[]{:T(128)S(6)} %select_n.35, s32[]{:T(128)S(6)} %select_n.39, s32[]{:T(128)S(6)} %select_n.37), kind=kLoop, calls=%fused_computation.48 | loop fusion | bytes 8257548 | tf_op jit(solution)/shard_map/jit(dynamic_index_in_dim)/squeeze | solution.py:57
  400.8 2.1 collective-permute-start.5
  404.0 19.8 %collective-permute-done.4 = bf16[512,1344]{0,1:T(8,128)(2,1)S(1)} collective-permute-done((bf16[512,1344]{0,1:T(8,128)(2,1)}, bf16[512,1344]{0,1:T(8,128)(2,1)S(1)}, u32[]{:S(2)}, u32[]{:S(2)}) %collective-permute-start.4) | collective-permute-done | bytes 1376288 | tf_op jit(solution)/shard_map/ppermute | solution.py:58
  423.8 68.9 %collective-permute-done.5 = bf16[512,1344]{0,1:T(8,128)(2,1)S(1)} collective-permute-done((bf16[512,1344]{0,1:T(8,128)(2,1)}, bf16[512,1344]{0,1:T(8,128)(2,1)S(1)}, u32[]{:S(2)}, u32[]{:S(2)}) %collective-permute-start.5) | collective-permute-done | bytes 1376288 | tf_op jit(solution)/shard_map/ppermute | solution.py:58
  492.7 3.6 fusion.25
  496.3 3.2 convert_element_type.140
  499.5 24.8 %reduce-scatter.3.cloned.1.call-done = bf16[672,2048]{1,0:T(8,128)(2,1)} async-done(((bf16[5376,2048]{1,0:T(8,128)(2,1)}), bf16[672,2048]{1,0:T(8,128)(2,1)}) %reduce-scatter.3.cloned.1.call-update) | async-done | bytes 2752528 | tf_op jit(solution)/shard_map/reduce_scatter | solution.py:216
  524.3 3.4 fusion.67
  527.7 1.9 slice.138
  (73 shorter events, 16.8 us)
Async XLA Ops:
  7.2 117.4 %all-gather.3.cloned.1.call-start = ((), (), s32[]{:S(2)}) async-start(), calls=%async_computation.2 | async-start | bytes 24772608 | tf_op jit(solution)/shard_map/all_gather | solution.py:127
  10.9 249.0 %all-gather.5.cloned.1.call-start = ((), (), s32[]{:S(2)}) async-start(), calls=%async_computation.3 | async-start | bytes 12386304 | tf_op jit(solution)/shard_map/all_gather | solution.py:130
  11.6 484.7 %reduce-scatter.5.cloned.1.call-start = ((), (), s32[]{:S(2)}) async-start(), calls=%async_computation.5 | async-start | bytes 12386304 | tf_op jit(solution)/shard_map/reduce_scatter | solution.py:213
  12.2 128.9 %copy-start.8 = (f32[512,64]{0,1:T(8,128)}, f32[512,64]{0,1:T(8,128)S(1)}, u32[]{:S(2)}) copy-start(f32[512,64]{0,1:T(8,128)S(1)} %get-tuple-element.33) | copy-start | bytes 393220
  12.5 133.3 %copy-start.6 = (f32[512,64]{1,0:T(8,128)}, f32[512,64]{1,0:T(8,128)S(1)}, u32[]{:S(2)}) copy-start(f32[512,64]{1,0:T(8,128)S(1)} %copy.70) | copy-start | bytes 393220
  141.2 1.9 copy-start.3
  146.6 8.9 %slice-start = ((f32[512,2048]{0,1:T(8,128)}), f32[512,1024]{0,1:T(8,128)S(1)}, s32[]{:S(2)}) async-start(f32[512,2048]{0,1:T(8,128)} %copy-done.3), calls=%async_computation.6 | async-start | bytes 4194304 | tf_op jit(solution)/shard_map/slice | solution.py:132
  146.6 8.9 %copy-start.9 = (f32[512,64]{0,1:T(8,128)S(1)}, f32[512,64]{0,1:T(8,128)}, u32[]{:S(2)}) copy-start(f32[512,64]{0,1:T(8,128)} %copy-done.8) | copy-start | bytes 393220
  147.6 42.0 %collective-permute-start = (bf16[512,1024]{0,1:T(8,128)(2,1)}, bf16[512,1024]{0,1:T(8,128)(2,1)}, u32[]{:S(2)}, u32[]{:S(2)}) collective-permute-start(bf16[512,1024]{0,1:T(8,128)(2,1)} %pad_maximum_fusion.3), channel_id=1, source_target_pairs={{0,8},{4,12},{8,16},{12,20},{16,24},{20,28},{1,9},{5,13},{9,17},{1... | collective-permute-start | bytes 3145736 | tf_op jit(solution)/shard_map/ppermute | solution.py:19
  149.8 64.0 %collective-permute-start.1 = (bf16[512,1024]{0,1:T(8,128)(2,1)}, bf16[512,1024]{0,1:T(8,128)(2,1)}, u32[]{:S(2)}, u32[]{:S(2)}) collective-permute-start(bf16[512,1024]{0,1:T(8,128)(2,1)} %pad_maximum_fusion.3), channel_id=1, source_target_pairs={{0,4},{4,8},{8,12},{12,16},{16,20},{20,24},{24,28},{1,5},{5,9},{9,... | collective-permute-start | bytes 3145736 | tf_op jit(solution)/shard_map/ppermute | solution.py:19
  242.8 4.6 copy-start
  247.3 1.0 copy-start.5
  259.8 264.5 %reduce-scatter.3.cloned.1.call-start = ((), (), s32[]{:S(2)}) async-start(), calls=%async_computation.4 | async-start | bytes 24772608 | tf_op jit(solution)/shard_map/reduce_scatter | solution.py:216
  292.7 12.6 %copy-start.1 = (bf16[4,2,512,1536]{2,3,1,0:T(8,128)(2,1)S(1)}, bf16[4,2,512,1536]{2,3,1,0:T(8,128)(2,1)}, u32[]{:S(2)}) copy-start(bf16[4,2,512,1536]{2,3,1,0:T(8,128)(2,1)} %fusion.2) | copy-start | bytes 37748740
  296.9 8.4 %copy-start.13 = (bf16[512,4,2,128]{3,0,2,1:T(8,128)(2,1)S(1)}, bf16[512,4,2,128]{3,0,2,1:T(8,128)(2,1)}, u32[]{:S(2)}) copy-start(bf16[512,4,2,128]{3,0,2,1:T(8,128)(2,1)} %fusion.26) | copy-start | bytes 3145732
  301.8 5.0 copy-start.4
  301.8 38.5 %collective-permute-start.2 = (bf16[512,1024]{0,1:T(8,128)(2,1)S(1)}, bf16[512,1024]{0,1:T(8,128)(2,1)S(1)}, u32[]{:S(2)}, u32[]{:S(2)}) collective-permute-start(bf16[512,1024]{0,1:T(8,128)(2,1)S(1)} %pad_maximum_fusion.4), channel_id=1, source_target_pairs={{4,0},{8,4},{12,8},{16,12},{20,16},{24,20},{28,24},{5,1},{9,5},{13... | collective-permute-start | bytes 3145736 | tf_op jit(solution)/shard_map/ppermute | solution.py:19
  306.8 6.3 %copy-start.11 = (bf16[512,4,128]{2,0,1:T(8,128)(2,1)S(1)}, bf16[512,4,128]{2,0,1:T(8,128)(2,1)}, u32[]{:S(2)}) copy-start(bf16[512,4,128]{2,0,1:T(8,128)(2,1)} %copy.73) | copy-start | bytes 1572868
  310.8 4.2 copy-start.10
  310.9 35.3 %collective-permute-start.3 = (bf16[512,1024]{0,1:T(8,128)(2,1)S(1)}, bf16[512,1024]{0,1:T(8,128)(2,1)S(1)}, u32[]{:S(2)}, u32[]{:S(2)}) collective-permute-start(bf16[512,1024]{0,1:T(8,128)(2,1)S(1)} %pad_maximum_fusion.5), channel_id=1, source_target_pairs={{8,0},{12,4},{16,8},{20,12},{24,16},{28,20},{9,1},{13,5},{17,9},{2... | collective-permute-start | bytes 3145736 | tf_op jit(solution)/shard_map/ppermute | solution.py:19
  347.4 0.9 copy-start.7
  366.1 1.2 copy-start.12
  366.1 1.4 copy-start.14
  399.6 24.3 %collective-permute-start.4 = (bf16[512,1344]{0,1:T(8,128)(2,1)}, bf16[512,1344]{0,1:T(8,128)(2,1)S(1)}, u32[]{:S(2)}, u32[]{:S(2)}) collective-permute-start(bf16[512,1344]{0,1:T(8,128)(2,1)} %get-tuple-element.9), channel_id=1, source_target_pairs={{0,1},{1,2},{2,3},{3,0},{4,5},{5,6},{6,7},{7,4},{8,9},{9,10},{10,1... | collective-permute-start | bytes 4128776 | tf_op jit(solution)/shard_map/ppermute | solution.py:58
  400.8 91.9 %collective-permute-start.5 = (bf16[512,1344]{0,1:T(8,128)(2,1)}, bf16[512,1344]{0,1:T(8,128)(2,1)S(1)}, u32[]{:S(2)}, u32[]{:S(2)}) collective-permute-start(bf16[512,1344]{0,1:T(8,128)(2,1)} %get-tuple-element.11), channel_id=1, source_target_pairs={{0,2},{1,3},{2,0},{3,1},{4,6},{5,7},{6,4},{7,5},{8,10},{9,11},{10,... | collective-permute-start | bytes 4128776 | tf_op jit(solution)/shard_map/ppermute | solution.py:58
  402.9 89.8 %collective-permute-start.6 = (bf16[512,1344]{0,1:T(8,128)(2,1)}, bf16[512,1344]{0,1:T(8,128)(2,1)}, u32[]{:S(2)}, u32[]{:S(2)}) collective-permute-start(bf16[512,1344]{0,1:T(8,128)(2,1)} %get-tuple-element.10), channel_id=1, source_target_pairs={{0,3},{1,0},{2,1},{3,2},{4,7},{5,4},{6,5},{7,6},{8,11},{9,8},{10,9... | collective-permute-start | bytes 4128776 | tf_op jit(solution)/shard_map/ppermute | solution.py:58
  524.3 3.4 copy-start.2
Sparse Core Ops, SparseCore 0:
  11.0 113.5 all-gather.2
  126.4 86.8 all-gather.4
  260.0 119.6 reduce-scatter.4
  383.2 141.0 reduce-scatter.2

commit v11 on v9

--- a/solution.py
+++ b/solution.py
@@ -206,7 +206,9 @@
     )
     value_gradient = own_values.astype(jnp.bfloat16)
     grads_qkv = jnp.concatenate([dquery, key_gradient, value_gradient], axis=1)
-    partial_in = dot_rows(grads_qkv, full_qkv)
+    partial_in = dot_rows(dquery, full_qkv[:, :query_cols]) + dot_rows(
+        grads_qkv[:, query_cols:], full_qkv[:, query_cols:]
+    )
     in_grad = sum_over_heads(partial_in.astype(jnp.bfloat16))
     grad_qkv_part = jnp.einsum("nd,nc->dc", hidden_in, grads_qkv, preferred_element_type=jnp.float32)
     grad_out_w = lax.psum_scatter(

time: 545 us -> 555 us (1.018)
  matrix products: 137 us -> 150 us
    dot_general x1 -> x2, matrix products: 18.2 us -> 31.1 us  [dot_rows(): lax.dot_general(left, weight, (((1,), (1,)), ((), ())), preferred_element...]
  transfers between devices with their start and end apart: 15 -> 15, of which waited for: 7 -> 7; matrix products, arithmetic and copies ran while one was open for 37% -> 38% of each run, Pallas kernels for 0% -> 0%
where the time goes in v11:
time: 555 us; the launch traced here: 548 us
  waiting for transfers between devices  289 us (52%)
  matrix products  150 us (27%)
  local copies, waits for them, and re-layouts  37.9 us (7%)
  other arithmetic  34.9 us (6%)
  starting transfers between devices  22 us (4%)
  between operations  14.4 us (3%)
    ppermute x3, waiting for transfers between devices, sum_over_heads(): lax.ppermute(outgoing, 'head', [(source, (source + shift) % count) for so...  116 us
    all_gather x1, waiting for transfers between devices, shards(): lax.all_gather(jnp.concatenate([w_query, key_weight, value_weight], axis=...  112 us
    ppermute x8, waiting for transfers between devices, from_behind(): lax.ppermute(value, axis, [(source, source + steps) for source in range(i...  61 us
    dot_general x2, matrix products, dot_rows(): lax.dot_general(left, weight, (((1,), (1,)), ((), ())), preferred_element...  31.1 us
    dot_general x1, matrix products, shards(): jnp.einsum('nd,nc->dc', hidden_in, grads_qkv, preferred_element_type=jnp....  20.3 us
    ppermute x8, starting transfers between devices, from_behind(): lax.ppermute(value, axis, [(source, source + steps) for source in range(i...  18.1 us
    dot_general x1, matrix products, shards(): projected = jnp.dot(hidden_in, full_qkv, preferred_element_type=jnp.float32)  16.7 us
    dot_general x1, matrix products, attend_backward(): jnp.einsum('ngrd,mgd->grnm', gradient_list, value_rows, preferred_element...  15.7 us
  transfers between devices with their start and end apart: 15, of which 7 were waited for; matrix products, arithmetic and copies ran while one was open for 38% of the time, Pallas kernels for 0%

profile of v11, /device:TPU:3, one launch (start us, length us, event | category | flops | bytes accessed | tf_op | source)
XLA Modules:
  0.0 548.2 jit_solution(15041581474096534021)
XLA Ops:
  7.2 3.6 pad_maximum_fusion
  12.5 112.0 %all-gather.3.cloned.1.call-done = bf16[5376,2048]{1,0:T(8,128)(2,1)} async-done(((bf16[672,2048]{1,0:T(8,128)(2,1)}), bf16[5376,2048]{1,0:T(8,128)(2,1)}) %all-gather.3.cloned.1.call-update) | async-done | bytes 22020112 | tf_op jit(solution)/shard_map/all_gather | solution.py:127
  124.6 16.7 %convolution_bitcast_fusion = f32[512,2048]{0,1:T(8,128)S(1)} fusion(bf16[5376,2048]{1,0:T(8,128)(2,1)} %all-gather.3.cloned.1.call-done, bf16[512,5376]{1,0:T(8,128)(2,1)} %param.6), kind=kOutput, calls=%fused_computation.32 | convolution fusion | flops 11274289152 | bytes 31719424 | tf_op jit(solution)/shard_map/dot_general | solution.py:131
  142.3 2.2 collective-permute-start.3
  144.5 3.2 collective-permute-start.2
  150.2 2.4 collective-permute-start.1
  152.6 2.1 collective-permute-start
  154.7 1.9 and_and_fusion
  156.6 1.8 multiply_subtract_fusion.1
  158.4 1.8 copy.72
  160.2 3.2 copy.71
  163.5 3.5 fusion.32
  167.0 32.3 %collective-permute-done.1 = bf16[512,512]{0,1:T(8,128)(2,1)} collective-permute-done((bf16[512,512]{0,1:T(8,128)(2,1)}, bf16[512,512]{0,1:T(8,128)(2,1)}, u32[]{:S(2)}, u32[]{:S(2)}) %collective-permute-start.1) | collective-permute-done | bytes 524320 | tf_op jit(solution)/shard_map/ppermute | solution.py:19
  200.6 13.3 %collective-permute-done = bf16[512,512]{0,1:T(8,128)(2,1)} collective-permute-done((bf16[512,512]{0,1:T(8,128)(2,1)}, bf16[512,512]{0,1:T(8,128)(2,1)}, u32[]{:S(2)}, u32[]{:S(2)}) %collective-permute-start) | collective-permute-done | bytes 524320 | tf_op jit(solution)/shard_map/ppermute | solution.py:19
  213.9 2.1 copy.69
  217.4 14.4 %fusion.84 = (f32[4,2,512]{2,1,0:T(2,128)S(1)}, f32[4,2,512,1536]{2,3,1,0:T(8,128)}) fusion(pred[512,1536]{0,1:T(8,128)(4,1)} %and_and_fusion, bf16[512,4,2,128]{3,0,2,1:T(8,128)(2,1)} %fusion.32, bf16[512,4,128]{2,0,1:T(8,128)(2,1)S(1)} %maximum_convert_fusion, bf16[512,4,128]{2,0,1:T(8,128)(2,1)S(1)} %copy.70, bf16[512,4,128]{2,0,1:T(8,128)(2,1)} %copy.69), kind=kOutput, calls=%fused_computation.104 | convolution fusion | flops 1634207232 | bytes 28590080 | tf_op jit(solution)/shard_map/sub | solution.py:78
  231.8 10.2 %fusion.11 = bf16[4,2,512,1536]{2,3,1,0:T(8,128)(2,1)S(1)} fusion(f32[4,2,512,1536]{2,3,1,0:T(8,128)} %get-tuple-element.29, f32[4,2,512]{2,1,0:T(2,128)S(1)} %get-tuple-element.28), kind=kLoop, calls=%fused_computation.18 | loop fusion | flops 12582912 | bytes 37765120 | tf_op jit(solution)/shard_map/convert_element_type | solution.py:80
  242.0 1.8 fusion.39
  243.9 2.7 copy-done
  247.5 11.5 %fusion.14 = bf16[5376,1024]{1,0:T(8,128)(2,1)} fusion(bf16[512,1024]{0,1:T(8,128)(2,1)S(1)} %bitcast.157, bf16[512,5376]{1,0:T(8,128)(2,1)} %param.7), kind=kOutput, calls=%fused_computation.19 | convolution fusion | flops 5642649600 | bytes 17563648 | tf_op jit(solution)/shard_map/nd,nc->dc/dot_general | solution.py:173
  259.2 11.0 %convolution_convert_fusion.2 = bf16[512,1024]{1,0:T(8,128)(2,1)} fusion(bf16[512,5376]{1,0:T(8,128)(2,1)} %param.7, bf16[5376,1024]{1,0:T(8,128)(2,1)} %all-gather.5.cloned.1.call-done), kind=kOutput, calls=%fused_computation.52 | convolution fusion | flops 5637668864 | bytes 17563648 | tf_op jit(solution)/shard_map/dot_general | solution.py:168
  270.2 2.5 copy.74
  272.7 6.1 %fusion.52 = bf16[4,128,512]{2,1,0:T(8,128)(2,1)} fusion(bf16[512,4,2,128]{0,3,2,1:T(8,128)(2,1)} %bitcast.152, bf16[4,2,512,1536]{2,3,1,0:T(8,128)(2,1)} %copy-done), kind=kOutput, calls=%fused_computation.62 | convolution fusion | flops 537133056 | bytes 5767168 | tf_op jit(solution)/shard_map/grnm,ngrd->mgd/dot_general | solution.py:107
  278.8 2.0 collective-permute-start.7
  280.9 4.5 fusion.55
  285.4 1.9 collective-permute-start.6
  287.6 15.7 %fusion.2 = bf16[4,2,512,1536]{2,3,1,0:T(8,128)(2,1)} fusion(bf16[1536,4,128,1]{0,2,3,1:T(8,128)(2,1)S(1)} %bitcast.150, bf16[512,4,2,128]{0,3,2,1:T(8,128)(2,1)} %bitcast.153, f32[4,2,512]{2,1,0:T(2,128)S(1)} %bitcast.164, f32[4,2,512,1536]{2,3,1,0:T(8,128)} %get-tuple-element.29, f32[4,2,512]{2,1,0:T(2,128)S(1)} %get-tuple-element.28), kind=kOutput, calls=%fused_computation.3 | convolution fusion | flops 1635778560 | bytes 40402944 | tf_op jit(solution)/shard_map/ngrd,mgd->grnm/dot_general | solution.py:90
  303.3 4.2 fusion.58
  307.5 2.2 collective-permute-start.5
  309.7 4.1 fusion.61
  313.8 2.1 collective-permute-start.4
  315.9 2.0 fusion.71
  321.9 4.7 fusion.19
  326.6 9.2 %collective-permute-done.5 = bf16[512,512]{0,1:T(8,128)(2,1)S(1)} collective-permute-done((bf16[512,512]{0,1:T(8,128)(2,1)S(1)}, bf16[512,512]{0,1:T(8,128)(2,1)S(1)}, u32[]{:S(2)}, u32[]{:S(2)}) %collective-permute-start.5) | collective-permute-done | bytes 524320 | tf_op jit(solution)/shard_map/ppermute | solution.py:19
  335.9 6.1 %collective-permute-done.4 = bf16[512,512]{0,1:T(8,128)(2,1)S(1)} collective-permute-done((bf16[512,512]{0,1:T(8,128)(2,1)S(1)}, bf16[512,512]{0,1:T(8,128)(2,1)S(1)}, u32[]{:S(2)}, u32[]{:S(2)}) %collective-permute-start.4) | collective-permute-done | bytes 524320 | tf_op jit(solution)/shard_map/ppermute | solution.py:19
  343.8 1.7 fusion.68
  345.6 20.3 %fusion.4 = bf16[5376,2048]{1,0:T(8,128)(2,1)} fusion(bf16[512,5376]{1,0:T(8,128)(2,1)} %param.6, bf16[512,512]{0,1:T(8,128)(2,1)S(1)} %fusion.68, bf16[512,512]{0,1:T(8,128)(2,1)S(1)} %bitcast.160, bf16[512,1024]{0,1:T(8,128)(2,1)S(1)} %bitcast.158), kind=kOutput, calls=%fused_computation.8 | convolution fusion | flops 11291590656 | bytes 29622272 | tf_op jit(solution)/shard_map/nd,nc->dc/dot_general | solution.py:213
  365.9 13.0 %fusion.7 = f32[512,5376]{1,0:T(8,128)} fusion(bf16[5376,2048]{1,0:T(8,128)(2,1)} %all-gather.3.cloned.1.call-done, bf16[512,512]{0,1:T(8,128)(2,1)S(1)} %fusion.68, bf16[512,512]{0,1:T(8,128)(2,1)S(1)} %bitcast.161), kind=kOutput, calls=%fused_computation.13 | convolution fusion | flops 5639241728 | bytes 23068672 | tf_op jit(solution)/shard_map/dot_general | solution.py:69
  378.9 18.1 %add_convert_fusion = bf16[512,5376]{1,0:T(8,128)(2,1)} fusion(f32[512,5376]{1,0:T(8,128)} %fusion.7, bf16[512,1024]{0,1:T(8,128)(2,1)S(1)} %bitcast.159, bf16[5376,2048]{1,0:T(8,128)(2,1)} %all-gather.3.cloned.1.call-done), kind=kOutput, calls=%fused_computation.17 | convolution fusion | flops 5642649600 | bytes 28573696 | tf_op jit(solution)/shard_map/dot_general | solution.py:69
  397.0 8.8 %copy.91 = bf16[512,5376]{0,1:T(8,128)(2,1)} copy(bf16[512,5376]{1,0:T(8,128)(2,1)} %add_convert_fusion) | data formatting | bytes 11010048 | tf_op jit(solution)/shard_map/convert_element_type | solution.py:212
  405.8 4.2 dynamic-slice_bitcast_fusion.2
  410.0 3.1 collective-permute-start.10
  413.7 29.8 %collective-permute-done.10 = bf16[512,1344]{0,1:T(8,128)(2,1)S(1)} collective-permute-done((bf16[512,1344]{0,1:T(8,128)(2,1)}, bf16[512,1344]{0,1:T(8,128)(2,1)S(1)}, u32[]{:S(2)}, u32[]{:S(2)}) %collective-permute-start.10) | collective-permute-done | bytes 1376288 | tf_op jit(solution)/shard_map/ppermute | solution.py:58
  443.5 85.9 %collective-permute-done.9 = bf16[512,1344]{0,1:T(8,128)(2,1)S(1)} collective-permute-done((bf16[512,1344]{0,1:T(8,128)(2,1)}, bf16[512,1344]{0,1:T(8,128)(2,1)S(1)}, u32[]{:S(2)}, u32[]{:S(2)}) %collective-permute-start.9) | collective-permute-done | bytes 1376288 | tf_op jit(solution)/shard_map/ppermute | solution.py:58
  529.4 3.6 fusion.31
  533.0 3.2 convert_element_type.186
  536.2 3.4 slice.110
  539.6 1.9 fusion.81
  (70 shorter events, 15.6 us)
Async XLA Ops:
  7.2 117.4 %all-gather.3.cloned.1.call-start = ((), (), s32[]{:S(2)}) async-start(), calls=%async_computation.2 | async-start | bytes 24772608 | tf_op jit(solution)/shard_map/all_gather | solution.py:127
  10.9 248.3 %all-gather.5.cloned.1.call-start = ((), (), s32[]{:S(2)}) async-start(), calls=%async_computation.3 | async-start | bytes 12386304 | tf_op jit(solution)/shard_map/all_gather | solution.py:130
  11.6 521.3 %reduce-scatter.5.cloned.1.call-start = ((), (), s32[]{:S(2)}) async-start(), calls=%async_computation.5 | async-start | bytes 12386304 | tf_op jit(solution)/shard_map/reduce_scatter | solution.py:214
  141.3 6.4 %copy-start.3 = (f32[512,2048]{0,1:T(8,128)}, f32[512,2048]{0,1:T(8,128)S(1)}, u32[]{:S(2)}) copy-start(f32[512,2048]{0,1:T(8,128)S(1)} %convolution_bitcast_fusion) | copy-start | bytes 12582916
  142.3 73.7 %collective-permute-start.3 = (bf16[512,512]{0,1:T(8,128)(2,1)}, bf16[512,512]{0,1:T(8,128)(2,1)}, u32[]{:S(2)}, u32[]{:S(2)}) collective-permute-start(bf16[512,512]{0,1:T(8,128)(2,1)} %slice.156), channel_id=1, source_target_pairs={{0,4},{4,8},{8,12},{12,16},{16,20},{20,24},{24,28},{1,5},{5,9},{9,... | collective-permute-start | bytes 1572872 | tf_op jit(solution)/shard_map/ppermute | solution.py:19
  144.5 71.4 %collective-permute-start.2 = (bf16[512,512]{0,1:T(8,128)(2,1)}, bf16[512,512]{0,1:T(8,128)(2,1)}, u32[]{:S(2)}, u32[]{:S(2)}) collective-permute-start(bf16[512,512]{0,1:T(8,128)(2,1)} %slice.156), channel_id=1, source_target_pairs={{0,8},{4,12},{8,16},{12,20},{16,24},{20,28},{1,9},{5,13},{9,17},{1... | collective-permute-start | bytes 1572872 | tf_op jit(solution)/shard_map/ppermute | solution.py:19
  148.8 7.7 %slice-start = ((f32[512,2048]{0,1:T(8,128)}), f32[512,1024]{0,1:T(8,128)S(1)}, s32[]{:S(2)}) async-start(f32[512,2048]{0,1:T(8,128)} %copy-done.3), calls=%async_computation.6 | async-start | bytes 4194304 | tf_op jit(solution)/shard_map/slice | solution.py:132
  150.2 49.1 %collective-permute-start.1 = (bf16[512,512]{0,1:T(8,128)(2,1)}, bf16[512,512]{0,1:T(8,128)(2,1)}, u32[]{:S(2)}, u32[]{:S(2)}) collective-permute-start(bf16[512,512]{0,1:T(8,128)(2,1)} %bitcast.162), channel_id=1, source_target_pairs={{0,4},{4,8},{8,12},{12,16},{16,20},{20,24},{24,28},{1,5},{5,9},{9,... | collective-permute-start | bytes 1572872 | tf_op jit(solution)/shard_map/ppermute | solution.py:19
  152.6 61.3 %collective-permute-start = (bf16[512,512]{0,1:T(8,128)(2,1)}, bf16[512,512]{0,1:T(8,128)(2,1)}, u32[]{:S(2)}, u32[]{:S(2)}) collective-permute-start(bf16[512,512]{0,1:T(8,128)(2,1)} %bitcast.163), channel_id=1, source_target_pairs={{0,8},{4,12},{8,16},{12,20},{16,24},{20,28},{1,9},{5,13},{9,17},{1... | collective-permute-start | bytes 1572872 | tf_op jit(solution)/shard_map/ppermute | solution.py:19
  242.0 4.5 copy-start
  246.6 1.0 copy-start.6
  259.1 277.1 %reduce-scatter.3.cloned.1.call-start = ((), (), s32[]{:S(2)}) async-start(), calls=%async_computation.4 | async-start | bytes 24772608 | tf_op jit(solution)/shard_map/reduce_scatter | solution.py:217
  272.7 8.2 %copy-start.4 = (bf16[512,1024]{0,1:T(8,128)(2,1)S(1)}, bf16[512,1024]{0,1:T(8,128)(2,1)}, u32[]{:S(2)}) copy-start(bf16[512,1024]{0,1:T(8,128)(2,1)} %copy.74) | copy-start | bytes 3145732
  278.8 8.5 %copy-start.7 = (bf16[512,4,2,128]{0,3,2,1:T(8,128)(2,1)S(1)}, bf16[512,4,2,128]{0,3,2,1:T(8,128)(2,1)}, u32[]{:S(2)}) copy-start(bf16[512,4,2,128]{0,3,2,1:T(8,128)(2,1)} %copy-done.6) | copy-start | bytes 3145732
  278.8 65.0 %collective-permute-start.7 = (bf16[512,512]{0,1:T(8,128)(2,1)}, bf16[512,512]{0,1:T(8,128)(2,1)}, u32[]{:S(2)}, u32[]{:S(2)}) collective-permute-start(bf16[512,512]{0,1:T(8,128)(2,1)} %bitcast.49), channel_id=1, source_target_pairs={{8,0},{12,4},{16,8},{20,12},{24,16},{28,20},{9,1},{13,5},{17,9},{2... | collective-permute-start | bytes 1572872 | tf_op jit(solution)/shard_map/ppermute | solution.py:19
  285.4 58.5 %collective-permute-start.6 = (bf16[512,512]{0,1:T(8,128)(2,1)}, bf16[512,512]{0,1:T(8,128)(2,1)}, u32[]{:S(2)}, u32[]{:S(2)}) collective-permute-start(bf16[512,512]{0,1:T(8,128)(2,1)} %bitcast.45), channel_id=1, source_target_pairs={{4,0},{8,4},{12,8},{16,12},{20,16},{24,20},{28,24},{5,1},{9,5},{13... | collective-permute-start | bytes 1572872 | tf_op jit(solution)/shard_map/ppermute | solution.py:19
  303.3 12.6 %copy-start.1 = (bf16[4,2,512,1536]{2,3,1,0:T(8,128)(2,1)S(1)}, bf16[4,2,512,1536]{2,3,1,0:T(8,128)(2,1)}, u32[]{:S(2)}) copy-start(bf16[4,2,512,1536]{2,3,1,0:T(8,128)(2,1)} %fusion.2) | copy-start | bytes 37748740
  307.5 8.4 %copy-start.8 = (bf16[512,4,128]{2,0,1:T(8,128)(2,1)S(1)}, bf16[512,4,128]{2,0,1:T(8,128)(2,1)}, u32[]{:S(2)}) copy-start(bf16[512,4,128]{2,0,1:T(8,128)(2,1)} %copy.69) | copy-start | bytes 1572868
  307.5 28.3 %collective-permute-start.5 = (bf16[512,512]{0,1:T(8,128)(2,1)S(1)}, bf16[512,512]{0,1:T(8,128)(2,1)S(1)}, u32[]{:S(2)}, u32[]{:S(2)}) collective-permute-start(bf16[512,512]{0,1:T(8,128)(2,1)S(1)} %bitcast.165), channel_id=1, source_target_pairs={{8,0},{12,4},{16,8},{20,12},{24,16},{28,20},{9,1},{13,5},{17,9},{2... | collective-permute-start | bytes 1572872 | tf_op jit(solution)/shard_map/ppermute | solution.py:19
  313.8 28.2 %collective-permute-start.4 = (bf16[512,512]{0,1:T(8,128)(2,1)S(1)}, bf16[512,512]{0,1:T(8,128)(2,1)S(1)}, u32[]{:S(2)}, u32[]{:S(2)}) collective-permute-start(bf16[512,512]{0,1:T(8,128)(2,1)S(1)} %bitcast.166), channel_id=1, source_target_pairs={{4,0},{8,4},{12,8},{16,12},{20,16},{24,20},{28,24},{5,1},{9,5},{13... | collective-permute-start | bytes 1572872 | tf_op jit(solution)/shard_map/ppermute | solution.py:19
  317.9 1.2 copy-start.10
  319.1 2.8 copy-start.5
  343.3 2.3 copy-start.9
  410.0 33.5 %collective-permute-start.10 = (bf16[512,1344]{0,1:T(8,128)(2,1)}, bf16[512,1344]{0,1:T(8,128)(2,1)S(1)}, u32[]{:S(2)}, u32[]{:S(2)}) collective-permute-start(bf16[512,1344]{0,1:T(8,128)(2,1)} %get-tuple-element.10), channel_id=1, source_target_pairs={{0,3},{1,0},{2,1},{3,2},{4,7},{5,4},{6,5},{7,6},{8,11},{9,8},{10,9... | collective-permute-start | bytes 4128776 | tf_op jit(solution)/shard_map/ppermute | solution.py:58
  413.1 116.3 %collective-permute-start.9 = (bf16[512,1344]{0,1:T(8,128)(2,1)}, bf16[512,1344]{0,1:T(8,128)(2,1)S(1)}, u32[]{:S(2)}, u32[]{:S(2)}) collective-permute-start(bf16[512,1344]{0,1:T(8,128)(2,1)} %get-tuple-element.11), channel_id=1, source_target_pairs={{0,2},{1,3},{2,0},{3,1},{4,6},{5,7},{6,4},{7,5},{8,10},{9,11},{10,... | collective-permute-start | bytes 4128776 | tf_op jit(solution)/shard_map/ppermute | solution.py:58
  413.1 116.3 %collective-permute-start.8 = (bf16[512,1344]{0,1:T(8,128)(2,1)}, bf16[512,1344]{0,1:T(8,128)(2,1)}, u32[]{:S(2)}, u32[]{:S(2)}) collective-permute-start(bf16[512,1344]{0,1:T(8,128)(2,1)} %get-tuple-element.9), channel_id=1, source_target_pairs={{0,1},{1,2},{2,3},{3,0},{4,5},{5,6},{6,7},{7,4},{8,9},{9,10},{10,1... | collective-permute-start | bytes 4128776 | tf_op jit(solution)/shard_map/ppermute | solution.py:58
  536.2 3.4 copy-start.2
Sparse Core Ops, SparseCore 0:
  11.0 113.5 all-gather.2
  126.4 87.9 all-gather.4
  259.2 108.0 reduce-scatter.4
  370.8 141.0 reduce-scatter.2
